TPU v7x, 512 devices: a whole 4x8x8 slice. The times are simulated.
512 devices in a mesh: req: 64 (over y, x, core), tp: 8 (over z).
Axes of the slice: x: 4, y: 8, z: 8, core: 2. Of those that a mesh axis runs over, the one named last changes fastest.
Arguments:
- hidden: bfloat16 [2048, 5, 2560], P('req', None, 'tp'), may hold values from -6 to 6
- norm_gain: bfloat16 [2560], replicated, may hold values from 0.099609375 to 1.8984375
- query_weight: bfloat16 [2560, 2560], P(None, 'tp'), may hold values from -0.125 to 0.125
- key_value_matrix: bfloat16 [2560, 8, 160], P(None, 'tp'), may hold values from -0.125 to 0.125
- output_weight: bfloat16 [2560, 2560], P('tp'), may hold values from -0.5 to 0.5
- key_value_cache: bfloat16 [2048, 64, 8, 160], P('req', None, 'tp'), as said below
- deal_order: int32 [2048], P('req'), may hold values from 0 to 2047, as said below
- cache_length: int32 [2048], P('req'), may hold values from 1 to 64, as said below
- accepted: int32 [2048], P('req'), may hold values from 1 to 5
Outputs:
- block_output: bfloat16 [2048, 5, 2560], P('req', None, 'tp')
- new_entries: bfloat16 [2048, 5, 8, 160], P('req', None, 'tp')
Inputs may be any that keep to these rules, and one draw needn't show every extreme that they name: deal_order is a permutation of the 2048 requests; slot i lies on index i // 32 of req, and request r arrives on index r // 32. Every index deals at most 1 of its requests to any one index, and exactly 1 to each of 32 indices. Cache entries of slot i at positions from cache_length[i] on are unused. `key_value_cache`: at positions below cache_length[i] the first 80 entries of each head are the keys, already rotated for their positions, and the last 80 the values.
All inputs are finite; a program needn't handle non-finite values.
Results may differ from a plain program's by a relative error of at most 0.0091.
Values may be sent and summed in bfloat16 or wider, within the bound.
No kernel may reach another device: no remote copies, remote signals or barrier semaphores. Data moves between devices by JAX's collectives and lax.ppermute only.
A program may use at most 128 MiB of HBM per device.

v0:
```python
import math

import jax
import jax.numpy as jnp
from jax import lax
from jax.sharding import PartitionSpec as P

HEAD_SIZE = 80


masked_score = -1e30


def rotate(values, positions):
    half_dim = HEAD_SIZE // 2
    frequency = 10000.0 ** (-2.0 * jnp.arange(half_dim, dtype=jnp.float32) / HEAD_SIZE)
    angles = positions.astype(jnp.float32)[..., None] * frequency
    cosine_part = jnp.cos(angles)
    sine_part = jnp.sin(angles)
    first_half = values[..., :half_dim]
    second_half = values[..., half_dim:]
    return jnp.concatenate(
        [
            first_half * cosine_part - second_half * sine_part,
            second_half * cosine_part + first_half * sine_part,
        ],
        axis=-1,
    )


def attend(query_rows, key_value_cache, fresh, cache_length):
    scale = 1.0 / math.sqrt(HEAD_SIZE)
    slot_count = query_rows.shape[0]
    verified = query_rows.shape[1]
    cache_keys = key_value_cache[..., :HEAD_SIZE]
    cache_values = key_value_cache[..., HEAD_SIZE:]
    fresh_keys = fresh[..., :HEAD_SIZE]
    fresh_values = fresh[..., HEAD_SIZE:]
    cache_scores = (
        jnp.einsum("rtghd,rcgd->rghtc", query_rows, cache_keys, preferred_element_type=jnp.float32)
        * scale
    )
    visible = jnp.arange(key_value_cache.shape[1], dtype=jnp.int32)[None, :] < cache_length[:, None]
    cache_scores = jnp.where(visible[:, None, None, None, :], cache_scores, masked_score)
    fresh_scores = (
        jnp.einsum("rtghd,rugd->rghtu", query_rows, fresh_keys, preferred_element_type=jnp.float32)
        * scale
    )
    causal = (
        jnp.arange(verified, dtype=jnp.int32)[:, None]
        >= jnp.arange(verified, dtype=jnp.int32)[None, :]
    )
    fresh_scores = jnp.where(causal[None, None, None, :, :], fresh_scores, masked_score)
    largest = jnp.maximum(jnp.max(cache_scores, axis=-1), jnp.max(fresh_scores, axis=-1))[..., None]
    cache_expos = jnp.exp(cache_scores - largest)
    fresh_expos = jnp.exp(fresh_scores - largest)
    totals = jnp.sum(cache_expos, axis=-1, keepdims=True) + jnp.sum(
        fresh_expos, axis=-1, keepdims=True
    )
    cache_weights = (cache_expos / totals).astype(jnp.bfloat16)
    fresh_weights = (fresh_expos / totals).astype(jnp.bfloat16)
    mixed = jnp.einsum(
        "rghtc,rcgd->rtghd", cache_weights, cache_values, preferred_element_type=jnp.float32
    )
    mixed = mixed + jnp.einsum(
        "rghtu,rugd->rtghd", fresh_weights, fresh_values, preferred_element_type=jnp.float32
    )
    return mixed.astype(jnp.bfloat16).reshape(slot_count, verified, -1)


def body(
    hidden,
    norm_gain,
    query_weight,
    key_value_matrix,
    output_weight,
    key_value_cache,
    deal_order,
    cache_length,
    accepted,
):
    slot_count = deal_order.shape[0]
    verified = hidden.shape[1]
    device_index = lax.axis_index("req")
    my_requests = device_index * slot_count + jnp.arange(slot_count, dtype=jnp.int32)
    piece = lax.all_gather(hidden, "req", axis=0, tiled=True)
    picker = (deal_order[:, None] == jnp.arange(piece.shape[0], dtype=jnp.int32)[None, :]).astype(
        jnp.bfloat16
    )
    dealt_rows = jnp.einsum(
        "in,ntf->itf", picker, piece, preferred_element_type=jnp.float32
    ).astype(jnp.bfloat16)
    features = lax.all_gather(dealt_rows, "tp", axis=2, tiled=True)
    widened = features.astype(jnp.float32)
    variance = jnp.mean(widened * widened, axis=-1, keepdims=True)
    normed = (widened * lax.rsqrt(variance + 1e-05) * norm_gain.astype(jnp.float32)).astype(
        jnp.bfloat16
    )
    heads_here = query_weight.shape[1] // HEAD_SIZE
    groups_here = key_value_matrix.shape[1]
    positions = cache_length[:, None] + jnp.arange(verified, dtype=jnp.int32)[None, :]
    query_rows = jnp.einsum("rtd,de->rte", normed, query_weight, preferred_element_type=jnp.float32)
    query_rows = query_rows.reshape(
        slot_count, verified, groups_here, heads_here // groups_here, HEAD_SIZE
    )
    query_rows = rotate(query_rows, positions[:, :, None, None]).astype(jnp.bfloat16)
    projected = jnp.einsum(
        "rtd,dge->rtge", normed, key_value_matrix, preferred_element_type=jnp.float32
    )
    fresh = jnp.concatenate(
        [rotate(projected[..., :HEAD_SIZE], positions[:, :, None]), projected[..., HEAD_SIZE:]],
        axis=-1,
    ).astype(jnp.bfloat16)
    keep = (jnp.arange(verified, dtype=jnp.int32)[None, :] < accepted[:, None])[:, :, None, None]
    new_entries = jnp.where(keep, fresh, jnp.zeros_like(fresh))
    mixed = attend(query_rows, key_value_cache, fresh, cache_length)
    partial_sum = jnp.einsum(
        "rte,ed->rtd", mixed, output_weight, preferred_element_type=jnp.float32
    )
    out_dealt = lax.psum_scatter(partial_sum, "tp", scatter_dimension=2, tiled=True).astype(
        jnp.bfloat16
    )
    piece_rows = lax.all_gather(out_dealt, "req", axis=0, tiled=True)
    piece_owners = lax.all_gather(deal_order, "req", axis=0, tiled=True)
    picker = (my_requests[:, None] == piece_owners[None, :]).astype(jnp.bfloat16)
    block_output = jnp.einsum(
        "jn,ntf->jtf", picker, piece_rows, preferred_element_type=jnp.float32
    ).astype(jnp.bfloat16)
    return (block_output, new_entries)


def solution(mesh):
    placed = (
        P("req", None, "tp"),
        P(),
        P(None, "tp"),
        P(None, "tp", None),
        P("tp", None),
        P("req", None, "tp", None),
        P("req"),
        P("req"),
        P("req"),
    )
    return jax.shard_map(
        body,
        mesh=mesh,
        in_specs=placed,
        out_specs=(P("req", None, "tp"), P("req", None, "tp", None)),
        check_vma=False,
    )
```

profile of v0, /device:TPU:1, one launch (start us, length us, event | category | flops | bytes accessed | tf_op | source)
XLA Modules:
  0.0 338.5 jit_solution(15841835390689357700)
XLA Ops:
  7.2 0.7 all-gather.3.cloned.1.call-update
  8.0 0.7 convert_element_type.71
  8.7 0.7 add_convert_fusion
  9.4 0.7 iota_compare_fusion.1
  10.2 0.5 multiply_cosine_fusion
  10.7 93.9 %all-gather.3.cloned.1.call-done = bf16[2048,5,320]{2,0,1:T(8,128)(2,1)} async-done(((bf16[32,5,320]{2,0,1:T(8,128)(2,1)}), bf16[2048,5,320]{2,0,1:T(8,128)(2,1)}) %all-gather.3.cloned.1.call-update) | async-done | bytes 6553616 | tf_op jit(solution)/shard_map/all_gather | solution.py:86
  104.6 4.7 %convolution_convert_fusion.1 = bf16[32,5,320]{2,0,1:T(8,128)(2,1)S(1)} fusion(bf16[2048,5,320]{2,0,1:T(8,128)(2,1)} %all-gather.3.cloned.1.call-done, s32[32]{0:T(128)} %param.15), kind=kOutput, calls=%fused_computation.21 | convolution fusion | flops 209831936 | bytes 6656128 | tf_op jit(solution)/shard_map/in,ntf->itf/dot_general | solution.py:90
  109.3 0.4 copy.43
  109.7 55.1 %all_gather.14 = bf16[32,5,2560]{0,1,2:T(8,128)(2,1)} all-gather(bf16[32,5,320]{0,1,2:T(8,128)(2,1)S(1)} %copy.43), channel_id=1, replica_groups=mesh['req'=64,'tp'=8] {'tp'}, dimensions={2}, use_global_device_ids=true | all-gather | bytes 921600 | tf_op jit(solution)/shard_map/all_gather | solution.py:93
  164.9 4.4 %copy.44 = bf16[32,5,2560]{2,0,1:T(8,128)(2,1)S(1)} copy(bf16[32,5,2560]{0,1,2:T(8,128)(2,1)} %all_gather.14) | data formatting | bytes 1638400 | tf_op jit(solution)/shard_map/all_gather | solution.py:93
  169.5 1.7 convolution_bitcast_fusion.1
  171.3 0.6 copy-done.1
  171.9 0.4 fusion.41
  172.3 0.8 fusion.5
  173.6 0.5 fusion.24
  174.1 1.4 fusion.51
  175.5 0.6 fusion.50
  176.3 0.4 fusion.21
  176.8 0.8 convolution_bitcast_fusion
  177.6 0.4 fusion.13
  178.2 0.6 fusion.3
  178.8 5.5 %copy.64 = f32[32,5,2560]{0,1,2:T(8,128)} copy(f32[32,5,2560]{2,0,1:T(8,128)S(1)} %fusion.3) | data formatting | bytes 3276800
  184.3 8.0 %reshape.347 = f32[2560,160]{1,0:T(8,128)} reshape(f32[2560,5,32]{2,1,0:T(8,128)} %bitcast.87) | data formatting | bytes 3276800
  192.4 39.6 %reduce-scatter.4.cloned.1.call-done = f32[320,160]{1,0:T(8,128)} async-done(((f32[2560,160]{1,0:T(8,128)}), f32[320,160]{1,0:T(8,128)}) %reduce-scatter.4.cloned.1.call-update) | async-done | bytes 204816
  232.1 1.2 reshape.348
  233.3 1.0 copy.65
  234.3 1.3 dynamic-slice
  236.5 21.3 %all-reduce = s32[2048]{0:T(1024)S(1)} all-reduce(s32[2048]{0:T(1024)S(1)} %dynamic-update-slice), channel_id=1, replica_groups=mesh['req'=64,'tp'=8] {'req'}, use_global_device_ids=true, to_apply=%add | all-reduce | flops 2048 | bytes 16384
  257.9 1.0 slice.51
  258.9 0.8 fusion.44
  259.7 67.0 %all-gather.5.cloned.1.call-done = bf16[2048,5,320]{2,0,1:T(8,128)(2,1)} async-done(((bf16[32,5,320]{2,0,1:T(8,128)(2,1)}), bf16[2048,5,320]{2,0,1:T(8,128)(2,1)}) %all-gather.5.cloned.1.call-update) | async-done | bytes 6553616 | tf_op jit(solution)/shard_map/all_gather | solution.py:123
  326.7 5.3 %convolution_convert_fusion = bf16[32,5,320]{2,0,1:T(8,128)(2,1)} fusion(bf16[2048,5,320]{2,0,1:T(8,128)(2,1)} %all-gather.5.cloned.1.call-done, s32[2048]{0:T(1024)S(1)} %all-reduce, s32[32]{0:T(128)S(1)} %iota_add_fusion), kind=kOutput, calls=%fused_computation.20 | convolution fusion | flops 209831936 | bytes 6664320 | tf_op jit(solution)/shard_map/jn,ntf->jtf/dot_general | solution.py:126
  (34 shorter events, 2.0 us)
Async XLA Ops:
  7.2 171.1 %copy-start = (bf16[320,2560]{1,0:T(8,128)(2,1)S(1)}, bf16[320,2560]{1,0:T(8,128)(2,1)}, u32[]{:S(2)}) copy-start(bf16[320,2560]{1,0:T(8,128)(2,1)} %param.13) | copy-start | bytes 4915204
  7.2 97.5 %all-gather.3.cloned.1.call-start = ((), (), s32[]{:S(2)}) async-start(), calls=%async_computation.1 | async-start | bytes 7987200 | tf_op jit(solution)/shard_map/all_gather | solution.py:86
  7.9 224.2 %reduce-scatter.4.cloned.1.call-start = ((), (), s32[]{:S(2)}) async-start(), calls=%async_computation.3 | async-start | bytes 2949120
  169.2 3.0 copy-start.4
  171.2 0.7 copy-start.1
  173.5 1.9 copy-start.2
  192.4 43.9 %copy-start.3 = (s32[32]{0:T(128)S(1)}, s32[32]{0:T(128)}, u32[]{:S(2)}) copy-start(s32[32]{0:T(128)} %param.15) | copy-start | bytes 388
  192.4 65.5 %copy-start.5 = (s32[32]{0:T(128)S(1)}, s32[32]{0:T(128)}, u32[]{:S(2)}) copy-start(s32[32]{0:T(128)} %param.17) | copy-start | bytes 388
  192.4 134.3 %all-gather.5.cloned.1.call-start = ((), (), s32[]{:S(2)}) async-start(), calls=%async_computation.2 | async-start | bytes 7987200 | tf_op jit(solution)/shard_map/all_gather | solution.py:123
Sparse Core Ops, SparseCore 0:
  11.3 93.2 all-gather.2
  192.5 39.5 reduce-scatter.3
  235.9 90.6 all-gather.4
where the time goes:
time: 339 us; the launch traced here: 338 us
  waiting for transfers between devices  201 us (59%)
  blocking collectives  76.4 us (23%)
  local copies, waits for them, and re-layouts  24.5 us (7%)
  matrix products  16.2 us (5%)
  between operations  14.6 us (4%)
  other arithmetic  5.35 us (2%)
    all_gather x1, waiting for transfers between devices, body(): piece = lax.all_gather(hidden, 'req', axis=0, tiled=True)  93.9 us
    all_gather x1, waiting for transfers between devices, body(): piece_rows = lax.all_gather(out_dealt, 'req', axis=0, tiled=True)  67 us
    all_gather x1, blocking collectives, body(): features = lax.all_gather(dealt_rows, 'tp', axis=2, tiled=True)  55.1 us
    unnamed x4, waiting for transfers between devices  40.3 us
    unnamed x1, blocking collectives  21.3 us
    unnamed x19, local copies, waits for them, and re-layouts  17.9 us
  transfers between devices with their start and end apart: 3, of which 3 were waited for; matrix products, arithmetic and copies ran while one was open for 2% of the time, Pallas kernels for 0%

commit v1 on v0

--- a/solution.py
+++ b/solution.py
@@ -1,3 +1,4 @@
+import functools
 import math
 
 import jax
@@ -78,35 +79,52 @@
     deal_order,
     cache_length,
     accepted,
+    *,
+    peers,
+    shards,
 ):
     slot_count = deal_order.shape[0]
     verified = hidden.shape[1]
-    device_index = lax.axis_index("req")
-    my_requests = device_index * slot_count + jnp.arange(slot_count, dtype=jnp.int32)
-    piece = lax.all_gather(hidden, "req", axis=0, tiled=True)
-    picker = (deal_order[:, None] == jnp.arange(piece.shape[0], dtype=jnp.int32)[None, :]).astype(
-        jnp.bfloat16
-    )
+    width = hidden.shape[2]
+    source = deal_order // slot_count
+    local = deal_order % slot_count
+    match = source[None, :] == jnp.arange(peers, dtype=jnp.int32)[:, None]
+    wish = jnp.sum(jnp.where(match, local[None, :] + 1, 0), axis=1) - 1
+    wanted = lax.all_to_all(wish, "req", 0, 0, tiled=True)
+    pick = (wanted[:, None] == jnp.arange(slot_count, dtype=jnp.int32)[None, :]).astype(jnp.bfloat16)
+    outgoing = jnp.einsum(
+        "dj,jtf->dtf", pick, hidden, preferred_element_type=jnp.float32
+    ).astype(jnp.bfloat16)
+    incoming = lax.all_to_all(outgoing, "req", 0, 0, tiled=True)
+    take = match.astype(jnp.bfloat16)
     dealt_rows = jnp.einsum(
-        "in,ntf->itf", picker, piece, preferred_element_type=jnp.float32
+        "pi,ptf->itf", take, incoming, preferred_element_type=jnp.float32
     ).astype(jnp.bfloat16)
-    features = lax.all_gather(dealt_rows, "tp", axis=2, tiled=True)
+    rows = slot_count * verified
+    features = lax.all_gather(dealt_rows.reshape(rows, width), "tp", axis=0, tiled=False)
     widened = features.astype(jnp.float32)
-    variance = jnp.mean(widened * widened, axis=-1, keepdims=True)
-    normed = (widened * lax.rsqrt(variance + 1e-05) * norm_gain.astype(jnp.float32)).astype(
-        jnp.bfloat16
-    )
+    variance = jnp.mean(widened * widened, axis=(0, 2), keepdims=True)
+    gain = norm_gain.reshape(shards, 1, width).astype(jnp.float32)
+    normed = (widened * lax.rsqrt(variance + 1e-05) * gain).astype(jnp.bfloat16)
     heads_here = query_weight.shape[1] // HEAD_SIZE
     groups_here = key_value_matrix.shape[1]
     positions = cache_length[:, None] + jnp.arange(verified, dtype=jnp.int32)[None, :]
-    query_rows = jnp.einsum("rtd,de->rte", normed, query_weight, preferred_element_type=jnp.float32)
+    query_rows = jnp.einsum(
+        "knf,kfe->ne",
+        normed,
+        query_weight.reshape(shards, width, -1),
+        preferred_element_type=jnp.float32,
+    )
     query_rows = query_rows.reshape(
         slot_count, verified, groups_here, heads_here // groups_here, HEAD_SIZE
     )
     query_rows = rotate(query_rows, positions[:, :, None, None]).astype(jnp.bfloat16)
     projected = jnp.einsum(
-        "rtd,dge->rtge", normed, key_value_matrix, preferred_element_type=jnp.float32
-    )
+        "knf,kfge->nge",
+        normed,
+        key_value_matrix.reshape(shards, width, groups_here, -1),
+        preferred_element_type=jnp.float32,
+    ).reshape(slot_count, verified, groups_here, -1)
     fresh = jnp.concatenate(
         [rotate(projected[..., :HEAD_SIZE], positions[:, :, None]), projected[..., HEAD_SIZE:]],
         axis=-1,
@@ -115,16 +133,19 @@
     new_entries = jnp.where(keep, fresh, jnp.zeros_like(fresh))
     mixed = attend(query_rows, key_value_cache, fresh, cache_length)
     partial_sum = jnp.einsum(
-        "rte,ed->rtd", mixed, output_weight, preferred_element_type=jnp.float32
+        "ne,ekf->knf",
+        mixed.reshape(rows, -1),
+        output_weight.reshape(-1, shards, width),
+        preferred_element_type=jnp.float32,
     )
-    out_dealt = lax.psum_scatter(partial_sum, "tp", scatter_dimension=2, tiled=True).astype(
-        jnp.bfloat16
-    )
-    piece_rows = lax.all_gather(out_dealt, "req", axis=0, tiled=True)
-    piece_owners = lax.all_gather(deal_order, "req", axis=0, tiled=True)
-    picker = (my_requests[:, None] == piece_owners[None, :]).astype(jnp.bfloat16)
+    out_dealt = lax.psum_scatter(partial_sum, "tp", scatter_dimension=0, tiled=True)
+    out_dealt = out_dealt.reshape(slot_count, verified, width).astype(jnp.bfloat16)
+    back_out = jnp.einsum(
+        "pi,itf->ptf", take, out_dealt, preferred_element_type=jnp.float32
+    ).astype(jnp.bfloat16)
+    returned = lax.all_to_all(back_out, "req", 0, 0, tiled=True)
     block_output = jnp.einsum(
-        "jn,ntf->jtf", picker, piece_rows, preferred_element_type=jnp.float32
+        "dj,dtf->jtf", pick, returned, preferred_element_type=jnp.float32
     ).astype(jnp.bfloat16)
     return (block_output, new_entries)
 
@@ -142,7 +163,7 @@
         P("req"),
     )
     return jax.shard_map(
-        body,
+        functools.partial(body, peers=mesh.shape["req"], shards=mesh.shape["tp"]),
         mesh=mesh,
         in_specs=placed,
         out_specs=(P("req", None, "tp"), P("req", None, "tp", None)),

time: 339 us -> 179 us (0.53)
  waiting for transfers between devices: 201 us -> 67.5 us
  blocking collectives: 76.4 us -> 27.6 us
  starting transfers between devices: 0.12 us -> 36.3 us
  local copies, waits for them, and re-layouts: 24.5 us -> 13.2 us
  matrix products: 16.2 us -> 8.8 us
  other arithmetic: 5.35 us -> 10.4 us
    all_gather x2 -> x0, waiting for transfers between devices: 161 us -> none  [the longest x1 93.9 us: body(): piece = lax.all_gather(hidden, 'req', axis=0, tiled=True)]
    unnamed x4 -> x1, waiting for transfers between devices: 40.3 us -> 0.02 us
    reduce_scatter x0 -> x1, waiting for transfers between devices: none -> 40 us  [body(): lax.psum_scatter(partial_sum, 'tp', scatter_dimension=0, tiled=True)]
    all_to_all x0 -> x3, starting transfers between devices: none -> 36.3 us  [the longest x1 14.4 us: body(): returned = lax.all_to_all(back_out, 'req', 0, 0, tiled=True)]
    all_gather x1, blocking collectives: 55.1 us -> 27.6 us  [body(): lax.all_gather(dealt_rows.reshape(rows, width), 'tp', axis=0, tiled=False)]
    all_to_all x0 -> x3, waiting for transfers between devices: none -> 27.4 us  [the longest x1 14.2 us: body(): returned = lax.all_to_all(back_out, 'req', 0, 0, tiled=True)]
    unnamed x1 -> x0, blocking collectives: 21.3 us -> none
    unnamed x19 -> x28, local copies, waits for them, and re-layouts: 17.9 us -> 1.09 us
  transfers between devices with their start and end apart: 3 -> 4, of which waited for: 3 -> 3; matrix products, arithmetic and copies ran while one was open for 2% -> 8% of each run, Pallas kernels for 0% -> 0%
where the time goes in v1:
time: 179 us; the launch traced here: 178 us
  waiting for transfers between devices  67.5 us (38%)
  starting transfers between devices  36.3 us (20%)
  blocking collectives  27.6 us (15%)
  between operations  14.3 us (8%)
  local copies, waits for them, and re-layouts  13.2 us (7%)
  other arithmetic  10.4 us (6%)
  matrix products  8.8 us (5%)
    reduce_scatter x1, waiting for transfers between devices, body(): lax.psum_scatter(partial_sum, 'tp', scatter_dimension=0, tiled=True)  40 us
    all_gather x1, blocking collectives, body(): lax.all_gather(dealt_rows.reshape(rows, width), 'tp', axis=0, tiled=False)  27.6 us
    all_to_all x1, starting transfers between devices, body(): returned = lax.all_to_all(back_out, 'req', 0, 0, tiled=True)  14.4 us
    all_to_all x1, waiting for transfers between devices, body(): returned = lax.all_to_all(back_out, 'req', 0, 0, tiled=True)  14.2 us
    all_to_all x1, waiting for transfers between devices, body(): incoming = lax.all_to_all(outgoing, 'req', 0, 0, tiled=True)  13.2 us
    all_to_all x1, starting transfers between devices, body(): wanted = lax.all_to_all(wish, 'req', 0, 0, tiled=True)  11.6 us
    all_to_all x1, starting transfers between devices, body(): incoming = lax.all_to_all(outgoing, 'req', 0, 0, tiled=True)  10.3 us
  transfers between devices with their start and end apart: 4, of which 3 were waited for; matrix products, arithmetic and copies ran while one was open for 8% of the time, Pallas kernels for 0%

profile of v1, /device:TPU:1, one launch (start us, length us, event | category | flops | bytes accessed | tf_op | source)
XLA Modules:
  0.0 178.2 jit_solution(17167947644802831720)
XLA Ops:
  7.2 0.8 and_select_fusion.1
  8.0 0.5 copy-done.8
  8.6 0.7 copy.59
  9.3 11.6 %all-to-all-start = ((s32[64,1,1]{2,1,0:T(1,128)}), s32[64,1,1]{2,1,0:T(1,128)S(1)}, u32[]{:S(2)}, u32[]{:S(2)}) async-start(s32[64,1,1]{2,1,0:T(1,128)} %copy.59), calls=%async_computation | async-start | bytes 65536 | tf_op jit(solution)/shard_map/all_to_all | solution.py:93
  20.9 0.6 iota_compare_fusion.4
  21.5 0.7 add_convert_fusion.1
  22.2 0.6 multiply_power_fusion
  22.8 1.4 reshape.372
  24.2 1.9 %reshape.365 = bf16[8,320,160]{1,0,2:T(8,128)(2,1)S(1)} reshape(bf16[2560,1,160]{0,2,1:T(8,128)(2,1)} %param.12) | data formatting | bytes 1638400 | tf_op jit(solution)/shard_map/reshape.20
  26.0 2.5 %reshape.362 = bf16[8,320,320]{1,0,2:T(8,128)(2,1)} reshape(bf16[2560,320]{0,1:T(8,128)(2,1)S(1)} %copy-done.2) | data formatting | bytes 3276800 | tf_op jit(solution)/shard_map/reshape | solution.py:115
  28.6 3.2 %reshape.371 = bf16[320,8,320]{2,1,0:T(8,128)(2,1)S(1)} reshape(bf16[320,2560]{1,0:T(8,128)(2,1)} %param.13) | data formatting | bytes 3276800 | tf_op jit(solution)/shard_map/reshape | solution.py:138
  31.8 1.2 reduce.4
  33.4 0.9 copy.60
  34.3 10.3 %all-to-all-start.1 = ((bf16[64,5,320]{2,1,0:T(8,128)(2,1)}), bf16[64,5,320]{2,1,0:T(8,128)(2,1)S(1)}, u32[]{:S(2)}, u32[]{:S(2)}) async-start(bf16[64,5,320]{2,1,0:T(8,128)(2,1)} %copy.60), calls=%async_computation.1 | async-start | bytes 786432 | tf_op jit(solution)/shard_map/all_to_all | solution.py:98
  44.7 1.7 multiply_cosine_fusion.1
  46.4 13.2 %all-to-all-done.1 = bf16[64,5,320]{2,1,0:T(8,128)(2,1)S(1)} async-done(((bf16[64,5,320]{2,1,0:T(8,128)(2,1)}), bf16[64,5,320]{2,1,0:T(8,128)(2,1)S(1)}, u32[]{:S(2)}, u32[]{:S(2)}) %all-to-all-start.1) | async-done | bytes 204832 | tf_op jit(solution)/shard_map/all_to_all | solution.py:98
  59.7 0.8 convolution_convert_fusion.3
  60.7 27.6 %all_gather.3 = bf16[8,160,320]{2,1,0:T(8,128)(2,1)S(1)} all-gather(bf16[1,160,320]{2,1,0:T(8,128)(2,1)S(1)} %all_gather_reshape.3), channel_id=1, replica_groups=mesh['req'=64,'tp'=8] {'tp'}, dimensions={0}, use_global_device_ids=true | all-gather | bytes 921600 | tf_op jit(solution)/shard_map/all_gather | solution.py:104
  88.2 1.0 fusion
  90.7 0.5 copy-done.1
  91.2 1.0 fusion.14
  92.6 1.3 fusion.61
  93.9 0.5 fusion.60
  95.2 0.8 convolution_bitcast_fusion
  96.7 2.0 %fusion.8 = f32[8,160,320]{2,1,0:T(8,128)} fusion(bf16[160,320,1]{1,0,2:T(8,128)(2,1)S(1)} %reshape.384, bf16[320,8,320]{2,1,0:T(8,128)(2,1)S(1)} %reshape.371), kind=kOutput, calls=%fused_computation.10 | convolution fusion | flops 262144000 | bytes 3379200 | tf_op jit(solution)/shard_map/ne,ekf->knf/dot_general | solution.py:135
  98.7 40.0 %reduce-scatter.2.cloned.1.call-done = f32[1,160,320]{2,1,0:T(8,128)} async-done(((f32[8,160,320]{2,1,0:T(8,128)}), f32[1,160,320]{2,1,0:T(8,128)}) %reduce-scatter.2.cloned.1.call-update) | async-done | bytes 204816 | tf_op jit(solution)/shard_map/reduce_scatter | solution.py:141
  138.7 1.0 convert_element_type.98
  140.1 0.9 copy.78
  141.0 14.4 %all-to-all-start.2 = ((bf16[64,5,320]{2,1,0:T(8,128)(2,1)}), bf16[64,5,320]{2,1,0:T(8,128)(2,1)S(1)}, u32[]{:S(2)}, u32[]{:S(2)}) async-start(bf16[64,5,320]{2,1,0:T(8,128)(2,1)} %copy.78), calls=%async_computation.3 | async-start | bytes 786432 | tf_op jit(solution)/shard_map/all_to_all | solution.py:146
  155.5 0.8 fusion.46
  156.3 14.2 %all-to-all-done.2 = bf16[64,5,320]{2,1,0:T(8,128)(2,1)S(1)} async-done(((bf16[64,5,320]{2,1,0:T(8,128)(2,1)}), bf16[64,5,320]{2,1,0:T(8,128)(2,1)S(1)}, u32[]{:S(2)}, u32[]{:S(2)}) %all-to-all-start.2) | async-done | bytes 204832 | tf_op jit(solution)/shard_map/all_to_all | solution.py:146
  170.5 0.8 convolution_convert_fusion.2
  (54 shorter events, 4.2 us)
Async XLA Ops:
  7.2 25.9 %copy-start = (bf16[32,5,320]{2,0,1:T(8,128)(2,1)S(1)}, bf16[32,5,320]{2,0,1:T(8,128)(2,1)}, u32[]{:S(2)}) copy-start(bf16[32,5,320]{2,0,1:T(8,128)(2,1)} %param.9) | copy-start | bytes 307204
  7.2 18.9 %copy-start.2 = (bf16[2560,320]{0,1:T(8,128)(2,1)S(1)}, bf16[2560,320]{0,1:T(8,128)(2,1)}, u32[]{:S(2)}) copy-start(bf16[2560,320]{0,1:T(8,128)(2,1)} %param.11) | copy-start | bytes 4915204
  8.0 0.5 copy-start.8
  9.3 22.5 %all-to-all-start = ((s32[64,1,1]{2,1,0:T(1,128)}), s32[64,1,1]{2,1,0:T(1,128)S(1)}, u32[]{:S(2)}, u32[]{:S(2)}) async-start(s32[64,1,1]{2,1,0:T(1,128)} %copy.59), calls=%async_computation | async-start | bytes 65536 | tf_op jit(solution)/shard_map/all_to_all | solution.py:93
  28.6 16.1 %copy-start.11 = (s32[32]{0:T(128)S(1)}, s32[32]{0:T(128)}, u32[]{:S(2)}) copy-start(s32[32]{0:T(128)} %param.16) | copy-start | bytes 388
  33.1 1.2 copy-start.6
  34.3 25.4 %all-to-all-start.1 = ((bf16[64,5,320]{2,1,0:T(8,128)(2,1)}), bf16[64,5,320]{2,1,0:T(8,128)(2,1)S(1)}, u32[]{:S(2)}, u32[]{:S(2)}) async-start(bf16[64,5,320]{2,1,0:T(8,128)(2,1)} %copy.60), calls=%async_computation.1 | async-start | bytes 786432 | tf_op jit(solution)/shard_map/all_to_all | solution.py:98
  44.6 94.1 %reduce-scatter.2.cloned.1.call-start = ((), (), s32[]{:S(2)}) async-start(), calls=%async_computation.4 | async-start | bytes 2211840 | tf_op jit(solution)/shard_map/reduce_scatter | solution.py:141
  60.5 28.8 %copy-start.5 = (f32[8,320]{1,0:T(8,128)S(1)}, f32[8,320]{1,0:T(8,128)}, u32[]{:S(2)}) copy-start(f32[8,320]{1,0:T(8,128)} %reshape.372) | copy-start | bytes 30724
  89.3 1.0 copy-start.10
  89.7 1.5 copy-start.1
  91.2 1.0 copy-start.3
  91.2 1.4 copy-start.12
  92.3 1.7 copy-start.4
  98.7 41.1 %copy-start.9 = (s32[32]{0:T(128)S(1)}, s32[32]{0:T(128)}, u32[]{:S(2)}) copy-start(s32[32]{0:T(128)} %copy-done.8) | copy-start | bytes 388
  98.7 56.7 %copy-start.13 = (s32[32]{0:T(128)S(1)}, s32[32]{0:T(128)}, u32[]{:S(2)}) copy-start(s32[32]{0:T(128)} %param.17) | copy-start | bytes 388
  98.7 71.8 %copy-start.7 = (s32[64]{0:T(128)S(1)}, s32[64]{0:T(128)}, u32[]{:S(2)}) copy-start(s32[64]{0:T(128)} %copy-done.6) | copy-start | bytes 772
  141.0 29.5 %all-to-all-start.2 = ((bf16[64,5,320]{2,1,0:T(8,128)(2,1)}), bf16[64,5,320]{2,1,0:T(8,128)(2,1)S(1)}, u32[]{:S(2)}, u32[]{:S(2)}) async-start(bf16[64,5,320]{2,1,0:T(8,128)(2,1)} %copy.78), calls=%async_computation.3 | async-start | bytes 786432 | tf_op jit(solution)/shard_map/all_to_all | solution.py:146
Sparse Core Ops, SparseCore 0:
  98.8 39.8 reduce-scatter.1

commit v2 on v1

--- a/solution.py
+++ b/solution.py
@@ -138,7 +138,8 @@
         output_weight.reshape(-1, shards, width),
         preferred_element_type=jnp.float32,
     )
-    out_dealt = lax.psum_scatter(partial_sum, "tp", scatter_dimension=0, tiled=True)
+    pieces = lax.all_to_all(partial_sum.astype(jnp.bfloat16), "tp", 0, 0, tiled=True)
+    out_dealt = jnp.sum(pieces.astype(jnp.float32), axis=0)
     out_dealt = out_dealt.reshape(slot_count, verified, width).astype(jnp.bfloat16)
     back_out = jnp.einsum(
         "pi,itf->ptf", take, out_dealt, preferred_element_type=jnp.float32

time: 179 us -> 146 us (0.82)
  waiting for transfers between devices: 67.5 us -> 27.5 us
  blocking collectives: 27.6 us -> 52 us
  between operations: 14.3 us -> 0.97 us
    reduce_scatter x1 -> x0, waiting for transfers between devices: 40 us -> none  [body(): lax.psum_scatter(partial_sum, 'tp', scatter_dimension=0, tiled=True)]
    all_to_all x0 -> x1, blocking collectives: none -> 24.4 us  [body(): lax.all_to_all(partial_sum.astype(jnp.bfloat16), 'tp', 0, 0, tiled=True)]
  transfers between devices with their start and end apart: 4 -> 3, of which waited for: 3 -> 2; matrix products, arithmetic and copies ran while one was open for 8% -> 10% of each run, Pallas kernels for 0% -> 0%
where the time goes in v2:
time: 146 us
  blocking collectives  52 us (36%)
  starting transfers between devices  34.7 us (24%)
  waiting for transfers between devices  27.5 us (19%)
  local copies, waits for them, and re-layouts  13.3 us (9%)
  other arithmetic  9.52 us (7%)
  matrix products  7.57 us (5%)
    all_gather x1, blocking collectives, body(): lax.all_gather(dealt_rows.reshape(rows, width), 'tp', axis=0, tiled=False)  27.6 us
    all_to_all x1, blocking collectives, body(): lax.all_to_all(partial_sum.astype(jnp.bfloat16), 'tp', 0, 0, tiled=True)  24.4 us
    all_to_all x1, waiting for transfers between devices, body(): returned = lax.all_to_all(back_out, 'req', 0, 0, tiled=True)  14.2 us
    all_to_all x1, waiting for transfers between devices, body(): incoming = lax.all_to_all(outgoing, 'req', 0, 0, tiled=True)  13.3 us
    all_to_all x1, starting transfers between devices, body(): returned = lax.all_to_all(back_out, 'req', 0, 0, tiled=True)  12.8 us
    all_to_all x1, starting transfers between devices, body(): wanted = lax.all_to_all(wish, 'req', 0, 0, tiled=True)  11.6 us
    all_to_all x1, starting transfers between devices, body(): incoming = lax.all_to_all(outgoing, 'req', 0, 0, tiled=True)  10.3 us
    reshape x1, local copies, waits for them, and re-layouts, body(): query_weight.reshape(shards, width, -1)  4.19 us
  transfers between devices with their start and end apart: 3, of which 2 were waited for; matrix products, arithmetic and copies ran while one was open for 10% of the time, Pallas kernels for 0%

profile of v2, /device:TPU:1, one launch (start us, length us, event | category | flops | bytes accessed | tf_op | source)
XLA Modules:
  0.0 145.6 jit_solution(702099578062719096)
XLA Ops:
  0.7 0.7 and_select_fusion.1
  1.5 0.7 copy.59
  2.2 11.6 %all-to-all-start = ((s32[64,1,1]{2,1,0:T(1,128)}), s32[64,1,1]{2,1,0:T(1,128)S(1)}, u32[]{:S(2)}, u32[]{:S(2)}) async-start(s32[64,1,1]{2,1,0:T(1,128)} %copy.59), calls=%async_computation | async-start | bytes 65536 | tf_op jit(solution)/shard_map/all_to_all | solution.py:93
  13.8 0.6 iota_compare_fusion.4
  14.4 0.7 add_convert_fusion.1
  15.1 0.6 multiply_power_fusion
  15.7 1.4 reshape.372
  17.0 4.2 %reshape.362 = bf16[8,320,320]{1,0,2:T(8,128)(2,1)} reshape(bf16[2560,320]{0,1:T(8,128)(2,1)} %param.11) | data formatting | bytes 3276800 | tf_op jit(solution)/shard_map/reshape | solution.py:115
  21.2 0.7 reshape.365
  22.0 3.2 %reshape.371 = bf16[320,8,320]{2,1,0:T(8,128)(2,1)S(1)} reshape(bf16[320,2560]{1,0:T(8,128)(2,1)} %param.13) | data formatting | bytes 3276800 | tf_op jit(solution)/shard_map/reshape | solution.py:138
  25.2 1.2 reduce.5
  26.8 0.9 copy.60
  27.7 10.3 %all-to-all-start.1 = ((bf16[64,5,320]{2,1,0:T(8,128)(2,1)}), bf16[64,5,320]{2,1,0:T(8,128)(2,1)S(1)}, u32[]{:S(2)}, u32[]{:S(2)}) async-start(bf16[64,5,320]{2,1,0:T(8,128)(2,1)} %copy.60), calls=%async_computation.1 | async-start | bytes 786432 | tf_op jit(solution)/shard_map/all_to_all | solution.py:98
  38.1 1.7 %multiply_cosine_fusion.1 = (f32[32,5,40]{2,0,1:T(8,128)S(1)}, f32[32,5,40]{2,0,1:T(8,128)}) fusion(f32[40]{0:T(128)} %multiply_power_fusion, f32[32,5]{0,1:T(8,128)S(1)} %add_convert_fusion.1), kind=kLoop, calls=%fused_computation.58 | loop fusion | flops 6400 | bytes 52000 | tf_op jit(solution)/shard_map/cos | solution.py:19
  39.8 13.3 %all-to-all-done.1 = bf16[64,5,320]{2,1,0:T(8,128)(2,1)S(1)} async-done(((bf16[64,5,320]{2,1,0:T(8,128)(2,1)}), bf16[64,5,320]{2,1,0:T(8,128)(2,1)S(1)}, u32[]{:S(2)}, u32[]{:S(2)}) %all-to-all-start.1) | async-done | bytes 204832 | tf_op jit(solution)/shard_map/all_to_all | solution.py:98
  53.1 0.9 convolution_convert_fusion.3
  54.1 27.6 %all_gather.3 = bf16[8,160,320]{2,1,0:T(8,128)(2,1)S(1)} all-gather(bf16[1,160,320]{2,1,0:T(8,128)(2,1)S(1)} %all_gather_reshape.3), channel_id=1, replica_groups=mesh['req'=64,'tp'=8] {'tp'}, dimensions={0}, use_global_device_ids=true | all-gather | bytes 921600 | tf_op jit(solution)/shard_map/all_gather | solution.py:104
  81.7 1.0 fusion
  83.2 0.4 convolution_bitcast_fusion.1
  84.1 0.6 copy-done.1
  84.7 1.0 fusion.17
  86.2 1.3 fusion.64
  87.5 0.5 fusion.63
  88.3 0.4 fusion.28
  88.8 0.8 convolution_bitcast_fusion
  90.2 0.7 fusion.11
  91.0 24.4 %all_to_all.21 = bf16[8,160,320]{2,1,0:T(8,128)(2,1)S(1)} all-to-all(bf16[8,160,320]{2,1,0:T(8,128)(2,1)S(1)} %fusion.11), channel_id=1, replica_groups=mesh['req'=64,'tp'=8] {'tp'}, dimensions={0} | all-to-all | bytes 1638400 | tf_op jit(solution)/shard_map/all_to_all | solution.py:141
  116.0 0.9 copy.78
  116.9 12.8 %all-to-all-start.3 = ((bf16[64,5,320]{2,1,0:T(8,128)(2,1)}), bf16[64,5,320]{2,1,0:T(8,128)(2,1)S(1)}, u32[]{:S(2)}, u32[]{:S(2)}) async-start(bf16[64,5,320]{2,1,0:T(8,128)(2,1)} %copy.78), calls=%async_computation.3 | async-start | bytes 786432 | tf_op jit(solution)/shard_map/all_to_all | solution.py:147
  129.8 0.8 fusion.49
  130.6 14.2 %all-to-all-done.3 = bf16[64,5,320]{2,1,0:T(8,128)(2,1)S(1)} async-done(((bf16[64,5,320]{2,1,0:T(8,128)(2,1)}), bf16[64,5,320]{2,1,0:T(8,128)(2,1)S(1)}, u32[]{:S(2)}, u32[]{:S(2)}) %all-to-all-start.3) | async-done | bytes 204832 | tf_op jit(solution)/shard_map/all_to_all | solution.py:147
  144.8 0.8 convolution_convert_fusion.2
  (52 shorter events, 3.4 us)
Async XLA Ops:
  0.6 25.8 %copy-start = (bf16[32,5,320]{2,0,1:T(8,128)(2,1)S(1)}, bf16[32,5,320]{2,0,1:T(8,128)(2,1)}, u32[]{:S(2)}) copy-start(bf16[32,5,320]{2,0,1:T(8,128)(2,1)} %param.9) | copy-start | bytes 307204
  0.6 20.6 %copy-start.2 = (bf16[2560,1,160]{0,2,1:T(8,128)(2,1)S(1)}, bf16[2560,1,160]{0,2,1:T(8,128)(2,1)}, u32[]{:S(2)}) copy-start(bf16[2560,1,160]{0,2,1:T(8,128)(2,1)} %param.12) | copy-start | bytes 2457604
  1.4 19.8 %copy-start.8 = (s32[32]{0:T(128)}, s32[32]{0:T(128)S(1)}, u32[]{:S(2)}) copy-start(s32[32]{0:T(128)S(1)} %get-tuple-element.16) | copy-start | bytes 388
  2.2 23.0 %all-to-all-start = ((s32[64,1,1]{2,1,0:T(1,128)}), s32[64,1,1]{2,1,0:T(1,128)S(1)}, u32[]{:S(2)}, u32[]{:S(2)}) async-start(s32[64,1,1]{2,1,0:T(1,128)} %copy.59), calls=%async_computation | async-start | bytes 65536 | tf_op jit(solution)/shard_map/all_to_all | solution.py:93
  22.0 16.0 %copy-start.11 = (s32[32]{0:T(128)S(1)}, s32[32]{0:T(128)}, u32[]{:S(2)}) copy-start(s32[32]{0:T(128)} %param.16) | copy-start | bytes 388
  26.5 11.5 %copy-start.6 = (s32[64]{0:T(128)}, s32[64]{0:T(128)S(1)}, u32[]{:S(2)}) copy-start(s32[64]{0:T(128)S(1)} %reduce.5) | copy-start | bytes 772
  27.7 25.4 %all-to-all-start.1 = ((bf16[64,5,320]{2,1,0:T(8,128)(2,1)}), bf16[64,5,320]{2,1,0:T(8,128)(2,1)S(1)}, u32[]{:S(2)}, u32[]{:S(2)}) async-start(bf16[64,5,320]{2,1,0:T(8,128)(2,1)} %copy.60), calls=%async_computation.1 | async-start | bytes 786432 | tf_op jit(solution)/shard_map/all_to_all | solution.py:98
  54.0 28.8 %copy-start.5 = (f32[8,320]{1,0:T(8,128)S(1)}, f32[8,320]{1,0:T(8,128)}, u32[]{:S(2)}) copy-start(f32[8,320]{1,0:T(8,128)} %reshape.372) | copy-start | bytes 30724
  82.7 0.9 copy-start.10
  83.2 1.5 %copy-start.1 = (bf16[8,320,320]{1,0,2:T(8,128)(2,1)S(1)}, bf16[8,320,320]{1,0,2:T(8,128)(2,1)}, u32[]{:S(2)}) copy-start(bf16[8,320,320]{1,0,2:T(8,128)(2,1)} %reshape.362) | copy-start | bytes 4915204
  84.7 1.1 copy-start.3
  84.7 1.5 %copy-start.12 = (pred[5,5]{0,1:T(8,128)(4,1)S(1)}, pred[5,5]{0,1:T(8,128)(4,1)}, u32[]{:S(2)}) copy-start(pred[5,5]{0,1:T(8,128)(4,1)} %iota_compare_fusion.4) | copy-start | bytes 79
  85.7 1.8 %copy-start.4 = (bf16[32,64,1,160]{3,1,2,0:T(8,128)(2,1)S(1)}, bf16[32,64,1,160]{3,1,2,0:T(8,128)(2,1)}, u32[]{:S(2)}) copy-start(bf16[32,64,1,160]{3,1,2,0:T(8,128)(2,1)} %param.14) | copy-start | bytes 1966084
  90.9 24.7 %copy-start.9 = (s32[32]{0:T(128)S(1)}, s32[32]{0:T(128)}, u32[]{:S(2)}) copy-start(s32[32]{0:T(128)} %copy-done.8) | copy-start | bytes 388
  115.4 14.3 %copy-start.13 = (s32[32]{0:T(128)S(1)}, s32[32]{0:T(128)}, u32[]{:S(2)}) copy-start(s32[32]{0:T(128)} %param.17) | copy-start | bytes 388
  115.4 29.4 %copy-start.7 = (s32[64]{0:T(128)S(1)}, s32[64]{0:T(128)}, u32[]{:S(2)}) copy-start(s32[64]{0:T(128)} %copy-done.6) | copy-start | bytes 772
  116.9 27.9 %all-to-all-start.3 = ((bf16[64,5,320]{2,1,0:T(8,128)(2,1)}), bf16[64,5,320]{2,1,0:T(8,128)(2,1)S(1)}, u32[]{:S(2)}, u32[]{:S(2)}) async-start(bf16[64,5,320]{2,1,0:T(8,128)(2,1)} %copy.78), calls=%async_computation.3 | async-start | bytes 786432 | tf_op jit(solution)/shard_map/all_to_all | solution.py:147

commit v3 on v2

--- a/solution.py
+++ b/solution.py
@@ -92,13 +92,18 @@
     wish = jnp.sum(jnp.where(match, local[None, :] + 1, 0), axis=1) - 1
     wanted = lax.all_to_all(wish, "req", 0, 0, tiled=True)
     pick = (wanted[:, None] == jnp.arange(slot_count, dtype=jnp.int32)[None, :]).astype(jnp.bfloat16)
+    row_size = verified * width
+    tile = 16 * 128
+    padded = -(-row_size // tile) * tile
     outgoing = jnp.einsum(
-        "dj,jtf->dtf", pick, hidden, preferred_element_type=jnp.float32
+        "dj,jx->dx", pick, hidden.reshape(slot_count, row_size), preferred_element_type=jnp.float32
     ).astype(jnp.bfloat16)
+    outgoing = jnp.pad(outgoing, ((0, 0), (0, padded - row_size))).reshape(peers, padded // 128, 128)
     incoming = lax.all_to_all(outgoing, "req", 0, 0, tiled=True)
+    incoming = incoming.reshape(peers, padded)[:, :row_size]
     take = match.astype(jnp.bfloat16)
     dealt_rows = jnp.einsum(
-        "pi,ptf->itf", take, incoming, preferred_element_type=jnp.float32
+        "pi,px->ix", take, incoming, preferred_element_type=jnp.float32
     ).astype(jnp.bfloat16)
     rows = slot_count * verified
     features = lax.all_gather(dealt_rows.reshape(rows, width), "tp", axis=0, tiled=False)
@@ -142,12 +147,14 @@
     out_dealt = jnp.sum(pieces.astype(jnp.float32), axis=0)
     out_dealt = out_dealt.reshape(slot_count, verified, width).astype(jnp.bfloat16)
     back_out = jnp.einsum(
-        "pi,itf->ptf", take, out_dealt, preferred_element_type=jnp.float32
+        "pi,ix->px", take, out_dealt.reshape(slot_count, row_size), preferred_element_type=jnp.float32
     ).astype(jnp.bfloat16)
+    back_out = jnp.pad(back_out, ((0, 0), (0, padded - row_size))).reshape(peers, padded // 128, 128)
     returned = lax.all_to_all(back_out, "req", 0, 0, tiled=True)
+    returned = returned.reshape(peers, padded)[:, :row_size]
     block_output = jnp.einsum(
-        "dj,dtf->jtf", pick, returned, preferred_element_type=jnp.float32
-    ).astype(jnp.bfloat16)
+        "dj,dx->jx", pick, returned, preferred_element_type=jnp.float32
+    ).astype(jnp.bfloat16).reshape(slot_count, verified, width)
     return (block_output, new_entries)
 
 

time: 146 us -> 141 us (0.966)
  waiting for transfers between devices: 27.5 us -> 25 us
  other arithmetic: 9.52 us -> 7.56 us
    unnamed x28 -> x24, local copies, waits for them, and re-layouts: 0.66 us -> 3.93 us
    all_to_all x1, waiting for transfers between devices: 14.2 us -> 12.3 us  [body(): returned = lax.all_to_all(back_out, 'req', 0, 0, tiled=True)]
    convert_element_type x3 -> x0, local copies, waits for them, and re-layouts: 1.9 us -> none  [the longest x1 0.93 us: body(): outgoing = jnp.einsum('dj,jtf->dtf', pick, hidden, preferred_element_type...]
  transfers between devices with their start and end apart: 3 -> 3, of which waited for: 2 -> 2; matrix products, arithmetic and copies ran while one was open for 10% -> 9% of each run, Pallas kernels for 0% -> 0%
where the time goes in v3:
time: 141 us; the launch traced here: 140 us
  blocking collectives  51.8 us (37%)
  starting transfers between devices  33.8 us (24%)
  waiting for transfers between devices  25 us (18%)
  local copies, waits for them, and re-layouts  14.6 us (10%)
  other arithmetic  7.56 us (5%)
  matrix products  6.31 us (4%)
    all_gather x1, blocking collectives, body(): lax.all_gather(dealt_rows.reshape(rows, width), 'tp', axis=0, tiled=False)  27.5 us
    all_to_all x1, blocking collectives, body(): lax.all_to_all(partial_sum.astype(jnp.bfloat16), 'tp', 0, 0, tiled=True)  24.3 us
    all_to_all x1, waiting for transfers between devices, body(): incoming = lax.all_to_all(outgoing, 'req', 0, 0, tiled=True)  12.7 us
    all_to_all x1, waiting for transfers between devices, body(): returned = lax.all_to_all(back_out, 'req', 0, 0, tiled=True)  12.3 us
    all_to_all x1, starting transfers between devices, body(): returned = lax.all_to_all(back_out, 'req', 0, 0, tiled=True)  11.9 us
    all_to_all x1, starting transfers between devices, body(): wanted = lax.all_to_all(wish, 'req', 0, 0, tiled=True)  11.6 us
    all_to_all x1, starting transfers between devices, body(): incoming = lax.all_to_all(outgoing, 'req', 0, 0, tiled=True)  10.3 us
    reshape x1, local copies, waits for them, and re-layouts, body(): query_weight.reshape(shards, width, -1)  4.17 us
  transfers between devices with their start and end apart: 3, of which 2 were waited for; matrix products, arithmetic and copies ran while one was open for 9% of the time, Pallas kernels for 0%

profile of v3, /device:TPU:1, one launch (start us, length us, event | category | flops | bytes accessed | tf_op | source)
XLA Modules:
  0.0 140.1 jit_solution(2310343515316995415)
XLA Ops:
  0.6 0.7 and_select_fusion.1
  1.4 0.7 copy.75
  2.1 11.6 %all-to-all-start = ((s32[64,1,1]{2,1,0:T(1,128)}), s32[64,1,1]{2,1,0:T(1,128)S(1)}, u32[]{:S(2)}, u32[]{:S(2)}) async-start(s32[64,1,1]{2,1,0:T(1,128)} %copy.75), calls=%async_computation | async-start | bytes 65536 | tf_op jit(solution)/shard_map/all_to_all | solution.py:93
  13.7 0.6 iota_compare_fusion.8
  14.3 0.7 add_convert_fusion.1
  15.0 1.0 copy.76
  16.1 0.9 reshape.398
  16.9 4.2 %reshape.385 = bf16[8,320,320]{1,0,2:T(8,128)(2,1)} reshape(bf16[2560,320]{0,1:T(8,128)(2,1)} %param.11) | data formatting | bytes 3276800 | tf_op jit(solution)/shard_map/reshape | solution.py:120
  21.1 0.7 reshape.388
  21.9 3.2 %reshape.394 = bf16[320,8,320]{2,1,0:T(8,128)(2,1)S(1)} reshape(bf16[320,2560]{1,0:T(8,128)(2,1)} %param.13) | data formatting | bytes 3276800 | tf_op jit(solution)/shard_map/reshape | solution.py:143
  25.1 1.2 reduce.5
  26.6 0.7 copy.107
  27.4 10.3 %all-to-all-start.1 = ((bf16[64,16,128]{2,1,0:T(8,128)(2,1)}), bf16[64,16,128]{2,1,0:T(8,128)(2,1)S(1)}, u32[]{:S(2)}, u32[]{:S(2)}) async-start(bf16[64,16,128]{2,1,0:T(8,128)(2,1)} %bitcast.53), calls=%async_computation.1 | async-start | bytes 524288 | tf_op jit(solution)/shard_map/all_to_all | solution.py:102
  38.2 12.7 %all-to-all-done.1 = bf16[64,16,128]{2,1,0:T(8,128)(2,1)S(1)} async-done(((bf16[64,16,128]{2,1,0:T(8,128)(2,1)}), bf16[64,16,128]{2,1,0:T(8,128)(2,1)S(1)}, u32[]{:S(2)}, u32[]{:S(2)}) %all-to-all-start.1) | async-done | bytes 262176 | tf_op jit(solution)/shard_map/all_to_all | solution.py:102
  51.3 27.5 %all_gather.3 = bf16[8,160,320]{2,1,0:T(8,128)(2,1)S(1)} all-gather(bf16[1,160,320]{2,1,0:T(8,128)(2,1)S(1)} %all_gather_reshape.3), channel_id=1, replica_groups=mesh['req'=64,'tp'=8] {'tp'}, dimensions={0}, use_global_device_ids=true | all-gather | bytes 921600 | tf_op jit(solution)/shard_map/all_gather | solution.py:109
  78.9 1.0 fusion
  79.9 0.4 fusion.2
  80.3 0.4 convolution_bitcast_fusion.1
  80.8 0.4 fusion.45
  81.3 0.6 copy-done
  81.9 1.0 fusion.17
  83.3 1.3 fusion.57
  84.6 0.5 fusion.56
  85.4 0.4 fusion.28
  85.9 0.8 convolution_bitcast_fusion
  87.4 0.7 fusion.11
  88.1 24.3 %all_to_all.21 = bf16[8,160,320]{2,1,0:T(8,128)(2,1)S(1)} all-to-all(bf16[8,160,320]{2,1,0:T(8,128)(2,1)S(1)} %fusion.11), channel_id=1, replica_groups=mesh['req'=64,'tp'=8] {'tp'}, dimensions={0} | all-to-all | bytes 1638400 | tf_op jit(solution)/shard_map/all_to_all | solution.py:146
  113.0 0.7 copy.109
  113.8 11.9 %all-to-all-start.3 = ((bf16[64,16,128]{2,1,0:T(8,128)(2,1)}), bf16[64,16,128]{2,1,0:T(8,128)(2,1)S(1)}, u32[]{:S(2)}, u32[]{:S(2)}) async-start(bf16[64,16,128]{2,1,0:T(8,128)(2,1)} %bitcast.60), calls=%async_computation.3 | async-start | bytes 524288 | tf_op jit(solution)/shard_map/all_to_all | solution.py:153
  125.8 0.8 fusion.48
  126.6 12.3 %all-to-all-done.3 = bf16[64,16,128]{2,1,0:T(8,128)(2,1)S(1)} async-done(((bf16[64,16,128]{2,1,0:T(8,128)(2,1)}), bf16[64,16,128]{2,1,0:T(8,128)(2,1)S(1)}, u32[]{:S(2)}, u32[]{:S(2)}) %all-to-all-start.3) | async-done | bytes 262176 | tf_op jit(solution)/shard_map/all_to_all | solution.py:153
  139.4 0.7 copy.91
  (47 shorter events, 4.1 us)
Async XLA Ops:
  2.1 23.0 %all-to-all-start = ((s32[64,1,1]{2,1,0:T(1,128)}), s32[64,1,1]{2,1,0:T(1,128)S(1)}, u32[]{:S(2)}, u32[]{:S(2)}) async-start(s32[64,1,1]{2,1,0:T(1,128)} %copy.75), calls=%async_computation | async-start | bytes 65536 | tf_op jit(solution)/shard_map/all_to_all | solution.py:93
  15.9 5.2 %copy-start.1 = (bf16[2560,1,160]{0,2,1:T(8,128)(2,1)S(1)}, bf16[2560,1,160]{0,2,1:T(8,128)(2,1)}, u32[]{:S(2)}) copy-start(bf16[2560,1,160]{0,2,1:T(8,128)(2,1)} %param.12) | copy-start | bytes 2457604
  21.8 15.9 %copy-start.5 = (s32[32]{0:T(128)S(1)}, s32[32]{0:T(128)}, u32[]{:S(2)}) copy-start(s32[32]{0:T(128)} %param.16) | copy-start | bytes 388
  27.4 23.5 %all-to-all-start.1 = ((bf16[64,16,128]{2,1,0:T(8,128)(2,1)}), bf16[64,16,128]{2,1,0:T(8,128)(2,1)S(1)}, u32[]{:S(2)}, u32[]{:S(2)}) async-start(bf16[64,16,128]{2,1,0:T(8,128)(2,1)} %bitcast.53), calls=%async_computation.1 | async-start | bytes 524288 | tf_op jit(solution)/shard_map/all_to_all | solution.py:102
  37.7 41.1 %copy-start.3 = (f32[40]{0:T(128)}, f32[40]{0:T(128)S(1)}, u32[]{:S(2)}) copy-start(f32[40]{0:T(128)S(1)} %multiply_power_fusion) | copy-start | bytes 484
  79.9 0.9 copy-start.4
  80.3 1.5 %copy-start = (bf16[8,320,320]{1,0,2:T(8,128)(2,1)S(1)}, bf16[8,320,320]{1,0,2:T(8,128)(2,1)}, u32[]{:S(2)}) copy-start(bf16[8,320,320]{1,0,2:T(8,128)(2,1)} %reshape.385) | copy-start | bytes 4915204
  81.9 1.4 %copy-start.6 = (pred[5,5]{0,1:T(8,128)(4,1)S(1)}, pred[5,5]{0,1:T(8,128)(4,1)}, u32[]{:S(2)}) copy-start(pred[5,5]{0,1:T(8,128)(4,1)} %iota_compare_fusion.8) | copy-start | bytes 79
  82.9 1.8 %copy-start.2 = (bf16[32,64,1,160]{3,1,2,0:T(8,128)(2,1)S(1)}, bf16[32,64,1,160]{3,1,2,0:T(8,128)(2,1)}, u32[]{:S(2)}) copy-start(bf16[32,64,1,160]{3,1,2,0:T(8,128)(2,1)} %param.14) | copy-start | bytes 1966084
  112.3 13.4 %copy-start.7 = (s32[32]{0:T(128)S(1)}, s32[32]{0:T(128)}, u32[]{:S(2)}) copy-start(s32[32]{0:T(128)} %param.17) | copy-start | bytes 388
  113.8 25.1 %all-to-all-start.3 = ((bf16[64,16,128]{2,1,0:T(8,128)(2,1)}), bf16[64,16,128]{2,1,0:T(8,128)(2,1)S(1)}, u32[]{:S(2)}, u32[]{:S(2)}) async-start(bf16[64,16,128]{2,1,0:T(8,128)(2,1)} %bitcast.60), calls=%async_computation.3 | async-start | bytes 524288 | tf_op jit(solution)/shard_map/all_to_all | solution.py:153

commit v4 on v3

--- a/solution.py
+++ b/solution.py
@@ -106,7 +106,9 @@
         "pi,px->ix", take, incoming, preferred_element_type=jnp.float32
     ).astype(jnp.bfloat16)
     rows = slot_count * verified
-    features = lax.all_gather(dealt_rows.reshape(rows, width), "tp", axis=0, tiled=False)
+    lanes = rows * width // 128
+    features = lax.all_gather(dealt_rows.reshape(lanes, 128), "tp", axis=0, tiled=False)
+    features = features.reshape(shards, rows, width)
     widened = features.astype(jnp.float32)
     variance = jnp.mean(widened * widened, axis=(0, 2), keepdims=True)
     gain = norm_gain.reshape(shards, 1, width).astype(jnp.float32)
@@ -143,7 +145,8 @@
         output_weight.reshape(-1, shards, width),
         preferred_element_type=jnp.float32,
     )
-    pieces = lax.all_to_all(partial_sum.astype(jnp.bfloat16), "tp", 0, 0, tiled=True)
+    pieces = partial_sum.astype(jnp.bfloat16).reshape(shards, lanes, 128)
+    pieces = lax.all_to_all(pieces, "tp", 0, 0, tiled=True)
     out_dealt = jnp.sum(pieces.astype(jnp.float32), axis=0)
     out_dealt = out_dealt.reshape(slot_count, verified, width).astype(jnp.bfloat16)
     back_out = jnp.einsum(

time: 141 us -> 139 us (0.986)
  local copies, waits for them, and re-layouts: 14.6 us -> 18.3 us
  blocking collectives: 51.8 us -> 48.5 us
  other arithmetic: 7.56 us -> 6.05 us
    all_to_all x1, blocking collectives: 24.3 us -> 21.5 us  [body(): pieces = lax.all_to_all(pieces, 'tp', 0, 0, tiled=True)]
where the time goes in v4:
time: 139 us; the launch traced here: 138 us
  blocking collectives  48.5 us (35%)
  starting transfers between devices  33.3 us (24%)
  waiting for transfers between devices  25.1 us (18%)
  local copies, waits for them, and re-layouts  18.3 us (13%)
  matrix products  6.3 us (5%)
  other arithmetic  6.05 us (4%)
    all_gather x1, blocking collectives, body(): lax.all_gather(dealt_rows.reshape(lanes, 128), 'tp', axis=0, tiled=False)  27 us
    all_to_all x1, blocking collectives, body(): pieces = lax.all_to_all(pieces, 'tp', 0, 0, tiled=True)  21.5 us
    all_to_all x1, waiting for transfers between devices, body(): incoming = lax.all_to_all(outgoing, 'req', 0, 0, tiled=True)  12.7 us
    all_to_all x1, waiting for transfers between devices, body(): returned = lax.all_to_all(back_out, 'req', 0, 0, tiled=True)  12.4 us
    all_to_all x1, starting transfers between devices, body(): wanted = lax.all_to_all(wish, 'req', 0, 0, tiled=True)  11.6 us
    all_to_all x1, starting transfers between devices, body(): returned = lax.all_to_all(back_out, 'req', 0, 0, tiled=True)  11.4 us
    all_to_all x1, starting transfers between devices, body(): incoming = lax.all_to_all(outgoing, 'req', 0, 0, tiled=True)  10.3 us
    unnamed x24, local copies, waits for them, and re-layouts  4.96 us
  transfers between devices with their start and end apart: 3, of which 2 were waited for; matrix products, arithmetic and copies ran while one was open for 9% of the time, Pallas kernels for 0%

profile of v4, /device:TPU:1, one launch (start us, length us, event | category | flops | bytes accessed | tf_op | source)
XLA Modules:
  0.0 138.5 jit_solution(7924932494184744593)
XLA Ops:
  0.6 0.7 and_select_fusion.1
  1.4 0.7 copy.91
  2.1 11.6 %all-to-all-start = ((s32[64,1,1]{2,1,0:T(1,128)}), s32[64,1,1]{2,1,0:T(1,128)S(1)}, u32[]{:S(2)}, u32[]{:S(2)}) async-start(s32[64,1,1]{2,1,0:T(1,128)} %copy.91), calls=%async_computation | async-start | bytes 65536 | tf_op jit(solution)/shard_map/all_to_all | solution.py:93
  13.8 0.7 add_convert_fusion.1
  14.4 1.0 copy.92
  15.5 0.9 reshape.407
  16.4 4.3 %reshape.392 = bf16[8,320,320]{1,0,2:T(8,128)(2,1)} reshape(bf16[2560,320]{0,1:T(8,128)(2,1)} %param.11) | data formatting | bytes 3276800 | tf_op jit(solution)/shard_map/reshape | solution.py:122
  20.7 1.7 %reshape.395 = bf16[8,320,160]{1,0,2:T(8,128)(2,1)} reshape(bf16[2560,1,160]{0,2,1:T(8,128)(2,1)S(1)} %copy-done.4) | data formatting | bytes 1638400 | tf_op jit(solution)/shard_map/reshape.11
  22.4 2.4 %reshape.401 = bf16[320,8,320]{2,1,0:T(8,128)(2,1)} reshape(bf16[320,2560]{1,0:T(8,128)(2,1)S(1)} %copy-done.2) | data formatting | bytes 3276800 | tf_op jit(solution)/shard_map/reshape | solution.py:145
  24.8 1.2 reduce.7
  26.4 0.8 copy.123
  27.1 10.3 %all-to-all-start.1 = ((bf16[64,16,128]{2,1,0:T(8,128)(2,1)}), bf16[64,16,128]{2,1,0:T(8,128)(2,1)S(1)}, u32[]{:S(2)}, u32[]{:S(2)}) async-start(bf16[64,16,128]{2,1,0:T(8,128)(2,1)} %bitcast.52), calls=%async_computation.1 | async-start | bytes 524288 | tf_op jit(solution)/shard_map/all_to_all | solution.py:102
  37.9 12.7 %all-to-all-done.1 = bf16[64,16,128]{2,1,0:T(8,128)(2,1)S(1)} async-done(((bf16[64,16,128]{2,1,0:T(8,128)(2,1)}), bf16[64,16,128]{2,1,0:T(8,128)(2,1)S(1)}, u32[]{:S(2)}, u32[]{:S(2)}) %all-to-all-start.1) | async-done | bytes 262176 | tf_op jit(solution)/shard_map/all_to_all | solution.py:102
  51.0 27.0 %all_gather.3 = bf16[8,400,128]{2,1,0:T(8,128)(2,1)S(1)} all-gather(bf16[1,400,128]{2,1,0:T(8,128)(2,1)S(1)} %all_gather_reshape.3), channel_id=1, replica_groups=mesh['req'=64,'tp'=8] {'tp'}, dimensions={0}, use_global_device_ids=true | all-gather | bytes 921600 | tf_op jit(solution)/shard_map/all_gather | solution.py:110
  78.0 0.8 reshape.406
  79.8 0.6 copy-done.3
  80.4 0.4 convolution_bitcast_fusion.1
  80.9 0.4 fusion.43
  81.5 1.0 fusion.14
  82.9 1.3 fusion.55
  84.2 0.5 fusion.54
  85.0 0.4 fusion.26
  85.5 0.8 convolution_bitcast_fusion
  86.9 0.9 copy-done
  87.9 0.7 fusion.8
  88.6 1.1 reshape.402
  89.8 21.5 %all_to_all.21 = bf16[8,400,128]{2,1,0:T(8,128)(2,1)S(1)} all-to-all(bf16[8,400,128]{2,1,0:T(8,128)(2,1)S(1)} %reshape.402), channel_id=1, replica_groups=mesh['req'=64,'tp'=8] {'tp'}, dimensions={0} | all-to-all | bytes 1638400 | tf_op jit(solution)/shard_map/all_to_all | solution.py:149
  111.9 0.7 copy.125
  112.6 11.4 %all-to-all-start.3 = ((bf16[64,16,128]{2,1,0:T(8,128)(2,1)}), bf16[64,16,128]{2,1,0:T(8,128)(2,1)S(1)}, u32[]{:S(2)}, u32[]{:S(2)}) async-start(bf16[64,16,128]{2,1,0:T(8,128)(2,1)} %bitcast.59), calls=%async_computation.3 | async-start | bytes 524288 | tf_op jit(solution)/shard_map/all_to_all | solution.py:156
  124.1 0.8 fusion.46
  124.9 12.4 %all-to-all-done.3 = bf16[64,16,128]{2,1,0:T(8,128)(2,1)S(1)} async-done(((bf16[64,16,128]{2,1,0:T(8,128)(2,1)}), bf16[64,16,128]{2,1,0:T(8,128)(2,1)S(1)}, u32[]{:S(2)}, u32[]{:S(2)}) %all-to-all-start.3) | async-done | bytes 262176 | tf_op jit(solution)/shard_map/all_to_all | solution.py:156
  137.8 0.7 copy.107
  (52 shorter events, 5.1 us)
Async XLA Ops:
  2.1 22.7 %all-to-all-start = ((s32[64,1,1]{2,1,0:T(1,128)}), s32[64,1,1]{2,1,0:T(1,128)S(1)}, u32[]{:S(2)}, u32[]{:S(2)}) async-start(s32[64,1,1]{2,1,0:T(1,128)} %copy.91), calls=%async_computation | async-start | bytes 65536 | tf_op jit(solution)/shard_map/all_to_all | solution.py:93
  15.4 5.3 %copy-start.4 = (bf16[2560,1,160]{0,2,1:T(8,128)(2,1)S(1)}, bf16[2560,1,160]{0,2,1:T(8,128)(2,1)}, u32[]{:S(2)}) copy-start(bf16[2560,1,160]{0,2,1:T(8,128)(2,1)} %param.12) | copy-start | bytes 2457604
  16.4 6.0 %copy-start.2 = (bf16[320,2560]{1,0:T(8,128)(2,1)S(1)}, bf16[320,2560]{1,0:T(8,128)(2,1)}, u32[]{:S(2)}) copy-start(bf16[320,2560]{1,0:T(8,128)(2,1)} %param.13) | copy-start | bytes 4915204
  22.4 15.0 %copy-start.6 = (s32[32]{0:T(128)S(1)}, s32[32]{0:T(128)}, u32[]{:S(2)}) copy-start(s32[32]{0:T(128)} %param.16) | copy-start | bytes 388
  27.1 23.5 %all-to-all-start.1 = ((bf16[64,16,128]{2,1,0:T(8,128)(2,1)}), bf16[64,16,128]{2,1,0:T(8,128)(2,1)S(1)}, u32[]{:S(2)}, u32[]{:S(2)}) async-start(bf16[64,16,128]{2,1,0:T(8,128)(2,1)} %bitcast.52), calls=%async_computation.1 | async-start | bytes 524288 | tf_op jit(solution)/shard_map/all_to_all | solution.py:102
  79.2 1.2 copy-start.3
  79.8 1.6 %copy-start.1 = (bf16[8,320,320]{1,0,2:T(8,128)(2,1)S(1)}, bf16[8,320,320]{1,0,2:T(8,128)(2,1)}, u32[]{:S(2)}) copy-start(bf16[8,320,320]{1,0,2:T(8,128)(2,1)} %reshape.392) | copy-start | bytes 4915204
  82.5 1.7 %copy-start.5 = (bf16[32,64,1,160]{3,1,2,0:T(8,128)(2,1)S(1)}, bf16[32,64,1,160]{3,1,2,0:T(8,128)(2,1)}, u32[]{:S(2)}) copy-start(bf16[32,64,1,160]{3,1,2,0:T(8,128)(2,1)} %param.14) | copy-start | bytes 1966084
  86.3 1.5 %copy-start = (bf16[320,8,320]{2,1,0:T(8,128)(2,1)S(1)}, bf16[320,8,320]{2,1,0:T(8,128)(2,1)}, u32[]{:S(2)}) copy-start(bf16[320,8,320]{2,1,0:T(8,128)(2,1)} %reshape.401) | copy-start | bytes 4915204
  89.8 34.3 %copy-start.7 = (s32[32]{0:T(128)S(1)}, s32[32]{0:T(128)}, u32[]{:S(2)}) copy-start(s32[32]{0:T(128)} %param.17) | copy-start | bytes 388
  112.6 24.7 %all-to-all-start.3 = ((bf16[64,16,128]{2,1,0:T(8,128)(2,1)}), bf16[64,16,128]{2,1,0:T(8,128)(2,1)S(1)}, u32[]{:S(2)}, u32[]{:S(2)}) async-start(bf16[64,16,128]{2,1,0:T(8,128)(2,1)} %bitcast.59), calls=%async_computation.3 | async-start | bytes 524288 | tf_op jit(solution)/shard_map/all_to_all | solution.py:156

commit v5 on v4

--- a/solution.py
+++ b/solution.py
@@ -107,7 +107,8 @@
     ).astype(jnp.bfloat16)
     rows = slot_count * verified
     lanes = rows * width // 128
-    features = lax.all_gather(dealt_rows.reshape(lanes, 128), "tp", axis=0, tiled=False)
+    copies = jnp.broadcast_to(dealt_rows.reshape(1, lanes, 128), (shards, lanes, 128))
+    features = lax.all_to_all(copies, "tp", 0, 0, tiled=True)
     features = features.reshape(shards, rows, width)
     widened = features.astype(jnp.float32)
     variance = jnp.mean(widened * widened, axis=(0, 2), keepdims=True)

time: 139 us -> 137 us (0.986)
  waiting for transfers between devices: 25.1 us -> 37.6 us
  starting transfers between devices: 33.3 us -> 26.5 us
  blocking collectives: 48.5 us -> 43.7 us
  local copies, waits for them, and re-layouts: 18.3 us -> 16 us
    all_gather x1 -> x0, blocking collectives: 27 us -> none  [body(): lax.all_gather(dealt_rows.reshape(lanes, 128), 'tp', axis=0, tiled=False)]
    all_to_all x0 -> x1, blocking collectives: none -> 17.3 us  [body(): incoming = lax.all_to_all(outgoing, 'req', 0, 0, tiled=True)]
    all_to_all x1, waiting for transfers between devices: 0.01 us -> 8.19 us  [body(): wanted = lax.all_to_all(wish, 'req', 0, 0, tiled=True)]
    all_to_all x1, starting transfers between devices: 11.4 us -> 4.87 us  [body(): returned = lax.all_to_all(back_out, 'req', 0, 0, tiled=True)]
    all_to_all x1, blocking collectives: 21.5 us -> 26.4 us  [body(): pieces = lax.all_to_all(pieces, 'tp', 0, 0, tiled=True)]
    all_to_all x1, waiting for transfers between devices: 12.7 us -> 17.1 us  [body(): features = lax.all_to_all(copies, 'tp', 0, 0, tiled=True)]
    reshape x1, local copies, waits for them, and re-layouts: 4.29 us -> 2.47 us  [body(): query_weight.reshape(shards, width, -1)]
    unnamed x24 -> x28, local copies, waits for them, and re-layouts: 4.96 us -> 4.27 us
  transfers between devices with their start and end apart: 3 -> 3, of which waited for: 2 -> 3; matrix products, arithmetic and copies ran while one was open for 9% -> 7% of each run, Pallas kernels for 0% -> 0%
where the time goes in v5:
time: 137 us
  blocking collectives  43.7 us (32%)
  waiting for transfers between devices  37.6 us (27%)
  starting transfers between devices  26.5 us (19%)
  local copies, waits for them, and re-layouts  16 us (12%)
  matrix products  6.3 us (5%)
  other arithmetic  5.39 us (4%)
    all_to_all x1, blocking collectives, body(): pieces = lax.all_to_all(pieces, 'tp', 0, 0, tiled=True)  26.4 us
    all_to_all x1, blocking collectives, body(): incoming = lax.all_to_all(outgoing, 'req', 0, 0, tiled=True)  17.3 us
    all_to_all x1, waiting for transfers between devices, body(): features = lax.all_to_all(copies, 'tp', 0, 0, tiled=True)  17.1 us
    all_to_all x1, waiting for transfers between devices, body(): returned = lax.all_to_all(back_out, 'req', 0, 0, tiled=True)  12.3 us
    all_to_all x1, starting transfers between devices, body(): wanted = lax.all_to_all(wish, 'req', 0, 0, tiled=True)  11.6 us
    all_to_all x1, starting transfers between devices, body(): features = lax.all_to_all(copies, 'tp', 0, 0, tiled=True)  10 us
    all_to_all x1, waiting for transfers between devices, body(): wanted = lax.all_to_all(wish, 'req', 0, 0, tiled=True)  8.19 us
    all_to_all x1, starting transfers between devices, body(): returned = lax.all_to_all(back_out, 'req', 0, 0, tiled=True)  4.87 us
  transfers between devices with their start and end apart: 3, of which 3 were waited for; matrix products, arithmetic and copies ran while one was open for 7% of the time, Pallas kernels for 0%

profile of v5, /device:TPU:1, one launch (start us, length us, event | category | flops | bytes accessed | tf_op | source)
XLA Modules:
  0.0 136.6 jit_solution(6961977407211682317)
XLA Ops:
  0.6 0.7 and_select_fusion.1
  1.4 0.7 copy.91
  2.1 11.6 %all-to-all-start = ((s32[64,1,1]{2,1,0:T(1,128)}), s32[64,1,1]{2,1,0:T(1,128)S(1)}, u32[]{:S(2)}, u32[]{:S(2)}) async-start(s32[64,1,1]{2,1,0:T(1,128)} %copy.91), calls=%async_computation | async-start | bytes 65536 | tf_op jit(solution)/shard_map/all_to_all | solution.py:93
  13.7 1.0 copy.92
  14.8 8.2 %all-to-all-done = s32[64,1,1]{2,1,0:T(1,128)S(1)} async-done(((s32[64,1,1]{2,1,0:T(1,128)}), s32[64,1,1]{2,1,0:T(1,128)S(1)}, u32[]{:S(2)}, u32[]{:S(2)}) %all-to-all-start) | async-done | bytes 288 | tf_op jit(solution)/shard_map/all_to_all | solution.py:93
  23.0 1.2 reduce.7
  24.6 17.3 %all_to_all.26 = bf16[64,16,128]{2,1,0:T(8,128)(2,1)S(1)} all-to-all(bf16[64,16,128]{2,1,0:T(8,128)(2,1)S(1)} %bitcast.113), channel_id=1, replica_groups=mesh['req'=64,'tp'=8] {'req'}, dimensions={0} | all-to-all | bytes 524288 | tf_op jit(solution)/shard_map/all_to_all | solution.py:102
  42.4 1.0 broadcast_in_dim.50
  43.5 10.0 %all-to-all-start.2 = ((bf16[8,400,128]{2,1,0:T(8,128)(2,1)}), bf16[8,400,128]{2,1,0:T(8,128)(2,1)S(1)}, u32[]{:S(2)}, u32[]{:S(2)}) async-start(bf16[8,400,128]{2,1,0:T(8,128)(2,1)} %broadcast_in_dim.50), calls=%async_computation.2 | async-start | bytes 1638400 | tf_op jit(solution)/shard_map/all_to_all | solution.py:111
  53.6 2.5 %reshape.394 = bf16[8,320,320]{1,0,2:T(8,128)(2,1)} reshape(bf16[2560,320]{0,1:T(8,128)(2,1)S(1)} %copy-done.2) | data formatting | bytes 3276800 | tf_op jit(solution)/shard_map/reshape | solution.py:123
  56.1 1.7 %reshape.397 = bf16[8,320,160]{1,0,2:T(8,128)(2,1)} reshape(bf16[2560,1,160]{0,2,1:T(8,128)(2,1)S(1)} %copy-done.5) | data formatting | bytes 1638400 | tf_op jit(solution)/shard_map/reshape.11
  57.8 2.4 %reshape.403 = bf16[320,8,320]{2,1,0:T(8,128)(2,1)} reshape(bf16[320,2560]{1,0:T(8,128)(2,1)S(1)} %copy-done.3) | data formatting | bytes 3276800 | tf_op jit(solution)/shard_map/reshape | solution.py:146
  60.3 0.4 multiply_cosine_fusion.1
  60.7 17.1 %all-to-all-done.2 = bf16[8,400,128]{2,1,0:T(8,128)(2,1)S(1)} async-done(((bf16[8,400,128]{2,1,0:T(8,128)(2,1)}), bf16[8,400,128]{2,1,0:T(8,128)(2,1)S(1)}, u32[]{:S(2)}, u32[]{:S(2)}) %all-to-all-start.2) | async-done | bytes 819232 | tf_op jit(solution)/shard_map/all_to_all | solution.py:111
  78.2 0.8 reshape.408
  79.6 0.6 copy-done.4
  80.2 0.4 convolution_bitcast_fusion.1
  80.6 0.4 fusion.43
  81.2 1.0 fusion.14
  82.7 1.3 fusion.55
  84.0 0.5 fusion.54
  84.8 0.4 fusion.26
  85.3 0.8 convolution_bitcast_fusion
  86.7 0.9 copy-done
  87.7 0.7 fusion.8
  88.4 1.1 reshape.404
  89.5 26.4 %all_to_all.27 = bf16[8,400,128]{2,1,0:T(8,128)(2,1)S(1)} all-to-all(bf16[8,400,128]{2,1,0:T(8,128)(2,1)S(1)} %reshape.404), channel_id=1, replica_groups=mesh['req'=64,'tp'=8] {'tp'}, dimensions={0} | all-to-all | bytes 1638400 | tf_op jit(solution)/shard_map/all_to_all | solution.py:150
  116.6 0.7 copy.125
  117.3 4.9 %all-to-all-start.4 = ((bf16[64,16,128]{2,1,0:T(8,128)(2,1)}), bf16[64,16,128]{2,1,0:T(8,128)(2,1)S(1)}, u32[]{:S(2)}, u32[]{:S(2)}) async-start(bf16[64,16,128]{2,1,0:T(8,128)(2,1)} %bitcast.59), calls=%async_computation.4 | async-start | bytes 524288 | tf_op jit(solution)/shard_map/all_to_all | solution.py:157
  122.3 0.8 fusion.46
  123.1 12.3 %all-to-all-done.4 = bf16[64,16,128]{2,1,0:T(8,128)(2,1)S(1)} async-done(((bf16[64,16,128]{2,1,0:T(8,128)(2,1)}), bf16[64,16,128]{2,1,0:T(8,128)(2,1)S(1)}, u32[]{:S(2)}, u32[]{:S(2)}) %all-to-all-start.4) | async-done | bytes 262176 | tf_op jit(solution)/shard_map/all_to_all | solution.py:157
  135.9 0.7 copy.107
  (57 shorter events, 4.9 us)
Async XLA Ops:
  2.1 20.9 %all-to-all-start = ((s32[64,1,1]{2,1,0:T(1,128)}), s32[64,1,1]{2,1,0:T(1,128)S(1)}, u32[]{:S(2)}, u32[]{:S(2)}) async-start(s32[64,1,1]{2,1,0:T(1,128)} %copy.91), calls=%async_computation | async-start | bytes 65536 | tf_op jit(solution)/shard_map/all_to_all | solution.py:93
  24.6 28.9 %copy-start.7 = (bf16[2560]{0:T(1024)(128)(2,1)S(1)}, bf16[2560]{0:T(1024)(128)(2,1)}, u32[]{:S(2)}) copy-start(bf16[2560]{0:T(1024)(128)(2,1)} %param.10) | copy-start | bytes 15364
  24.6 29.0 %copy-start.2 = (bf16[2560,320]{0,1:T(8,128)(2,1)S(1)}, bf16[2560,320]{0,1:T(8,128)(2,1)}, u32[]{:S(2)}) copy-start(bf16[2560,320]{0,1:T(8,128)(2,1)} %param.11) | copy-start | bytes 4915204
  43.5 34.4 %all-to-all-start.2 = ((bf16[8,400,128]{2,1,0:T(8,128)(2,1)}), bf16[8,400,128]{2,1,0:T(8,128)(2,1)S(1)}, u32[]{:S(2)}, u32[]{:S(2)}) async-start(bf16[8,400,128]{2,1,0:T(8,128)(2,1)} %broadcast_in_dim.50), calls=%async_computation.2 | async-start | bytes 1638400 | tf_op jit(solution)/shard_map/all_to_all | solution.py:111
  53.5 2.6 %copy-start.5 = (bf16[2560,1,160]{0,2,1:T(8,128)(2,1)S(1)}, bf16[2560,1,160]{0,2,1:T(8,128)(2,1)}, u32[]{:S(2)}) copy-start(bf16[2560,1,160]{0,2,1:T(8,128)(2,1)} %param.12) | copy-start | bytes 2457604
  56.1 1.7 %copy-start.3 = (bf16[320,2560]{1,0:T(8,128)(2,1)S(1)}, bf16[320,2560]{1,0:T(8,128)(2,1)}, u32[]{:S(2)}) copy-start(bf16[320,2560]{1,0:T(8,128)(2,1)} %param.13) | copy-start | bytes 4915204
  57.8 2.5 %copy-start.8 = (s32[32]{0:T(128)S(1)}, s32[32]{0:T(128)}, u32[]{:S(2)}) copy-start(s32[32]{0:T(128)} %param.16) | copy-start | bytes 388
  79.0 1.2 copy-start.4
  79.6 1.6 %copy-start.1 = (bf16[8,320,320]{1,0,2:T(8,128)(2,1)S(1)}, bf16[8,320,320]{1,0,2:T(8,128)(2,1)}, u32[]{:S(2)}) copy-start(bf16[8,320,320]{1,0,2:T(8,128)(2,1)} %reshape.394) | copy-start | bytes 4915204
  82.2 1.7 %copy-start.6 = (bf16[32,64,1,160]{3,1,2,0:T(8,128)(2,1)S(1)}, bf16[32,64,1,160]{3,1,2,0:T(8,128)(2,1)}, u32[]{:S(2)}) copy-start(bf16[32,64,1,160]{3,1,2,0:T(8,128)(2,1)} %param.14) | copy-start | bytes 1966084
  86.1 1.5 %copy-start = (bf16[320,8,320]{2,1,0:T(8,128)(2,1)S(1)}, bf16[320,8,320]{2,1,0:T(8,128)(2,1)}, u32[]{:S(2)}) copy-start(bf16[320,8,320]{2,1,0:T(8,128)(2,1)} %reshape.403) | copy-start | bytes 4915204
  89.5 32.7 %copy-start.9 = (s32[32]{0:T(128)S(1)}, s32[32]{0:T(128)}, u32[]{:S(2)}) copy-start(s32[32]{0:T(128)} %param.17) | copy-start | bytes 388
  117.3 18.0 %all-to-all-start.4 = ((bf16[64,16,128]{2,1,0:T(8,128)(2,1)}), bf16[64,16,128]{2,1,0:T(8,128)(2,1)S(1)}, u32[]{:S(2)}, u32[]{:S(2)}) async-start(bf16[64,16,128]{2,1,0:T(8,128)(2,1)} %bitcast.59), calls=%async_computation.4 | async-start | bytes 524288 | tf_op jit(solution)/shard_map/all_to_all | solution.py:157

commit v6 on v5

--- a/solution.py
+++ b/solution.py
@@ -12,12 +12,15 @@
 masked_score = -1e30
 
 
-def rotate(values, positions):
+def turning(positions):
     half_dim = HEAD_SIZE // 2
     frequency = 10000.0 ** (-2.0 * jnp.arange(half_dim, dtype=jnp.float32) / HEAD_SIZE)
     angles = positions.astype(jnp.float32)[..., None] * frequency
-    cosine_part = jnp.cos(angles)
-    sine_part = jnp.sin(angles)
+    return jnp.cos(angles), jnp.sin(angles)
+
+
+def rotate(values, cosine_part, sine_part):
+    half_dim = HEAD_SIZE // 2
     first_half = values[..., :half_dim]
     second_half = values[..., half_dim:]
     return jnp.concatenate(
@@ -29,7 +32,7 @@
     )
 
 
-def attend(query_rows, key_value_cache, fresh, cache_length):
+def attend(query_rows, key_value_cache, fresh, visible, causal):
     scale = 1.0 / math.sqrt(HEAD_SIZE)
     slot_count = query_rows.shape[0]
     verified = query_rows.shape[1]
@@ -41,15 +44,10 @@
         jnp.einsum("rtghd,rcgd->rghtc", query_rows, cache_keys, preferred_element_type=jnp.float32)
         * scale
     )
-    visible = jnp.arange(key_value_cache.shape[1], dtype=jnp.int32)[None, :] < cache_length[:, None]
     cache_scores = jnp.where(visible[:, None, None, None, :], cache_scores, masked_score)
     fresh_scores = (
         jnp.einsum("rtghd,rugd->rghtu", query_rows, fresh_keys, preferred_element_type=jnp.float32)
         * scale
-    )
-    causal = (
-        jnp.arange(verified, dtype=jnp.int32)[:, None]
-        >= jnp.arange(verified, dtype=jnp.int32)[None, :]
     )
     fresh_scores = jnp.where(causal[None, None, None, :, :], fresh_scores, masked_score)
     largest = jnp.maximum(jnp.max(cache_scores, axis=-1), jnp.max(fresh_scores, axis=-1))[..., None]
@@ -91,6 +89,22 @@
     match = source[None, :] == jnp.arange(peers, dtype=jnp.int32)[:, None]
     wish = jnp.sum(jnp.where(match, local[None, :] + 1, 0), axis=1) - 1
     wanted = lax.all_to_all(wish, "req", 0, 0, tiled=True)
+    positions = cache_length[:, None] + jnp.arange(verified, dtype=jnp.int32)[None, :]
+    cosine_part, sine_part = turning(positions)
+    visible = jnp.arange(key_value_cache.shape[1], dtype=jnp.int32)[None, :] < cache_length[:, None]
+    causal = (
+        jnp.arange(verified, dtype=jnp.int32)[:, None]
+        >= jnp.arange(verified, dtype=jnp.int32)[None, :]
+    )
+    keep = (jnp.arange(verified, dtype=jnp.int32)[None, :] < accepted[:, None])[:, :, None, None]
+    query_t = jnp.transpose(query_weight.reshape(shards, width, -1), (2, 0, 1))
+    pair_t = jnp.transpose(key_value_matrix.reshape(shards, width, -1), (2, 0, 1))
+    out_w = output_weight.reshape(-1, shards, width)
+    gain = norm_gain.reshape(shards, 1, width).astype(jnp.float32)
+    held = (wanted, cosine_part, sine_part, visible, causal, keep, query_t, pair_t, out_w, gain, key_value_cache)
+    (wanted, cosine_part, sine_part, visible, causal, keep, query_t, pair_t, out_w, gain, key_value_cache) = (
+        lax.optimization_barrier(held)
+    )
     pick = (wanted[:, None] == jnp.arange(slot_count, dtype=jnp.int32)[None, :]).astype(jnp.bfloat16)
     row_size = verified * width
     tile = 16 * 128
@@ -112,41 +126,39 @@
     features = features.reshape(shards, rows, width)
     widened = features.astype(jnp.float32)
     variance = jnp.mean(widened * widened, axis=(0, 2), keepdims=True)
-    gain = norm_gain.reshape(shards, 1, width).astype(jnp.float32)
     normed = (widened * lax.rsqrt(variance + 1e-05) * gain).astype(jnp.bfloat16)
     heads_here = query_weight.shape[1] // HEAD_SIZE
     groups_here = key_value_matrix.shape[1]
-    positions = cache_length[:, None] + jnp.arange(verified, dtype=jnp.int32)[None, :]
     query_rows = jnp.einsum(
-        "knf,kfe->ne",
+        "knf,ekf->ne",
         normed,
-        query_weight.reshape(shards, width, -1),
+        query_t,
         preferred_element_type=jnp.float32,
     )
     query_rows = query_rows.reshape(
         slot_count, verified, groups_here, heads_here // groups_here, HEAD_SIZE
     )
-    query_rows = rotate(query_rows, positions[:, :, None, None]).astype(jnp.bfloat16)
+    query_rows = rotate(query_rows, cosine_part[:, :, None, None], sine_part[:, :, None, None]).astype(jnp.bfloat16)
     projected = jnp.einsum(
-        "knf,kfge->nge",
+        "knf,ekf->ne",
         normed,
-        key_value_matrix.reshape(shards, width, groups_here, -1),
+        pair_t,
         preferred_element_type=jnp.float32,
     ).reshape(slot_count, verified, groups_here, -1)
     fresh = jnp.concatenate(
-        [rotate(projected[..., :HEAD_SIZE], positions[:, :, None]), projected[..., HEAD_SIZE:]],
+        [rotate(projected[..., :HEAD_SIZE], cosine_part[:, :, None], sine_part[:, :, None]), projected[..., HEAD_SIZE:]],
         axis=-1,
     ).astype(jnp.bfloat16)
-    keep = (jnp.arange(verified, dtype=jnp.int32)[None, :] < accepted[:, None])[:, :, None, None]
     new_entries = jnp.where(keep, fresh, jnp.zeros_like(fresh))
-    mixed = attend(query_rows, key_value_cache, fresh, cache_length)
+    mixed = attend(query_rows, key_value_cache, fresh, visible, causal)
     partial_sum = jnp.einsum(
         "ne,ekf->knf",
         mixed.reshape(rows, -1),
-        output_weight.reshape(-1, shards, width),
+        out_w,
         preferred_element_type=jnp.float32,
     )
     pieces = partial_sum.astype(jnp.bfloat16).reshape(shards, lanes, 128)
+    pieces, new_entries = lax.optimization_barrier((pieces, new_entries))
     pieces = lax.all_to_all(pieces, "tp", 0, 0, tiled=True)
     out_dealt = jnp.sum(pieces.astype(jnp.float32), axis=0)
     out_dealt = out_dealt.reshape(slot_count, verified, width).astype(jnp.bfloat16)

time: 137 us -> 146 us (1.066)
  blocking collectives: 43.7 us -> 101 us
  waiting for transfers between devices: 37.6 us -> 0.01 us
  starting transfers between devices: 26.5 us -> 11.8 us
  other arithmetic: 5.39 us -> 8.94 us
    all_to_all x0 -> x2, blocking collectives: none -> 53.1 us  [the longest x1 33.6 us: body(): features = lax.all_to_all(copies, 'tp', 0, 0, tiled=True)]
    all_to_all x2 -> x0, waiting for transfers between devices: 29.4 us -> none  [the longest x1 17.1 us: body(): features = lax.all_to_all(copies, 'tp', 0, 0, tiled=True)]
    all_to_all x2 -> x0, starting transfers between devices: 14.9 us -> none  [the longest x1 10 us: body(): features = lax.all_to_all(copies, 'tp', 0, 0, tiled=True)]
    all_to_all x1, waiting for transfers between devices: 8.19 us -> 0.01 us  [body(): wanted = lax.all_to_all(wish, 'req', 0, 0, tiled=True)]
    all_to_all x1, blocking collectives: 17.3 us -> 23.3 us  [body(): incoming = lax.all_to_all(outgoing, 'req', 0, 0, tiled=True)]
    reshape x2 -> x4, local copies, waits for them, and re-layouts: 4.9 us -> 7.95 us  [the longest x2 3.05 us: body(): key_value_matrix.reshape(shards, width, -1)]
    all_to_all x1, blocking collectives: 26.4 us -> 24.3 us  [body(): pieces = lax.all_to_all(pieces, 'tp', 0, 0, tiled=True)]
    another operation x2 -> x1, local copies, waits for them, and re-layouts: 1.78 us -> 0.08 us
  transfers between devices with their start and end apart: 3 -> 1, of which waited for: 3 -> 0; matrix products, arithmetic and copies ran while one was open for 7% -> 10% of each run, Pallas kernels for 0% -> 0%
where the time goes in v6:
time: 146 us
  blocking collectives  101 us (69%)
  local copies, waits for them, and re-layouts  17.2 us (12%)
  starting transfers between devices  11.8 us (8%)
  other arithmetic  8.94 us (6%)
  matrix products  6.25 us (4%)
    all_to_all x1, blocking collectives, body(): features = lax.all_to_all(copies, 'tp', 0, 0, tiled=True)  33.6 us
    all_to_all x1, blocking collectives, body(): pieces = lax.all_to_all(pieces, 'tp', 0, 0, tiled=True)  24.3 us
    all_to_all x1, blocking collectives, body(): incoming = lax.all_to_all(outgoing, 'req', 0, 0, tiled=True)  23.3 us
    all_to_all x1, blocking collectives, body(): returned = lax.all_to_all(back_out, 'req', 0, 0, tiled=True)  19.6 us
    all_to_all x1, starting transfers between devices, body(): wanted = lax.all_to_all(wish, 'req', 0, 0, tiled=True)  11.8 us
    unnamed x26, local copies, waits for them, and re-layouts  3.7 us
    reshape x2, local copies, waits for them, and re-layouts, body(): key_value_matrix.reshape(shards, width, -1)  3.05 us
  transfers between devices with their start and end apart: 1, of which 0 were waited for; matrix products, arithmetic and copies ran while one was open for 10% of the time, Pallas kernels for 0%

profile of v6, /device:TPU:1, one launch (start us, length us, event | category | flops | bytes accessed | tf_op | source)
XLA Modules:
  0.0 145.8 jit_solution(2386377922485540191)
XLA Ops:
  0.6 0.7 and_select_fusion.1
  1.4 0.7 copy.91
  2.1 11.8 %all-to-all-start = ((s32[64,1,1]{2,1,0:T(1,128)}), s32[64,1,1]{2,1,0:T(1,128)}, u32[]{:S(2)}, u32[]{:S(2)}) async-start(s32[64,1,1]{2,1,0:T(1,128)} %copy.91), calls=%async_computation | async-start | bytes 65536 | tf_op jit(solution)/shard_map/all_to_all | solution.py:91
  13.9 0.6 iota_compare_fusion.8
  14.5 0.7 iota_compare_fusion.3
  15.3 0.7 add_convert_fusion.1
  15.9 1.2 iota_compare_fusion.7
  17.1 1.4 reshape.330
  18.5 0.4 multiply_sine_fusion
  18.9 1.0 copy.95
  20.0 2.0 %reshape.314 = bf16[8,320,160]{1,0,2:T(8,128)(2,1)S(1)} reshape(bf16[2560,1,160]{0,2,1:T(8,128)(2,1)} %param.12) | data formatting | bytes 1638400 | tf_op jit(solution)/shard_map/reshape | solution.py:101
  21.9 1.1 copy.160
  23.0 2.4 %reshape.313 = bf16[8,320,320]{1,0,2:T(8,128)(2,1)} reshape(bf16[2560,320]{0,1:T(8,128)(2,1)S(1)} %copy-done.2) | data formatting | bytes 3276800 | tf_op jit(solution)/shard_map/reshape | solution.py:100
  25.5 2.5 %reshape.315 = bf16[320,8,320]{2,1,0:T(8,128)(2,1)} reshape(bf16[320,2560]{1,0:T(8,128)(2,1)S(1)} %copy-done.3) | data formatting | bytes 3276800 | tf_op jit(solution)/shard_map/reshape | solution.py:102
  27.9 2.0 %reduce.7 = s32[64]{0:T(128)S(1)} reduce(s32[64,1,1]{2,1,0:T(1,128)} %all-to-all-done, s32[]{:T(128)} %constant.43.clone.1), dimensions={1,2}, to_apply=%all_to_all.18.reduce_sub_computation | reduce | bytes 516 | tf_op jit(solution)/shard_map/all_to_all | solution.py:91
  30.3 23.3 %all_to_all.29 = bf16[64,16,128]{2,1,0:T(8,128)(2,1)S(1)} all-to-all(bf16[64,16,128]{2,1,0:T(8,128)(2,1)S(1)} %bitcast.131), channel_id=1, replica_groups=mesh['req'=64,'tp'=8] {'req'}, dimensions={0} | all-to-all | bytes 524288 | tf_op jit(solution)/shard_map/all_to_all | solution.py:116
  54.1 33.6 %all_to_all.30 = bf16[8,400,128]{2,1,0:T(8,128)(2,1)S(1)} all-to-all(bf16[8,400,128]{2,1,0:T(8,128)(2,1)S(1)} %broadcast_in_dim.90), channel_id=1, replica_groups=mesh['req'=64,'tp'=8] {'tp'}, dimensions={0} | all-to-all | bytes 1638400 | tf_op jit(solution)/shard_map/all_to_all | solution.py:125
  88.1 0.8 reshape.331
  89.5 0.6 copy-done.4
  90.1 0.4 convolution_bitcast_fusion
  90.8 1.0 fusion.14
  92.5 1.3 fusion.50
  93.8 0.5 fusion.49
  94.6 0.4 fusion.26
  95.1 0.8 fusion.25
  96.5 1.0 copy-done
  97.4 0.7 fusion.8
  98.2 1.1 reshape.326
  99.3 0.8 maximum_select_fusion
  100.1 24.3 %all_to_all.31 = bf16[8,400,128]{2,1,0:T(8,128)(2,1)S(1)} all-to-all(bf16[8,400,128]{2,1,0:T(8,128)(2,1)S(1)} %reshape.326), channel_id=1, replica_groups=mesh['req'=64,'tp'=8] {'tp'}, dimensions={0} | all-to-all | bytes 1638400 | tf_op jit(solution)/shard_map/all_to_all | solution.py:162
  125.0 19.6 %all_to_all.32 = bf16[64,16,128]{2,1,0:T(8,128)(2,1)S(1)} all-to-all(bf16[64,16,128]{2,1,0:T(8,128)(2,1)S(1)} %bitcast.133), channel_id=1, replica_groups=mesh['req'=64,'tp'=8] {'req'}, dimensions={0} | all-to-all | bytes 524288 | tf_op jit(solution)/shard_map/all_to_all | solution.py:169
  145.1 0.7 copy.107
  (54 shorter events, 5.1 us)
Async XLA Ops:
  2.1 25.8 %all-to-all-start = ((s32[64,1,1]{2,1,0:T(1,128)}), s32[64,1,1]{2,1,0:T(1,128)}, u32[]{:S(2)}, u32[]{:S(2)}) async-start(s32[64,1,1]{2,1,0:T(1,128)} %copy.91), calls=%async_computation | async-start | bytes 65536 | tf_op jit(solution)/shard_map/all_to_all | solution.py:91
  19.8 3.2 %copy-start.2 = (bf16[2560,320]{0,1:T(8,128)(2,1)S(1)}, bf16[2560,320]{0,1:T(8,128)(2,1)}, u32[]{:S(2)}) copy-start(bf16[2560,320]{0,1:T(8,128)(2,1)} %param.11) | copy-start | bytes 4915204
  23.0 2.4 %copy-start.3 = (bf16[320,2560]{1,0:T(8,128)(2,1)S(1)}, bf16[320,2560]{1,0:T(8,128)(2,1)}, u32[]{:S(2)}) copy-start(bf16[320,2560]{1,0:T(8,128)(2,1)} %param.13) | copy-start | bytes 4915204
  87.8 1.0 copy-start.5
  88.9 1.2 copy-start.4
  89.2 1.6 %copy-start.1 = (bf16[8,320,320]{1,0,2:T(8,128)(2,1)S(1)}, bf16[8,320,320]{1,0,2:T(8,128)(2,1)}, u32[]{:S(2)}) copy-start(bf16[8,320,320]{1,0,2:T(8,128)(2,1)} %reshape.313) | copy-start | bytes 4915204
  91.8 0.7 copy-start.7
  91.8 2.0 %copy-start.8 = (bf16[32,64,1,160]{3,1,2,0:T(8,128)(2,1)S(1)}, bf16[32,64,1,160]{3,1,2,0:T(8,128)(2,1)}, u32[]{:S(2)}) copy-start(bf16[32,64,1,160]{3,1,2,0:T(8,128)(2,1)} %param.14) | copy-start | bytes 1966084
  95.9 1.6 %copy-start = (bf16[320,8,320]{2,1,0:T(8,128)(2,1)S(1)}, bf16[320,8,320]{2,1,0:T(8,128)(2,1)}, u32[]{:S(2)}) copy-start(bf16[320,8,320]{2,1,0:T(8,128)(2,1)} %reshape.315) | copy-start | bytes 4915204
  97.4 1.9 %copy-start.6 = (pred[32,5,1,1]{0,1,3,2:T(8,128)(4,1)S(1)}, pred[32,5,1,1]{0,1,3,2:T(8,128)(4,1)}, u32[]{:S(2)}) copy-start(pred[32,5,1,1]{0,1,3,2:T(8,128)(4,1)} %iota_compare_fusion.7) | copy-start | bytes 484

commit v7 on v6

--- a/solution.py
+++ b/solution.py
@@ -97,12 +97,10 @@
         >= jnp.arange(verified, dtype=jnp.int32)[None, :]
     )
     keep = (jnp.arange(verified, dtype=jnp.int32)[None, :] < accepted[:, None])[:, :, None, None]
-    query_t = jnp.transpose(query_weight.reshape(shards, width, -1), (2, 0, 1))
-    pair_t = jnp.transpose(key_value_matrix.reshape(shards, width, -1), (2, 0, 1))
-    out_w = output_weight.reshape(-1, shards, width)
-    gain = norm_gain.reshape(shards, 1, width).astype(jnp.float32)
-    held = (wanted, cosine_part, sine_part, visible, causal, keep, query_t, pair_t, out_w, gain, key_value_cache)
-    (wanted, cosine_part, sine_part, visible, causal, keep, query_t, pair_t, out_w, gain, key_value_cache) = (
+    pair_w = key_value_matrix.reshape(key_value_matrix.shape[0], -1)
+    gain = norm_gain.astype(jnp.float32)
+    held = (wanted, cosine_part, sine_part, visible, causal, keep, gain, key_value_cache)
+    (wanted, cosine_part, sine_part, visible, causal, keep, gain, key_value_cache) = (
         lax.optimization_barrier(held)
     )
     pick = (wanted[:, None] == jnp.arange(slot_count, dtype=jnp.int32)[None, :]).astype(jnp.bfloat16)
@@ -124,25 +122,22 @@
     copies = jnp.broadcast_to(dealt_rows.reshape(1, lanes, 128), (shards, lanes, 128))
     features = lax.all_to_all(copies, "tp", 0, 0, tiled=True)
     features = features.reshape(shards, rows, width)
-    widened = features.astype(jnp.float32)
-    variance = jnp.mean(widened * widened, axis=(0, 2), keepdims=True)
+    widened = jnp.transpose(features.astype(jnp.float32), (1, 0, 2)).reshape(rows, shards * width)
+    variance = jnp.mean(widened * widened, axis=1, keepdims=True)
     normed = (widened * lax.rsqrt(variance + 1e-05) * gain).astype(jnp.bfloat16)
     heads_here = query_weight.shape[1] // HEAD_SIZE
     groups_here = key_value_matrix.shape[1]
     query_rows = jnp.einsum(
-        "knf,ekf->ne",
-        normed,
-        query_t,
-        preferred_element_type=jnp.float32,
+        "nd,de->ne", normed, query_weight, preferred_element_type=jnp.float32
     )
     query_rows = query_rows.reshape(
         slot_count, verified, groups_here, heads_here // groups_here, HEAD_SIZE
     )
     query_rows = rotate(query_rows, cosine_part[:, :, None, None], sine_part[:, :, None, None]).astype(jnp.bfloat16)
     projected = jnp.einsum(
-        "knf,ekf->ne",
+        "nd,de->ne",
         normed,
-        pair_t,
+        pair_w,
         preferred_element_type=jnp.float32,
     ).reshape(slot_count, verified, groups_here, -1)
     fresh = jnp.concatenate(
@@ -152,11 +147,9 @@
     new_entries = jnp.where(keep, fresh, jnp.zeros_like(fresh))
     mixed = attend(query_rows, key_value_cache, fresh, visible, causal)
     partial_sum = jnp.einsum(
-        "ne,ekf->knf",
-        mixed.reshape(rows, -1),
-        out_w,
-        preferred_element_type=jnp.float32,
+        "ne,ed->nd", mixed.reshape(rows, -1), output_weight, preferred_element_type=jnp.float32
     )
+    partial_sum = jnp.transpose(partial_sum.reshape(rows, shards, width), (1, 0, 2))
     pieces = partial_sum.astype(jnp.bfloat16).reshape(shards, lanes, 128)
     pieces, new_entries = lax.optimization_barrier((pieces, new_entries))
     pieces = lax.all_to_all(pieces, "tp", 0, 0, tiled=True)

time: 146 us -> 146 us (level)
  blocking collectives: 101 us -> 62.4 us
  waiting for transfers between devices: 0.01 us -> 25.5 us
  starting transfers between devices: 11.8 us -> 21.7 us
  matrix products: 6.25 us -> 9.49 us
  local copies, waits for them, and re-layouts: 17.2 us -> 14.7 us
    all_to_all x1 -> x0, blocking collectives: 33.6 us -> none  [body(): features = lax.all_to_all(copies, 'tp', 0, 0, tiled=True)]
    all_to_all x0 -> x1, waiting for transfers between devices: none -> 20.4 us  [body(): features = lax.all_to_all(copies, 'tp', 0, 0, tiled=True)]
    all_to_all x0 -> x1, starting transfers between devices: none -> 10 us  [body(): features = lax.all_to_all(copies, 'tp', 0, 0, tiled=True)]
    reshape x4 -> x0, local copies, waits for them, and re-layouts: 7.95 us -> none  [the longest x2 3.05 us: body(): key_value_matrix.reshape(shards, width, -1)]
    all_to_all x1, waiting for transfers between devices: 0.01 us -> 5.05 us  [body(): wanted = lax.all_to_all(wish, 'req', 0, 0, tiled=True)]
    all_to_all x1, blocking collectives: 23.3 us -> 18.2 us  [body(): incoming = lax.all_to_all(outgoing, 'req', 0, 0, tiled=True)]
    dot_general x1, local copies, waits for them, and re-layouts: 0.33 us -> 3.85 us  [body(): jnp.einsum('ne,ed->nd', mixed.reshape(rows, -1), output_weight, preferred...]
    dot_general x3, matrix products: 2.18 us -> 5.42 us  [the longest x1 2.42 us: body(): jnp.einsum('ne,ed->nd', mixed.reshape(rows, -1), output_weight, preferred...]
  transfers between devices with their start and end apart: 1 -> 2, of which waited for: 0 -> 2; matrix products, arithmetic and copies ran while one was open for 10% -> 6% of each run, Pallas kernels for 0% -> 0%
where the time goes in v7:
time: 146 us; the launch traced here: 145 us
  blocking collectives  62.4 us (43%)
  waiting for transfers between devices  25.5 us (17%)
  starting transfers between devices  21.7 us (15%)
  local copies, waits for them, and re-layouts  14.7 us (10%)
  other arithmetic  10.3 us (7%)
  matrix products  9.49 us (6%)
    all_to_all x1, blocking collectives, body(): pieces = lax.all_to_all(pieces, 'tp', 0, 0, tiled=True)  26.3 us
    all_to_all x1, waiting for transfers between devices, body(): features = lax.all_to_all(copies, 'tp', 0, 0, tiled=True)  20.4 us
    all_to_all x1, blocking collectives, body(): incoming = lax.all_to_all(outgoing, 'req', 0, 0, tiled=True)  18.2 us
    all_to_all x1, blocking collectives, body(): returned = lax.all_to_all(back_out, 'req', 0, 0, tiled=True)  17.9 us
    all_to_all x1, starting transfers between devices, body(): wanted = lax.all_to_all(wish, 'req', 0, 0, tiled=True)  11.6 us
    all_to_all x1, starting transfers between devices, body(): features = lax.all_to_all(copies, 'tp', 0, 0, tiled=True)  10 us
    all_to_all x1, waiting for transfers between devices, body(): wanted = lax.all_to_all(wish, 'req', 0, 0, tiled=True)  5.05 us
    dot_general x1, local copies, waits for them, and re-layouts, body(): jnp.einsum('ne,ed->nd', mixed.reshape(rows, -1), output_weight, preferred...  3.85 us
  transfers between devices with their start and end apart: 2, of which 2 were waited for; matrix products, arithmetic and copies ran while one was open for 6% of the time, Pallas kernels for 0%

profile of v7, /device:TPU:1, one launch (start us, length us, event | category | flops | bytes accessed | tf_op | source)
XLA Modules:
  0.0 145.0 jit_solution(7072114722944065874)
XLA Ops:
  0.6 0.8 and_select_fusion.1
  1.5 0.7 copy.82
  2.2 11.6 %all-to-all-start = ((s32[64,1,1]{2,1,0:T(1,128)}), s32[64,1,1]{2,1,0:T(1,128)S(1)}, u32[]{:S(2)}, u32[]{:S(2)}) async-start(s32[64,1,1]{2,1,0:T(1,128)} %copy.82), calls=%async_computation | async-start | bytes 65536 | tf_op jit(solution)/shard_map/all_to_all | solution.py:91
  13.9 0.7 iota_compare_fusion.3
  14.6 0.7 add_convert_fusion.1
  15.3 0.7 iota_compare_fusion.7
  15.9 0.4 multiply_sine_fusion
  16.3 0.7 convert_element_type.91
  17.0 1.0 copy.85
  18.1 5.1 %all-to-all-done = s32[64,1,1]{2,1,0:T(1,128)S(1)} async-done(((s32[64,1,1]{2,1,0:T(1,128)}), s32[64,1,1]{2,1,0:T(1,128)S(1)}, u32[]{:S(2)}, u32[]{:S(2)}) %all-to-all-start) | async-done | bytes 288 | tf_op jit(solution)/shard_map/all_to_all | solution.py:91
  23.2 1.2 reduce.7
  24.8 18.2 %all_to_all.29 = bf16[64,16,128]{2,1,0:T(8,128)(2,1)S(1)} all-to-all(bf16[64,16,128]{2,1,0:T(8,128)(2,1)S(1)} %bitcast.119), channel_id=1, replica_groups=mesh['req'=64,'tp'=8] {'req'}, dimensions={0} | all-to-all | bytes 524288 | tf_op jit(solution)/shard_map/all_to_all | solution.py:114
  43.4 1.0 broadcast_in_dim.60
  44.4 10.0 %all-to-all-start.2 = ((bf16[8,400,128]{2,1,0:T(8,128)(2,1)}), bf16[8,400,128]{2,1,0:T(8,128)(2,1)S(1)}, u32[]{:S(2)}, u32[]{:S(2)}) async-start(bf16[8,400,128]{2,1,0:T(8,128)(2,1)} %broadcast_in_dim.60), calls=%async_computation.2 | async-start | bytes 1638400 | tf_op jit(solution)/shard_map/all_to_all | solution.py:123
  54.5 3.8 %copy.110 = bf16[2560,320]{1,0:T(8,128)(2,1)} copy(bf16[2560,320]{0,1:T(8,128)(2,1)} %bitcast.117) | data formatting | bytes 3276800 | tf_op jit(solution)/shard_map/ne,ed->nd/dot_general | solution.py:149
  58.4 20.4 %all-to-all-done.2 = bf16[8,400,128]{2,1,0:T(8,128)(2,1)S(1)} async-done(((bf16[8,400,128]{2,1,0:T(8,128)(2,1)}), bf16[8,400,128]{2,1,0:T(8,128)(2,1)S(1)}, u32[]{:S(2)}, u32[]{:S(2)}) %all-to-all-start.2) | async-done | bytes 819232 | tf_op jit(solution)/shard_map/all_to_all | solution.py:123
  78.8 2.1 %reshape.340 = f32[8,160,320]{2,1,0:T(8,128)} reshape(bf16[8,400,128]{2,1,0:T(8,128)(2,1)S(1)} %all-to-all-done.2) | data formatting | bytes 2457600 | tf_op jit(solution)/shard_map/convert_element_type | solution.py:125
  80.9 1.9 %multiply_reduce_fusion = f32[160]{0:T(256)S(1)} fusion(f32[8,160,320]{2,1,0:T(8,128)} %reshape.340), kind=kLoop, calls=%fused_computation.5 | loop fusion | flops 819040 | bytes 1639040 | tf_op jit(solution)/shard_map/reduce_sum | solution.py:126
  83.6 1.8 %convert_element_type.98 = bf16[32,5,2560]{2,1,0:T(8,128)(2,1)} reshape(bf16[160,8,320]{2,1,0:T(8,128)(2,1)S(1)} %copy.86) | data formatting | bytes 1638400 | tf_op jit(solution)/shard_map/convert_element_type | solution.py:127
  85.5 2.1 %convolution_bitcast_fusion.1 = f32[32,5,1,160]{3,0,1,2:T(8,128)S(1)} fusion(bf16[2560,1,160]{0,2,1:T(8,128)(2,1)} %param.12, bf16[32,5,2560]{2,1,0:T(8,128)(2,1)} %convert_element_type.98), kind=kOutput, calls=%fused_computation.19 | convolution fusion | flops 131072000 | bytes 1740800 | tf_op jit(solution)/shard_map/nd,de->ne/dot_general | solution.py:137
  87.7 0.7 slice.77
  88.5 0.9 convolution_bitcast_fusion
  89.8 1.3 fusion.37
  91.1 0.5 fusion.36
  91.9 0.4 fusion.13
  92.4 0.8 fusion.12
  93.8 2.4 %fusion = bf16[8,160,320]{2,1,0:T(8,128)(2,1)S(1)} fusion(bf16[160,320,1]{1,0,2:T(8,128)(2,1)S(1)} %reshape.348, bf16[8,320,320]{2,1,0:T(8,128)(2,1)} %bitcast.116), kind=kOutput, calls=%fused_computation.7 | convolution fusion | flops 262553600 | bytes 2560000 | tf_op jit(solution)/shard_map/ne,ed->nd/dot_general | solution.py:149
  96.2 1.1 reshape.336
  97.3 1.6 %maximum_select_fusion = bf16[32,5,1,160]{3,0,1,2:T(8,128)(2,1)} fusion(bf16[32,5,1,80]{3,0,1,2:T(8,128)(2,1)} %slice.77, bf16[32,5,1,40]{3,0,1,2:T(8,128)(2,1)S(1)} %get-tuple-element.37, bf16[32,5,1,40]{3,0,1,2:T(8,128)(2,1)S(1)} %get-tuple-element.36, pred[32,5]{0,1:T(8,128)(4,1)S(1)} %bitcast.126), kind=kLoop, calls=%fused_computation.53 | loop fusion | flops 179200 | bytes 102560 | tf_op jit(solution)/shard_map/jit(_where)/select_n | solution.py:147
  98.9 26.3 %all_to_all.30 = bf16[8,400,128]{2,1,0:T(8,128)(2,1)S(1)} all-to-all(bf16[8,400,128]{2,1,0:T(8,128)(2,1)S(1)} %reshape.336), channel_id=1, replica_groups=mesh['req'=64,'tp'=8] {'tp'}, dimensions={0} | all-to-all | bytes 1638400 | tf_op jit(solution)/shard_map/all_to_all | solution.py:155
  125.8 17.9 %all_to_all.31 = bf16[64,16,128]{2,1,0:T(8,128)(2,1)S(1)} all-to-all(bf16[64,16,128]{2,1,0:T(8,128)(2,1)S(1)} %bitcast.121), channel_id=1, replica_groups=mesh['req'=64,'tp'=8] {'req'}, dimensions={0} | all-to-all | bytes 524288 | tf_op jit(solution)/shard_map/all_to_all | solution.py:162
  144.3 0.7 copy.96
  (42 shorter events, 4.6 us)
Async XLA Ops:
  0.6 87.8 %copy-start = (bf16[2560,320]{0,1:T(8,128)(2,1)S(1)}, bf16[2560,320]{0,1:T(8,128)(2,1)}, u32[]{:S(2)}) copy-start(bf16[2560,320]{0,1:T(8,128)(2,1)} %param.11) | copy-start | bytes 4915204
  2.2 20.9 %all-to-all-start = ((s32[64,1,1]{2,1,0:T(1,128)}), s32[64,1,1]{2,1,0:T(1,128)S(1)}, u32[]{:S(2)}, u32[]{:S(2)}) async-start(s32[64,1,1]{2,1,0:T(1,128)} %copy.82), calls=%async_computation | async-start | bytes 65536 | tf_op jit(solution)/shard_map/all_to_all | solution.py:91
  44.4 34.4 %all-to-all-start.2 = ((bf16[8,400,128]{2,1,0:T(8,128)(2,1)}), bf16[8,400,128]{2,1,0:T(8,128)(2,1)S(1)}, u32[]{:S(2)}, u32[]{:S(2)}) async-start(bf16[8,400,128]{2,1,0:T(8,128)(2,1)} %broadcast_in_dim.60), calls=%async_computation.2 | async-start | bytes 1638400 | tf_op jit(solution)/shard_map/all_to_all | solution.py:123
  80.9 2.1 %copy-start.1 = (f32[8,160,320]{2,1,0:T(8,128)S(1)}, f32[8,160,320]{2,1,0:T(8,128)}, u32[]{:S(2)}) copy-start(f32[8,160,320]{2,1,0:T(8,128)} %reshape.340) | copy-start | bytes 4915204
  85.5 3.0 %copy-start.2 = (bf16[32,5,2560]{2,1,0:T(8,128)(2,1)S(1)}, bf16[32,5,2560]{2,1,0:T(8,128)(2,1)}, u32[]{:S(2)}) copy-start(bf16[32,5,2560]{2,1,0:T(8,128)(2,1)} %convert_element_type.98) | copy-start | bytes 2457604
  89.4 1.7 %copy-start.3 = (bf16[32,64,1,160]{3,1,2,0:T(8,128)(2,1)S(1)}, bf16[32,64,1,160]{3,1,2,0:T(8,128)(2,1)}, u32[]{:S(2)}) copy-start(bf16[32,64,1,160]{3,1,2,0:T(8,128)(2,1)} %param.14) | copy-start | bytes 1966084

commit v8 on v6

--- a/solution.py
+++ b/solution.py
@@ -97,14 +97,9 @@
         >= jnp.arange(verified, dtype=jnp.int32)[None, :]
     )
     keep = (jnp.arange(verified, dtype=jnp.int32)[None, :] < accepted[:, None])[:, :, None, None]
-    query_t = jnp.transpose(query_weight.reshape(shards, width, -1), (2, 0, 1))
-    pair_t = jnp.transpose(key_value_matrix.reshape(shards, width, -1), (2, 0, 1))
-    out_w = output_weight.reshape(-1, shards, width)
     gain = norm_gain.reshape(shards, 1, width).astype(jnp.float32)
-    held = (wanted, cosine_part, sine_part, visible, causal, keep, query_t, pair_t, out_w, gain, key_value_cache)
-    (wanted, cosine_part, sine_part, visible, causal, keep, query_t, pair_t, out_w, gain, key_value_cache) = (
-        lax.optimization_barrier(held)
-    )
+    held = (wanted, cosine_part, sine_part, visible, causal, keep, gain)
+    (wanted, cosine_part, sine_part, visible, causal, keep, gain) = lax.optimization_barrier(held)
     pick = (wanted[:, None] == jnp.arange(slot_count, dtype=jnp.int32)[None, :]).astype(jnp.bfloat16)
     row_size = verified * width
     tile = 16 * 128
@@ -121,8 +116,7 @@
     ).astype(jnp.bfloat16)
     rows = slot_count * verified
     lanes = rows * width // 128
-    copies = jnp.broadcast_to(dealt_rows.reshape(1, lanes, 128), (shards, lanes, 128))
-    features = lax.all_to_all(copies, "tp", 0, 0, tiled=True)
+    features = lax.all_gather(dealt_rows.reshape(lanes, 128), "tp", axis=0, tiled=False)
     features = features.reshape(shards, rows, width)
     widened = features.astype(jnp.float32)
     variance = jnp.mean(widened * widened, axis=(0, 2), keepdims=True)
@@ -130,9 +124,9 @@
     heads_here = query_weight.shape[1] // HEAD_SIZE
     groups_here = key_value_matrix.shape[1]
     query_rows = jnp.einsum(
-        "knf,ekf->ne",
+        "knf,kfe->ne",
         normed,
-        query_t,
+        query_weight.reshape(shards, width, -1),
         preferred_element_type=jnp.float32,
     )
     query_rows = query_rows.reshape(
@@ -140,9 +134,9 @@
     )
     query_rows = rotate(query_rows, cosine_part[:, :, None, None], sine_part[:, :, None, None]).astype(jnp.bfloat16)
     projected = jnp.einsum(
-        "knf,ekf->ne",
+        "knf,kfge->nge",
         normed,
-        pair_t,
+        key_value_matrix.reshape(shards, width, groups_here, -1),
         preferred_element_type=jnp.float32,
     ).reshape(slot_count, verified, groups_here, -1)
     fresh = jnp.concatenate(
@@ -154,11 +148,10 @@
     partial_sum = jnp.einsum(
         "ne,ekf->knf",
         mixed.reshape(rows, -1),
-        out_w,
+        output_weight.reshape(-1, shards, width),
         preferred_element_type=jnp.float32,
     )
     pieces = partial_sum.astype(jnp.bfloat16).reshape(shards, lanes, 128)
-    pieces, new_entries = lax.optimization_barrier((pieces, new_entries))
     pieces = lax.all_to_all(pieces, "tp", 0, 0, tiled=True)
     out_dealt = jnp.sum(pieces.astype(jnp.float32), axis=0)
     out_dealt = out_dealt.reshape(slot_count, verified, width).astype(jnp.bfloat16)

time: 146 us -> 135 us (0.925)
  blocking collectives: 101 us -> 48.5 us
  waiting for transfers between devices: 0.01 us -> 22.2 us
  starting transfers between devices: 11.8 us -> 30.1 us
    all_to_all x3 -> x0, blocking collectives: 76.4 us -> none  [the longest x1 33.6 us: body(): features = lax.all_to_all(copies, 'tp', 0, 0, tiled=True)]
    all_gather x0 -> x1, blocking collectives: none -> 27 us  [body(): lax.all_gather(dealt_rows.reshape(lanes, 128), 'tp', axis=0, tiled=False)]
    all_to_all x0 -> x2, waiting for transfers between devices: none -> 18.9 us  [the longest x1 12.4 us: body(): returned = lax.all_to_all(back_out, 'req', 0, 0, tiled=True)]
    all_to_all x0 -> x2, starting transfers between devices: none -> 18.5 us  [the longest x1 11.4 us: body(): returned = lax.all_to_all(back_out, 'req', 0, 0, tiled=True)]
    all_to_all x1, waiting for transfers between devices: 0.01 us -> 3.25 us  [body(): wanted = lax.all_to_all(wish, 'req', 0, 0, tiled=True)]
    reshape x4 -> x2, local copies, waits for them, and re-layouts: 7.95 us -> 4.91 us  [the longest x1 2.48 us: body(): output_weight.reshape(-1, shards, width)]
    all_to_all x1, blocking collectives: 24.3 us -> 21.5 us  [body(): pieces = lax.all_to_all(pieces, 'tp', 0, 0, tiled=True)]
    unnamed x26 -> x40, local copies, waits for them, and re-layouts: 3.7 us -> 5.82 us
  transfers between devices with their start and end apart: 1 -> 3, of which waited for: 0 -> 3; matrix products, arithmetic and copies ran while one was open for 10% -> 10% of each run, Pallas kernels for 0% -> 0%
where the time goes in v8:
time: 135 us; the launch traced here: 134 us
  blocking collectives  48.5 us (36%)
  starting transfers between devices  30.1 us (22%)
  waiting for transfers between devices  22.2 us (16%)
  local copies, waits for them, and re-layouts  17.2 us (13%)
  other arithmetic  8.95 us (7%)
  matrix products  6.3 us (5%)
    all_gather x1, blocking collectives, body(): lax.all_gather(dealt_rows.reshape(lanes, 128), 'tp', axis=0, tiled=False)  27 us
    all_to_all x1, blocking collectives, body(): pieces = lax.all_to_all(pieces, 'tp', 0, 0, tiled=True)  21.5 us
    all_to_all x1, waiting for transfers between devices, body(): returned = lax.all_to_all(back_out, 'req', 0, 0, tiled=True)  12.4 us
    all_to_all x1, starting transfers between devices, body(): wanted = lax.all_to_all(wish, 'req', 0, 0, tiled=True)  11.6 us
    all_to_all x1, starting transfers between devices, body(): returned = lax.all_to_all(back_out, 'req', 0, 0, tiled=True)  11.4 us
    all_to_all x1, starting transfers between devices, body(): incoming = lax.all_to_all(outgoing, 'req', 0, 0, tiled=True)  7.05 us
    all_to_all x1, waiting for transfers between devices, body(): incoming = lax.all_to_all(outgoing, 'req', 0, 0, tiled=True)  6.53 us
    unnamed x40, local copies, waits for them, and re-layouts  5.82 us
  transfers between devices with their start and end apart: 3, of which 3 were waited for; matrix products, arithmetic and copies ran while one was open for 10% of the time, Pallas kernels for 0%

profile of v8, /device:TPU:1, one launch (start us, length us, event | category | flops | bytes accessed | tf_op | source)
XLA Modules:
  0.0 134.2 jit_solution(17697620083008109449)
XLA Ops:
  0.6 0.7 and_select_fusion.1
  2.0 0.7 copy.91
  2.7 11.6 %all-to-all-start = ((s32[64,1,1]{2,1,0:T(1,128)}), s32[64,1,1]{2,1,0:T(1,128)S(1)}, u32[]{:S(2)}, u32[]{:S(2)}) async-start(s32[64,1,1]{2,1,0:T(1,128)} %copy.91), calls=%async_computation | async-start | bytes 65536 | tf_op jit(solution)/shard_map/all_to_all | solution.py:91
  14.4 0.7 add_convert_fusion.1
  15.0 0.7 iota_compare_fusion.3
  15.8 1.2 iota_compare_fusion.7
  17.0 1.0 multiply_sine_fusion
  18.0 0.6 iota_compare_fusion.8
  18.6 0.8 reshape.334
  19.4 1.0 copy.92
  20.5 3.3 %all-to-all-done = s32[64,1,1]{2,1,0:T(1,128)S(1)} async-done(((s32[64,1,1]{2,1,0:T(1,128)}), s32[64,1,1]{2,1,0:T(1,128)S(1)}, u32[]{:S(2)}, u32[]{:S(2)}) %all-to-all-start) | async-done | bytes 288 | tf_op jit(solution)/shard_map/all_to_all | solution.py:91
  23.7 1.2 reduce.7
  25.3 0.8 copy.123
  26.0 7.0 %all-to-all-start.1 = ((bf16[64,16,128]{2,1,0:T(8,128)(2,1)}), bf16[64,16,128]{2,1,0:T(8,128)(2,1)S(1)}, u32[]{:S(2)}, u32[]{:S(2)}) async-start(bf16[64,16,128]{2,1,0:T(8,128)(2,1)} %bitcast.56), calls=%async_computation.1 | async-start | bytes 524288 | tf_op jit(solution)/shard_map/all_to_all | solution.py:111
  33.1 1.7 %reshape.323 = bf16[8,320,160]{1,0,2:T(8,128)(2,1)} reshape(bf16[2560,1,160]{0,2,1:T(8,128)(2,1)S(1)} %copy-done.5) | data formatting | bytes 1638400 | tf_op jit(solution)/shard_map/reshape.9
  34.8 2.4 %reshape.320 = bf16[8,320,320]{1,0,2:T(8,128)(2,1)} reshape(bf16[2560,320]{0,1:T(8,128)(2,1)S(1)} %copy-done.2) | data formatting | bytes 3276800 | tf_op jit(solution)/shard_map/reshape | solution.py:129
  37.2 2.5 %reshape.329 = bf16[320,8,320]{2,1,0:T(8,128)(2,1)} reshape(bf16[320,2560]{1,0:T(8,128)(2,1)S(1)} %copy-done.3) | data formatting | bytes 3276800 | tf_op jit(solution)/shard_map/reshape | solution.py:151
  39.7 6.5 %all-to-all-done.1 = bf16[64,16,128]{2,1,0:T(8,128)(2,1)S(1)} async-done(((bf16[64,16,128]{2,1,0:T(8,128)(2,1)}), bf16[64,16,128]{2,1,0:T(8,128)(2,1)S(1)}, u32[]{:S(2)}, u32[]{:S(2)}) %all-to-all-start.1) | async-done | bytes 262176 | tf_op jit(solution)/shard_map/all_to_all | solution.py:111
  46.7 27.0 %all_gather.3 = bf16[8,400,128]{2,1,0:T(8,128)(2,1)S(1)} all-gather(bf16[1,400,128]{2,1,0:T(8,128)(2,1)S(1)} %all_gather_reshape.3), channel_id=1, replica_groups=mesh['req'=64,'tp'=8] {'tp'}, dimensions={0}, use_global_device_ids=true | all-gather | bytes 921600 | tf_op jit(solution)/shard_map/all_gather | solution.py:119
  73.7 0.8 reshape.335
  77.2 1.0 fusion.14
  78.6 1.3 fusion.51
  81.2 0.9 convolution_bitcast_fusion
  82.7 0.9 copy-done
  83.6 0.7 fusion.8
  84.4 1.1 reshape.330
  85.5 21.5 %all_to_all.24 = bf16[8,400,128]{2,1,0:T(8,128)(2,1)S(1)} all-to-all(bf16[8,400,128]{2,1,0:T(8,128)(2,1)S(1)} %reshape.330), channel_id=1, replica_groups=mesh['req'=64,'tp'=8] {'tp'}, dimensions={0} | all-to-all | bytes 1638400 | tf_op jit(solution)/shard_map/all_to_all | solution.py:155
  107.6 0.7 copy.125
  108.3 11.4 %all-to-all-start.3 = ((bf16[64,16,128]{2,1,0:T(8,128)(2,1)}), bf16[64,16,128]{2,1,0:T(8,128)(2,1)S(1)}, u32[]{:S(2)}, u32[]{:S(2)}) async-start(bf16[64,16,128]{2,1,0:T(8,128)(2,1)} %bitcast.63), calls=%async_computation.3 | async-start | bytes 524288 | tf_op jit(solution)/shard_map/all_to_all | solution.py:162
  119.8 0.8 fusion.38
  120.6 12.4 %all-to-all-done.3 = bf16[64,16,128]{2,1,0:T(8,128)(2,1)S(1)} async-done(((bf16[64,16,128]{2,1,0:T(8,128)(2,1)}), bf16[64,16,128]{2,1,0:T(8,128)(2,1)S(1)}, u32[]{:S(2)}, u32[]{:S(2)}) %all-to-all-start.3) | async-done | bytes 262176 | tf_op jit(solution)/shard_map/all_to_all | solution.py:162
  133.5 0.7 copy.107
  (68 shorter events, 7.6 us)
Async XLA Ops:
  0.6 32.5 %copy-start.5 = (bf16[2560,1,160]{0,2,1:T(8,128)(2,1)S(1)}, bf16[2560,1,160]{0,2,1:T(8,128)(2,1)}, u32[]{:S(2)}) copy-start(bf16[2560,1,160]{0,2,1:T(8,128)(2,1)} %param.12) | copy-start | bytes 2457604
  1.4 0.5 copy-start.11
  2.7 21.0 %all-to-all-start = ((s32[64,1,1]{2,1,0:T(1,128)}), s32[64,1,1]{2,1,0:T(1,128)S(1)}, u32[]{:S(2)}, u32[]{:S(2)}) async-start(s32[64,1,1]{2,1,0:T(1,128)} %copy.91), calls=%async_computation | async-start | bytes 65536 | tf_op jit(solution)/shard_map/all_to_all | solution.py:91
  20.3 14.5 %copy-start.2 = (bf16[2560,320]{0,1:T(8,128)(2,1)S(1)}, bf16[2560,320]{0,1:T(8,128)(2,1)}, u32[]{:S(2)}) copy-start(bf16[2560,320]{0,1:T(8,128)(2,1)} %param.11) | copy-start | bytes 4915204
  25.0 8.1 %copy-start.9 = (s32[64]{0:T(128)}, s32[64]{0:T(128)S(1)}, u32[]{:S(2)}) copy-start(s32[64]{0:T(128)S(1)} %reduce.7) | copy-start | bytes 772
  26.0 20.2 %all-to-all-start.1 = ((bf16[64,16,128]{2,1,0:T(8,128)(2,1)}), bf16[64,16,128]{2,1,0:T(8,128)(2,1)S(1)}, u32[]{:S(2)}, u32[]{:S(2)}) async-start(bf16[64,16,128]{2,1,0:T(8,128)(2,1)} %bitcast.56), calls=%async_computation.1 | async-start | bytes 524288 | tf_op jit(solution)/shard_map/all_to_all | solution.py:111
  34.8 2.4 %copy-start.3 = (bf16[320,2560]{1,0:T(8,128)(2,1)S(1)}, bf16[320,2560]{1,0:T(8,128)(2,1)}, u32[]{:S(2)}) copy-start(bf16[320,2560]{1,0:T(8,128)(2,1)} %param.13) | copy-start | bytes 4915204
  37.2 9.1 %copy-start.12 = (s32[32]{0:T(128)S(1)}, s32[32]{0:T(128)}, u32[]{:S(2)}) copy-start(s32[32]{0:T(128)} %copy-done.11) | copy-start | bytes 388
  74.9 1.2 copy-start.4
  75.2 1.4 %copy-start.6 = (f32[32,5,40]{2,0,1:T(8,128)S(1)}, f32[32,5,40]{2,0,1:T(8,128)}, u32[]{:S(2)}) copy-start(f32[32,5,40]{2,0,1:T(8,128)} %get-tuple-element.13) | copy-start | bytes 76804
  75.2 1.4 %copy-start.7 = (f32[32,5,40]{2,0,1:T(8,128)S(1)}, f32[32,5,40]{2,0,1:T(8,128)}, u32[]{:S(2)}) copy-start(f32[32,5,40]{2,0,1:T(8,128)} %get-tuple-element.12) | copy-start | bytes 76804
  75.5 1.6 %copy-start.1 = (bf16[8,320,320]{1,0,2:T(8,128)(2,1)S(1)}, bf16[8,320,320]{1,0,2:T(8,128)(2,1)}, u32[]{:S(2)}) copy-start(bf16[8,320,320]{1,0,2:T(8,128)(2,1)} %reshape.320) | copy-start | bytes 4915204
  77.2 1.4 %copy-start.15 = (pred[5,5]{0,1:T(8,128)(4,1)S(1)}, pred[5,5]{0,1:T(8,128)(4,1)}, u32[]{:S(2)}) copy-start(pred[5,5]{0,1:T(8,128)(4,1)} %iota_compare_fusion.8) | copy-start | bytes 79
  78.2 1.8 %copy-start.8 = (bf16[32,64,1,160]{3,1,2,0:T(8,128)(2,1)S(1)}, bf16[32,64,1,160]{3,1,2,0:T(8,128)(2,1)}, u32[]{:S(2)}) copy-start(bf16[32,64,1,160]{3,1,2,0:T(8,128)(2,1)} %param.14) | copy-start | bytes 1966084
  82.1 1.5 %copy-start = (bf16[320,8,320]{2,1,0:T(8,128)(2,1)S(1)}, bf16[320,8,320]{2,1,0:T(8,128)(2,1)}, u32[]{:S(2)}) copy-start(bf16[320,8,320]{2,1,0:T(8,128)(2,1)} %reshape.329) | copy-start | bytes 4915204
  84.3 22.9 %copy-start.13 = (s32[32]{0:T(128)S(1)}, s32[32]{0:T(128)}, u32[]{:S(2)}) copy-start(s32[32]{0:T(128)} %copy-done.11) | copy-start | bytes 388
  85.5 34.3 %copy-start.14 = (pred[32,5,1,1]{0,1,3,2:T(8,128)(4,1)S(1)}, pred[32,5,1,1]{0,1,3,2:T(8,128)(4,1)}, u32[]{:S(2)}) copy-start(pred[32,5,1,1]{0,1,3,2:T(8,128)(4,1)} %iota_compare_fusion.7) | copy-start | bytes 484
  107.0 26.1 %copy-start.10 = (s32[64]{0:T(128)S(1)}, s32[64]{0:T(128)}, u32[]{:S(2)}) copy-start(s32[64]{0:T(128)} %copy-done.9) | copy-start | bytes 772
  108.3 24.7 %all-to-all-start.3 = ((bf16[64,16,128]{2,1,0:T(8,128)(2,1)}), bf16[64,16,128]{2,1,0:T(8,128)(2,1)S(1)}, u32[]{:S(2)}, u32[]{:S(2)}) async-start(bf16[64,16,128]{2,1,0:T(8,128)(2,1)} %bitcast.63), calls=%async_computation.3 | async-start | bytes 524288 | tf_op jit(solution)/shard_map/all_to_all | solution.py:162

commit v9 on v8

--- a/solution.py
+++ b/solution.py
@@ -4,7 +4,7 @@
 import jax
 import jax.numpy as jnp
 from jax import lax
-from jax.sharding import PartitionSpec as P
+from jax.sharding import Mesh, PartitionSpec as P
 
 HEAD_SIZE = 80
 
@@ -104,19 +104,22 @@
     row_size = verified * width
     tile = 16 * 128
     padded = -(-row_size // tile) * tile
+    partner = lax.ppermute(hidden, "tp_lo", [(0, 1), (1, 0)])
+    low = lax.axis_index("tp_lo")
+    pair = jnp.where(low == 0, jnp.stack([hidden, partner]), jnp.stack([partner, hidden]))
     outgoing = jnp.einsum(
-        "dj,jx->dx", pick, hidden.reshape(slot_count, row_size), preferred_element_type=jnp.float32
+        "dj,qjx->dqx", pick, pair.reshape(2, slot_count, row_size), preferred_element_type=jnp.float32
     ).astype(jnp.bfloat16)
-    outgoing = jnp.pad(outgoing, ((0, 0), (0, padded - row_size))).reshape(peers, padded // 128, 128)
+    outgoing = jnp.pad(outgoing, ((0, 0), (0, 0), (0, padded - row_size))).reshape(peers, 2 * padded // 128, 128)
     incoming = lax.all_to_all(outgoing, "req", 0, 0, tiled=True)
-    incoming = incoming.reshape(peers, padded)[:, :row_size]
+    incoming = incoming.reshape(peers, 2, padded)[:, :, :row_size]
     take = match.astype(jnp.bfloat16)
     dealt_rows = jnp.einsum(
-        "pi,px->ix", take, incoming, preferred_element_type=jnp.float32
+        "pi,pqx->qix", take, incoming, preferred_element_type=jnp.float32
     ).astype(jnp.bfloat16)
     rows = slot_count * verified
     lanes = rows * width // 128
-    features = lax.all_gather(dealt_rows.reshape(lanes, 128), "tp", axis=0, tiled=False)
+    features = lax.all_gather(dealt_rows.reshape(2, lanes, 128), "tp_hi", axis=0, tiled=False)
     features = features.reshape(shards, rows, width)
     widened = features.astype(jnp.float32)
     variance = jnp.mean(widened * widened, axis=(0, 2), keepdims=True)
@@ -152,7 +155,7 @@
         preferred_element_type=jnp.float32,
     )
     pieces = partial_sum.astype(jnp.bfloat16).reshape(shards, lanes, 128)
-    pieces = lax.all_to_all(pieces, "tp", 0, 0, tiled=True)
+    pieces = lax.all_to_all(pieces, ("tp_hi", "tp_lo"), 0, 0, tiled=True)
     out_dealt = jnp.sum(pieces.astype(jnp.float32), axis=0)
     out_dealt = out_dealt.reshape(slot_count, verified, width).astype(jnp.bfloat16)
     back_out = jnp.einsum(
@@ -168,21 +171,24 @@
 
 
 def solution(mesh):
+    req, tp = mesh.shape["req"], mesh.shape["tp"]
+    split = Mesh(mesh.devices.reshape(req, tp // 2, 2), ("req", "tp_hi", "tp_lo"))
+    both = ("tp_hi", "tp_lo")
     placed = (
-        P("req", None, "tp"),
+        P("req", None, both),
         P(),
-        P(None, "tp"),
-        P(None, "tp", None),
-        P("tp", None),
-        P("req", None, "tp", None),
+        P(None, both),
+        P(None, both, None),
+        P(both, None),
+        P("req", None, both, None),
         P("req"),
         P("req"),
         P("req"),
     )
     return jax.shard_map(
-        functools.partial(body, peers=mesh.shape["req"], shards=mesh.shape["tp"]),
-        mesh=mesh,
+        functools.partial(body, peers=req, shards=tp),
+        mesh=split,
         in_specs=placed,
-        out_specs=(P("req", None, "tp"), P("req", None, "tp", None)),
+        out_specs=(P("req", None, both), P("req", None, both, None)),
         check_vma=False,
     )

time: 135 us -> 141 us (1.044)
  local copies, waits for them, and re-layouts: 17.2 us -> 20.2 us
  starting transfers between devices: 30.1 us -> 33 us
  blocking collectives: 48.5 us -> 50.4 us
  other arithmetic: 8.95 us -> 7.07 us
    ppermute x0 -> x1, starting transfers between devices: none -> 4 us  [body(): partner = lax.ppermute(hidden, 'tp_lo', [(0, 1), (1, 0)])]
    all_to_all x1, blocking collectives: 21.5 us -> 25.2 us  [body(): pieces = lax.all_to_all(pieces, ('tp_hi', 'tp_lo'), 0, 0, tiled=True)]
    all_to_all x1, starting transfers between devices: 11.4 us -> 7.73 us  [body(): returned = lax.all_to_all(back_out, 'req', 0, 0, tiled=True)]
    all_to_all x1, waiting for transfers between devices: 6.53 us -> 9.41 us  [body(): incoming = lax.all_to_all(outgoing, 'req', 0, 0, tiled=True)]
    all_to_all x1, starting transfers between devices: 7.05 us -> 9.63 us  [body(): incoming = lax.all_to_all(outgoing, 'req', 0, 0, tiled=True)]
    all_to_all x1, waiting for transfers between devices: 3.25 us -> 0.96 us  [body(): wanted = lax.all_to_all(wish, 'req', 0, 0, tiled=True)]
    all_gather x1, blocking collectives: 27 us -> 25.2 us  [body(): lax.all_gather(dealt_rows.reshape(2, lanes, 128), 'tp_hi', axis=0, tiled=...]
    reshape x1, local copies, waits for them, and re-layouts: 2.48 us -> 4.12 us  [body(): output_weight.reshape(-1, shards, width)]
  transfers between devices with their start and end apart: 3 -> 4, of which waited for: 3 -> 3; matrix products, arithmetic and copies ran while one was open for 10% -> 10% of each run, Pallas kernels for 0% -> 0%
where the time goes in v9:
time: 141 us
  blocking collectives  50.4 us (36%)
  starting transfers between devices  33 us (23%)
  waiting for transfers between devices  22.7 us (16%)
  local copies, waits for them, and re-layouts  20.2 us (14%)
  other arithmetic  7.07 us (5%)
  matrix products  6.29 us (4%)
    all_to_all x1, blocking collectives, body(): pieces = lax.all_to_all(pieces, ('tp_hi', 'tp_lo'), 0, 0, tiled=True)  25.2 us
    all_gather x1, blocking collectives, body(): lax.all_gather(dealt_rows.reshape(2, lanes, 128), 'tp_hi', axis=0, tiled=...  25.2 us
    all_to_all x1, waiting for transfers between devices, body(): returned = lax.all_to_all(back_out, 'req', 0, 0, tiled=True)  12.3 us
    all_to_all x1, starting transfers between devices, body(): wanted = lax.all_to_all(wish, 'req', 0, 0, tiled=True)  11.6 us
    all_to_all x1, starting transfers between devices, body(): incoming = lax.all_to_all(outgoing, 'req', 0, 0, tiled=True)  9.63 us
    all_to_all x1, waiting for transfers between devices, body(): incoming = lax.all_to_all(outgoing, 'req', 0, 0, tiled=True)  9.41 us
    all_to_all x1, starting transfers between devices, body(): returned = lax.all_to_all(back_out, 'req', 0, 0, tiled=True)  7.73 us
    unnamed x18, local copies, waits for them, and re-layouts  4.85 us
  transfers between devices with their start and end apart: 4, of which 3 were waited for; matrix products, arithmetic and copies ran while one was open for 10% of the time, Pallas kernels for 0%

profile of v9, /device:TPU:1, one launch (start us, length us, event | category | flops | bytes accessed | tf_op | source)
XLA Modules:
  0.0 140.6 jit_solution(14893332172144525470)
XLA Ops:
  0.6 0.7 and_select_fusion.1
  1.4 0.7 copy.103
  2.1 11.6 %all-to-all-start = ((s32[64,1,1]{2,1,0:T(1,128)}), s32[64,1,1]{2,1,0:T(1,128)S(1)}, u32[]{:S(2)}, u32[]{:S(2)}) async-start(s32[64,1,1]{2,1,0:T(1,128)} %copy.103), calls=%async_computation | async-start | bytes 65536 | tf_op jit(solution)/shard_map/all_to_all | solution.py:91
  13.7 4.0 %collective-permute-start = (bf16[32,5,320]{2,0,1:T(8,128)(2,1)}, bf16[32,5,320]{2,0,1:T(8,128)(2,1)S(1)}, u32[]{:S(2)}, u32[]{:S(2)}) collective-permute-start(bf16[32,5,320]{2,0,1:T(8,128)(2,1)} %param.9), channel_id=1, source_target_pairs={{0,1},{1,0},{2,3},{3,2},{4,5},{5,4},{6,7},{7,6},{8,9},{9,8},{10,11... | collective-permute-start | bytes 307208 | tf_op jit(solution)/shard_map/ppermute | solution.py:107
  17.8 0.7 add_convert_fusion.1
  18.4 0.7 iota_compare_fusion.2
  19.2 0.7 iota_compare_fusion.5
  20.2 1.0 copy.104
  21.2 0.8 reshape.339
  22.1 1.0 all-to-all-done
  23.0 1.2 reduce.7
  25.7 1.1 reshape.323
  26.8 9.6 %all-to-all-start.1 = ((bf16[64,32,128]{2,1,0:T(8,128)(2,1)}), bf16[64,32,128]{2,1,0:T(8,128)(2,1)S(1)}, u32[]{:S(2)}, u32[]{:S(2)}) async-start(bf16[64,32,128]{2,1,0:T(8,128)(2,1)} %reshape.323), calls=%async_computation.1 | async-start | bytes 1048576 | tf_op jit(solution)/shard_map/all_to_all | solution.py:114
  36.4 1.7 %reshape.328 = bf16[8,320,160]{1,0,2:T(8,128)(2,1)} reshape(bf16[2560,1,160]{0,2,1:T(8,128)(2,1)S(1)} %copy-done.4) | data formatting | bytes 1638400 | tf_op jit(solution)/shard_map/reshape.9
  38.1 2.5 %reshape.325 = bf16[8,320,320]{1,0,2:T(8,128)(2,1)} reshape(bf16[2560,320]{0,1:T(8,128)(2,1)S(1)} %copy-done.2) | data formatting | bytes 3276800 | tf_op jit(solution)/shard_map/reshape | solution.py:132
  40.6 4.1 %reshape.334 = bf16[320,8,320]{2,1,0:T(8,128)(2,1)} reshape(bf16[320,2560]{1,0:T(8,128)(2,1)} %param.13) | data formatting | bytes 3276800 | tf_op jit(solution)/shard_map/reshape | solution.py:154
  44.7 9.4 %all-to-all-done.1 = bf16[64,32,128]{2,1,0:T(8,128)(2,1)S(1)} async-done(((bf16[64,32,128]{2,1,0:T(8,128)(2,1)}), bf16[64,32,128]{2,1,0:T(8,128)(2,1)S(1)}, u32[]{:S(2)}, u32[]{:S(2)}) %all-to-all-start.1) | async-done | bytes 524320 | tf_op jit(solution)/shard_map/all_to_all | solution.py:114
  55.1 25.2 %all_gather.3 = bf16[4,2,400,128]{3,2,1,0:T(8,128)(2,1)S(1)} all-gather(bf16[1,2,400,128]{3,2,1,0:T(8,128)(2,1)S(1)} %all_gather_reshape.3), channel_id=1, replica_groups=mesh['req'=64,'tp_hi'=4,'tp_lo'=2] {'tp_hi'}, dimensions={0}, use_global_device_ids=true | all-gather | bytes 1024000 | tf_op jit(solution)/shard_map/all_gather | solution.py:122
  80.3 0.8 reshape.340
  82.1 0.6 copy-done.3
  83.7 1.0 fusion.15
  85.2 1.3 fusion.63
  87.8 0.8 convolution_bitcast_fusion
  89.2 0.9 copy-done
  90.2 0.7 fusion.9
  90.9 1.1 reshape.335
  92.0 25.2 %all_to_all.24 = bf16[8,400,128]{2,1,0:T(8,128)(2,1)S(1)} all-to-all(bf16[8,400,128]{2,1,0:T(8,128)(2,1)S(1)} %reshape.335), channel_id=1, replica_groups=mesh['req'=64,'tp_hi'=4,'tp_lo'=2] {'tp_hi','tp_lo'}, dimensions={0} | all-to-all | bytes 1638400 | tf_op jit(solution)/shard_map/all_to_all | solution.py:158
  117.9 0.7 copy.140
  118.6 7.7 %all-to-all-start.3 = ((bf16[64,16,128]{2,1,0:T(8,128)(2,1)}), bf16[64,16,128]{2,1,0:T(8,128)(2,1)S(1)}, u32[]{:S(2)}, u32[]{:S(2)}) async-start(bf16[64,16,128]{2,1,0:T(8,128)(2,1)} %bitcast.63), calls=%async_computation.3 | async-start | bytes 524288 | tf_op jit(solution)/shard_map/all_to_all | solution.py:165
  126.4 0.8 fusion.45
  127.2 12.3 %all-to-all-done.3 = bf16[64,16,128]{2,1,0:T(8,128)(2,1)S(1)} async-done(((bf16[64,16,128]{2,1,0:T(8,128)(2,1)}), bf16[64,16,128]{2,1,0:T(8,128)(2,1)S(1)}, u32[]{:S(2)}, u32[]{:S(2)}) %all-to-all-start.3) | async-done | bytes 262176 | tf_op jit(solution)/shard_map/all_to_all | solution.py:165
  139.9 0.7 copy.122
  (54 shorter events, 8.2 us)
Async XLA Ops:
  2.1 20.9 %all-to-all-start = ((s32[64,1,1]{2,1,0:T(1,128)}), s32[64,1,1]{2,1,0:T(1,128)S(1)}, u32[]{:S(2)}, u32[]{:S(2)}) async-start(s32[64,1,1]{2,1,0:T(1,128)} %copy.103), calls=%async_computation | async-start | bytes 65536 | tf_op jit(solution)/shard_map/all_to_all | solution.py:91
  13.7 10.5 %collective-permute-start = (bf16[32,5,320]{2,0,1:T(8,128)(2,1)}, bf16[32,5,320]{2,0,1:T(8,128)(2,1)S(1)}, u32[]{:S(2)}, u32[]{:S(2)}) collective-permute-start(bf16[32,5,320]{2,0,1:T(8,128)(2,1)} %param.9), channel_id=1, source_target_pairs={{0,1},{1,0},{2,3},{3,2},{4,5},{5,4},{6,7},{7,6},{8,9},{9,8},{10,11... | collective-permute-start | bytes 307208 | tf_op jit(solution)/shard_map/ppermute | solution.py:107
  24.8 11.6 %copy-start.4 = (bf16[2560,1,160]{0,2,1:T(8,128)(2,1)S(1)}, bf16[2560,1,160]{0,2,1:T(8,128)(2,1)}, u32[]{:S(2)}) copy-start(bf16[2560,1,160]{0,2,1:T(8,128)(2,1)} %param.12) | copy-start | bytes 2457604
  25.7 12.5 %copy-start.2 = (bf16[2560,320]{0,1:T(8,128)(2,1)S(1)}, bf16[2560,320]{0,1:T(8,128)(2,1)}, u32[]{:S(2)}) copy-start(bf16[2560,320]{0,1:T(8,128)(2,1)} %param.11) | copy-start | bytes 4915204
  26.8 27.4 %all-to-all-start.1 = ((bf16[64,32,128]{2,1,0:T(8,128)(2,1)}), bf16[64,32,128]{2,1,0:T(8,128)(2,1)S(1)}, u32[]{:S(2)}, u32[]{:S(2)}) async-start(bf16[64,32,128]{2,1,0:T(8,128)(2,1)} %reshape.323), calls=%async_computation.1 | async-start | bytes 1048576 | tf_op jit(solution)/shard_map/all_to_all | solution.py:114
  81.5 1.2 copy-start.3
  82.1 1.6 %copy-start.1 = (bf16[8,320,320]{1,0,2:T(8,128)(2,1)S(1)}, bf16[8,320,320]{1,0,2:T(8,128)(2,1)}, u32[]{:S(2)}) copy-start(bf16[8,320,320]{1,0,2:T(8,128)(2,1)} %reshape.325) | copy-start | bytes 4915204
  84.7 1.8 %copy-start.5 = (bf16[32,64,1,160]{3,1,2,0:T(8,128)(2,1)S(1)}, bf16[32,64,1,160]{3,1,2,0:T(8,128)(2,1)}, u32[]{:S(2)}) copy-start(bf16[32,64,1,160]{3,1,2,0:T(8,128)(2,1)} %param.14) | copy-start | bytes 1966084
  88.6 1.5 %copy-start = (bf16[320,8,320]{2,1,0:T(8,128)(2,1)S(1)}, bf16[320,8,320]{2,1,0:T(8,128)(2,1)}, u32[]{:S(2)}) copy-start(bf16[320,8,320]{2,1,0:T(8,128)(2,1)} %reshape.334) | copy-start | bytes 4915204
  118.6 20.9 %all-to-all-start.3 = ((bf16[64,16,128]{2,1,0:T(8,128)(2,1)}), bf16[64,16,128]{2,1,0:T(8,128)(2,1)S(1)}, u32[]{:S(2)}, u32[]{:S(2)}) async-start(bf16[64,16,128]{2,1,0:T(8,128)(2,1)} %bitcast.63), calls=%async_computation.3 | async-start | bytes 524288 | tf_op jit(solution)/shard_map/all_to_all | solution.py:165

commit v10 on v8

--- a/solution.py
+++ b/solution.py
@@ -152,6 +152,7 @@
         preferred_element_type=jnp.float32,
     )
     pieces = partial_sum.astype(jnp.bfloat16).reshape(shards, lanes, 128)
+    pieces, new_entries = lax.optimization_barrier((pieces, new_entries))
     pieces = lax.all_to_all(pieces, "tp", 0, 0, tiled=True)
     out_dealt = jnp.sum(pieces.astype(jnp.float32), axis=0)
     out_dealt = out_dealt.reshape(slot_count, verified, width).astype(jnp.bfloat16)

time: 135 us -> 134 us (level)
  blocking collectives: 48.5 us -> 72.5 us
  waiting for transfers between devices: 22.2 us -> 9.79 us
  starting transfers between devices: 30.1 us -> 18.7 us
    all_to_all x0 -> x1, blocking collectives: none -> 24.1 us  [body(): returned = lax.all_to_all(back_out, 'req', 0, 0, tiled=True)]
    all_to_all x1 -> x0, waiting for transfers between devices: 12.4 us -> none  [body(): returned = lax.all_to_all(back_out, 'req', 0, 0, tiled=True)]
    all_to_all x1 -> x0, starting transfers between devices: 11.4 us -> none  [body(): returned = lax.all_to_all(back_out, 'req', 0, 0, tiled=True)]
  transfers between devices with their start and end apart: 3 -> 2, of which waited for: 3 -> 2; matrix products, arithmetic and copies ran while one was open for 10% -> 9% of each run, Pallas kernels for 0% -> 0%
where the time goes in v10:
time: 134 us
  blocking collectives  72.5 us (54%)
  starting transfers between devices  18.7 us (14%)
  local copies, waits for them, and re-layouts  16.5 us (12%)
  waiting for transfers between devices  9.79 us (7%)
  other arithmetic  8.93 us (7%)
  matrix products  6.32 us (5%)
    all_gather x1, blocking collectives, body(): lax.all_gather(dealt_rows.reshape(lanes, 128), 'tp', axis=0, tiled=False)  27 us
    all_to_all x1, blocking collectives, body(): returned = lax.all_to_all(back_out, 'req', 0, 0, tiled=True)  24.1 us
    all_to_all x1, blocking collectives, body(): pieces = lax.all_to_all(pieces, 'tp', 0, 0, tiled=True)  21.4 us
    all_to_all x1, starting transfers between devices, body(): wanted = lax.all_to_all(wish, 'req', 0, 0, tiled=True)  11.6 us
    all_to_all x1, starting transfers between devices, body(): incoming = lax.all_to_all(outgoing, 'req', 0, 0, tiled=True)  7.04 us
    all_to_all x1, waiting for transfers between devices, body(): incoming = lax.all_to_all(outgoing, 'req', 0, 0, tiled=True)  6.53 us
    unnamed x40, local copies, waits for them, and re-layouts  5.06 us
    all_to_all x1, waiting for transfers between devices, body(): wanted = lax.all_to_all(wish, 'req', 0, 0, tiled=True)  3.27 us
  transfers between devices with their start and end apart: 2, of which 2 were waited for; matrix products, arithmetic and copies ran while one was open for 9% of the time, Pallas kernels for 0%

profile of v10, /device:TPU:1, one launch (start us, length us, event | category | flops | bytes accessed | tf_op | source)
XLA Modules:
  0.0 133.7 jit_solution(4455258281044848576)
XLA Ops:
  0.6 0.7 and_select_fusion.1
  1.4 0.6 copy-done.11
  2.0 0.7 copy.91
  2.7 11.6 %all-to-all-start = ((s32[64,1,1]{2,1,0:T(1,128)}), s32[64,1,1]{2,1,0:T(1,128)S(1)}, u32[]{:S(2)}, u32[]{:S(2)}) async-start(s32[64,1,1]{2,1,0:T(1,128)} %copy.91), calls=%async_computation | async-start | bytes 65536 | tf_op jit(solution)/shard_map/all_to_all | solution.py:91
  14.4 0.7 add_convert_fusion.1
  15.0 0.7 iota_compare_fusion.3
  15.8 1.2 iota_compare_fusion.7
  17.0 1.0 multiply_sine_fusion
  18.0 0.6 iota_compare_fusion.8
  18.6 0.8 reshape.334
  19.4 1.0 copy.92
  20.5 3.3 %all-to-all-done = s32[64,1,1]{2,1,0:T(1,128)S(1)} async-done(((s32[64,1,1]{2,1,0:T(1,128)}), s32[64,1,1]{2,1,0:T(1,128)S(1)}, u32[]{:S(2)}, u32[]{:S(2)}) %all-to-all-start) | async-done | bytes 288 | tf_op jit(solution)/shard_map/all_to_all | solution.py:91
  23.7 1.2 reduce.7
  25.3 0.8 copy.123
  26.0 7.0 %all-to-all-start.1 = ((bf16[64,16,128]{2,1,0:T(8,128)(2,1)}), bf16[64,16,128]{2,1,0:T(8,128)(2,1)S(1)}, u32[]{:S(2)}, u32[]{:S(2)}) async-start(bf16[64,16,128]{2,1,0:T(8,128)(2,1)} %bitcast.56), calls=%async_computation.1 | async-start | bytes 524288 | tf_op jit(solution)/shard_map/all_to_all | solution.py:111
  33.1 1.7 %reshape.323 = bf16[8,320,160]{1,0,2:T(8,128)(2,1)} reshape(bf16[2560,1,160]{0,2,1:T(8,128)(2,1)S(1)} %copy-done.5) | data formatting | bytes 1638400 | tf_op jit(solution)/shard_map/reshape.9
  34.8 2.4 %reshape.320 = bf16[8,320,320]{1,0,2:T(8,128)(2,1)} reshape(bf16[2560,320]{0,1:T(8,128)(2,1)S(1)} %copy-done.2) | data formatting | bytes 3276800 | tf_op jit(solution)/shard_map/reshape | solution.py:129
  37.2 2.5 %reshape.329 = bf16[320,8,320]{2,1,0:T(8,128)(2,1)} reshape(bf16[320,2560]{1,0:T(8,128)(2,1)S(1)} %copy-done.3) | data formatting | bytes 3276800 | tf_op jit(solution)/shard_map/reshape | solution.py:151
  39.7 6.5 %all-to-all-done.1 = bf16[64,16,128]{2,1,0:T(8,128)(2,1)S(1)} async-done(((bf16[64,16,128]{2,1,0:T(8,128)(2,1)}), bf16[64,16,128]{2,1,0:T(8,128)(2,1)S(1)}, u32[]{:S(2)}, u32[]{:S(2)}) %all-to-all-start.1) | async-done | bytes 262176 | tf_op jit(solution)/shard_map/all_to_all | solution.py:111
  46.7 27.0 %all_gather.3 = bf16[8,400,128]{2,1,0:T(8,128)(2,1)S(1)} all-gather(bf16[1,400,128]{2,1,0:T(8,128)(2,1)S(1)} %all_gather_reshape.3), channel_id=1, replica_groups=mesh['req'=64,'tp'=8] {'tp'}, dimensions={0}, use_global_device_ids=true | all-gather | bytes 921600 | tf_op jit(solution)/shard_map/all_gather | solution.py:119
  73.7 0.8 reshape.335
  75.5 0.6 copy-done.4
  77.2 1.0 fusion.14
  78.6 1.3 fusion.50
  81.2 0.9 convolution_bitcast_fusion
  82.7 0.9 copy-done
  83.6 0.7 fusion.8
  84.4 1.1 reshape.330
  85.5 0.8 maximum_select_fusion
  86.3 21.4 %all_to_all.24 = bf16[8,400,128]{2,1,0:T(8,128)(2,1)S(1)} all-to-all(bf16[8,400,128]{2,1,0:T(8,128)(2,1)S(1)} %reshape.330), channel_id=1, replica_groups=mesh['req'=64,'tp'=8] {'tp'}, dimensions={0} | all-to-all | bytes 1638400 | tf_op jit(solution)/shard_map/all_to_all | solution.py:156
  108.4 24.1 %all_to_all.25 = bf16[64,16,128]{2,1,0:T(8,128)(2,1)S(1)} all-to-all(bf16[64,16,128]{2,1,0:T(8,128)(2,1)S(1)} %bitcast.132), channel_id=1, replica_groups=mesh['req'=64,'tp'=8] {'req'}, dimensions={0} | all-to-all | bytes 524288 | tf_op jit(solution)/shard_map/all_to_all | solution.py:163
  133.0 0.7 copy.107
  (67 shorter events, 6.4 us)
Async XLA Ops:
  0.6 32.5 %copy-start.5 = (bf16[2560,1,160]{0,2,1:T(8,128)(2,1)S(1)}, bf16[2560,1,160]{0,2,1:T(8,128)(2,1)}, u32[]{:S(2)}) copy-start(bf16[2560,1,160]{0,2,1:T(8,128)(2,1)} %param.12) | copy-start | bytes 2457604
  1.4 0.6 copy-start.11
  2.7 21.0 %all-to-all-start = ((s32[64,1,1]{2,1,0:T(1,128)}), s32[64,1,1]{2,1,0:T(1,128)S(1)}, u32[]{:S(2)}, u32[]{:S(2)}) async-start(s32[64,1,1]{2,1,0:T(1,128)} %copy.91), calls=%async_computation | async-start | bytes 65536 | tf_op jit(solution)/shard_map/all_to_all | solution.py:91
  20.3 14.5 %copy-start.2 = (bf16[2560,320]{0,1:T(8,128)(2,1)S(1)}, bf16[2560,320]{0,1:T(8,128)(2,1)}, u32[]{:S(2)}) copy-start(bf16[2560,320]{0,1:T(8,128)(2,1)} %param.11) | copy-start | bytes 4915204
  25.0 8.1 %copy-start.9 = (s32[64]{0:T(128)}, s32[64]{0:T(128)S(1)}, u32[]{:S(2)}) copy-start(s32[64]{0:T(128)S(1)} %reduce.7) | copy-start | bytes 772
  26.0 20.2 %all-to-all-start.1 = ((bf16[64,16,128]{2,1,0:T(8,128)(2,1)}), bf16[64,16,128]{2,1,0:T(8,128)(2,1)S(1)}, u32[]{:S(2)}, u32[]{:S(2)}) async-start(bf16[64,16,128]{2,1,0:T(8,128)(2,1)} %bitcast.56), calls=%async_computation.1 | async-start | bytes 524288 | tf_op jit(solution)/shard_map/all_to_all | solution.py:111
  34.8 2.4 %copy-start.3 = (bf16[320,2560]{1,0:T(8,128)(2,1)S(1)}, bf16[320,2560]{1,0:T(8,128)(2,1)}, u32[]{:S(2)}) copy-start(bf16[320,2560]{1,0:T(8,128)(2,1)} %param.13) | copy-start | bytes 4915204
  37.2 9.1 %copy-start.12 = (s32[32]{0:T(128)S(1)}, s32[32]{0:T(128)}, u32[]{:S(2)}) copy-start(s32[32]{0:T(128)} %copy-done.11) | copy-start | bytes 388
  74.9 1.2 copy-start.4
  75.2 1.5 %copy-start.6 = (f32[32,5,40]{2,0,1:T(8,128)S(1)}, f32[32,5,40]{2,0,1:T(8,128)}, u32[]{:S(2)}) copy-start(f32[32,5,40]{2,0,1:T(8,128)} %get-tuple-element.15) | copy-start | bytes 76804
  75.2 1.5 %copy-start.7 = (f32[32,5,40]{2,0,1:T(8,128)S(1)}, f32[32,5,40]{2,0,1:T(8,128)}, u32[]{:S(2)}) copy-start(f32[32,5,40]{2,0,1:T(8,128)} %get-tuple-element.14) | copy-start | bytes 76804
  75.5 1.6 %copy-start.1 = (bf16[8,320,320]{1,0,2:T(8,128)(2,1)S(1)}, bf16[8,320,320]{1,0,2:T(8,128)(2,1)}, u32[]{:S(2)}) copy-start(bf16[8,320,320]{1,0,2:T(8,128)(2,1)} %reshape.320) | copy-start | bytes 4915204
  77.2 1.4 %copy-start.15 = (pred[5,5]{0,1:T(8,128)(4,1)S(1)}, pred[5,5]{0,1:T(8,128)(4,1)}, u32[]{:S(2)}) copy-start(pred[5,5]{0,1:T(8,128)(4,1)} %iota_compare_fusion.8) | copy-start | bytes 79
  78.2 1.8 %copy-start.8 = (bf16[32,64,1,160]{3,1,2,0:T(8,128)(2,1)S(1)}, bf16[32,64,1,160]{3,1,2,0:T(8,128)(2,1)}, u32[]{:S(2)}) copy-start(bf16[32,64,1,160]{3,1,2,0:T(8,128)(2,1)} %param.14) | copy-start | bytes 1966084
  82.1 1.5 %copy-start = (bf16[320,8,320]{2,1,0:T(8,128)(2,1)S(1)}, bf16[320,8,320]{2,1,0:T(8,128)(2,1)}, u32[]{:S(2)}) copy-start(bf16[320,8,320]{2,1,0:T(8,128)(2,1)} %reshape.329) | copy-start | bytes 4915204
  83.6 1.9 %copy-start.14 = (pred[32,5,1,1]{0,1,3,2:T(8,128)(4,1)S(1)}, pred[32,5,1,1]{0,1,3,2:T(8,128)(4,1)}, u32[]{:S(2)}) copy-start(pred[32,5,1,1]{0,1,3,2:T(8,128)(4,1)} %iota_compare_fusion.7) | copy-start | bytes 484
  84.4 23.6 %copy-start.13 = (s32[32]{0:T(128)S(1)}, s32[32]{0:T(128)}, u32[]{:S(2)}) copy-start(s32[32]{0:T(128)} %copy-done.11) | copy-start | bytes 388
  107.7 24.8 %copy-start.10 = (s32[64]{0:T(128)S(1)}, s32[64]{0:T(128)}, u32[]{:S(2)}) copy-start(s32[64]{0:T(128)} %copy-done.9) | copy-start | bytes 772

commit v11 on v10

--- a/solution.py
+++ b/solution.py
@@ -36,33 +36,26 @@
     scale = 1.0 / math.sqrt(HEAD_SIZE)
     slot_count = query_rows.shape[0]
     verified = query_rows.shape[1]
-    cache_keys = key_value_cache[..., :HEAD_SIZE]
-    cache_values = key_value_cache[..., HEAD_SIZE:]
-    fresh_keys = fresh[..., :HEAD_SIZE]
-    fresh_values = fresh[..., HEAD_SIZE:]
-    cache_scores = (
-        jnp.einsum("rtghd,rcgd->rghtc", query_rows, cache_keys, preferred_element_type=jnp.float32)
+    entries = jnp.concatenate([key_value_cache, fresh], axis=1)
+    keys = entries[..., :HEAD_SIZE]
+    values = entries[..., HEAD_SIZE:]
+    seen = jnp.concatenate(
+        [
+            jnp.broadcast_to(visible[:, None, :], (slot_count, verified, visible.shape[1])),
+            jnp.broadcast_to(causal[None, :, :], (slot_count, verified, verified)),
+        ],
+        axis=2,
+    )
+    scores = (
+        jnp.einsum("rtghd,rcgd->rghtc", query_rows, keys, preferred_element_type=jnp.float32)
         * scale
     )
-    cache_scores = jnp.where(visible[:, None, None, None, :], cache_scores, masked_score)
-    fresh_scores = (
-        jnp.einsum("rtghd,rugd->rghtu", query_rows, fresh_keys, preferred_element_type=jnp.float32)
-        * scale
-    )
-    fresh_scores = jnp.where(causal[None, None, None, :, :], fresh_scores, masked_score)
-    largest = jnp.maximum(jnp.max(cache_scores, axis=-1), jnp.max(fresh_scores, axis=-1))[..., None]
-    cache_expos = jnp.exp(cache_scores - largest)
-    fresh_expos = jnp.exp(fresh_scores - largest)
-    totals = jnp.sum(cache_expos, axis=-1, keepdims=True) + jnp.sum(
-        fresh_expos, axis=-1, keepdims=True
-    )
-    cache_weights = (cache_expos / totals).astype(jnp.bfloat16)
-    fresh_weights = (fresh_expos / totals).astype(jnp.bfloat16)
+    scores = jnp.where(seen[:, None, None, :, :], scores, masked_score)
+    largest = jnp.max(scores, axis=-1, keepdims=True)
+    expos = jnp.exp(scores - largest)
+    weights = (expos / jnp.sum(expos, axis=-1, keepdims=True)).astype(jnp.bfloat16)
     mixed = jnp.einsum(
-        "rghtc,rcgd->rtghd", cache_weights, cache_values, preferred_element_type=jnp.float32
-    )
-    mixed = mixed + jnp.einsum(
-        "rghtu,rugd->rtghd", fresh_weights, fresh_values, preferred_element_type=jnp.float32
+        "rghtc,rcgd->rtghd", weights, values, preferred_element_type=jnp.float32
     )
     return mixed.astype(jnp.bfloat16).reshape(slot_count, verified, -1)
 

time: 134 us -> 132 us (0.985)
  matrix products: 6.32 us -> 4.4 us
    reshape x0 -> x1, local copies, waits for them, and re-layouts: none -> 2.61 us
    dot_general x4 -> x2, matrix products: 3.06 us -> 1.12 us  [the longest x1 0.6 us: attend(): jnp.einsum('rghtc,rcgd->rtghd', weights, values, preferred_element_type=j...]
    another operation x2 -> x0, local copies, waits for them, and re-layouts: 1.78 us -> none
    unnamed x40 -> x38, local copies, waits for them, and re-layouts: 5.06 us -> 4.62 us
  transfers between devices with their start and end apart: 2 -> 2, of which waited for: 2 -> 2; matrix products, arithmetic and copies ran while one was open for 9% -> 11% of each run, Pallas kernels for 0% -> 0%
where the time goes in v11:
time: 132 us; the launch traced here: 131 us
  blocking collectives  72.9 us (55%)
  starting transfers between devices  18.7 us (14%)
  local copies, waits for them, and re-layouts  17 us (13%)
  other arithmetic  8.75 us (7%)
  waiting for transfers between devices  8.64 us (7%)
  matrix products  4.4 us (3%)
    all_gather x1, blocking collectives, body(): lax.all_gather(dealt_rows.reshape(lanes, 128), 'tp', axis=0, tiled=False)  27 us
    all_to_all x1, blocking collectives, body(): returned = lax.all_to_all(back_out, 'req', 0, 0, tiled=True)  24.5 us
    all_to_all x1, blocking collectives, body(): pieces = lax.all_to_all(pieces, 'tp', 0, 0, tiled=True)  21.4 us
    all_to_all x1, starting transfers between devices, body(): wanted = lax.all_to_all(wish, 'req', 0, 0, tiled=True)  11.6 us
    all_to_all x1, starting transfers between devices, body(): incoming = lax.all_to_all(outgoing, 'req', 0, 0, tiled=True)  7.07 us
    all_to_all x1, waiting for transfers between devices, body(): incoming = lax.all_to_all(outgoing, 'req', 0, 0, tiled=True)  5.4 us
    unnamed x38, local copies, waits for them, and re-layouts  4.62 us
    all_to_all x1, waiting for transfers between devices, body(): wanted = lax.all_to_all(wish, 'req', 0, 0, tiled=True)  3.23 us
  transfers between devices with their start and end apart: 2, of which 2 were waited for; matrix products, arithmetic and copies ran while one was open for 11% of the time, Pallas kernels for 0%

profile of v11, /device:TPU:1, one launch (start us, length us, event | category | flops | bytes accessed | tf_op | source)
XLA Modules:
  0.0 131.3 jit_solution(17687738939244888010)
XLA Ops:
  0.6 0.8 and_select_fusion.1
  1.4 0.5 copy-done.10
  2.0 0.7 copy.71
  2.7 11.6 %all-to-all-start = ((s32[64,1,1]{2,1,0:T(1,128)}), s32[64,1,1]{2,1,0:T(1,128)S(1)}, u32[]{:S(2)}, u32[]{:S(2)}) async-start(s32[64,1,1]{2,1,0:T(1,128)} %copy.71), calls=%async_computation | async-start | bytes 65536 | tf_op jit(solution)/shard_map/all_to_all | solution.py:84
  14.4 0.7 add_convert_fusion.1
  15.0 0.7 iota_compare_fusion.3
  15.8 1.2 iota_compare_fusion.7
  17.0 1.0 multiply_sine_fusion
  18.0 0.6 iota_compare_fusion.8
  18.6 0.8 reshape.289
  19.4 1.0 copy.72
  20.5 3.2 %all-to-all-done = s32[64,1,1]{2,1,0:T(1,128)S(1)} async-done(((s32[64,1,1]{2,1,0:T(1,128)}), s32[64,1,1]{2,1,0:T(1,128)S(1)}, u32[]{:S(2)}, u32[]{:S(2)}) %all-to-all-start) | async-done | bytes 288 | tf_op jit(solution)/shard_map/all_to_all | solution.py:84
  23.7 1.2 reduce.5
  25.3 0.8 copy.92
  26.0 7.1 %all-to-all-start.1 = ((bf16[64,16,128]{2,1,0:T(8,128)(2,1)}), bf16[64,16,128]{2,1,0:T(8,128)(2,1)S(1)}, u32[]{:S(2)}, u32[]{:S(2)}) async-start(bf16[64,16,128]{2,1,0:T(8,128)(2,1)} %bitcast.43), calls=%async_computation.1 | async-start | bytes 524288 | tf_op jit(solution)/shard_map/all_to_all | solution.py:104
  33.1 2.5 %reshape.281 = bf16[8,320,320]{1,0,2:T(8,128)(2,1)} reshape(bf16[2560,320]{0,1:T(8,128)(2,1)S(1)} %copy-done.2) | data formatting | bytes 3276800 | tf_op jit(solution)/shard_map/reshape | solution.py:122
  35.6 2.6 %reshape.278 = bf16[8,320,160]{1,0,2:T(8,128)(2,1)} reshape(bf16[2560,1,160]{0,2,1:T(8,128)(2,1)} %param.12) | data formatting | bytes 1638400 | tf_op jit(solution)/shard_map/reshape
  38.2 2.5 %reshape.284 = bf16[320,8,320]{2,1,0:T(8,128)(2,1)} reshape(bf16[320,2560]{1,0:T(8,128)(2,1)S(1)} %copy-done.3) | data formatting | bytes 3276800 | tf_op jit(solution)/shard_map/reshape | solution.py:144
  40.9 5.4 %all-to-all-done.1 = bf16[64,16,128]{2,1,0:T(8,128)(2,1)S(1)} async-done(((bf16[64,16,128]{2,1,0:T(8,128)(2,1)}), bf16[64,16,128]{2,1,0:T(8,128)(2,1)S(1)}, u32[]{:S(2)}, u32[]{:S(2)}) %all-to-all-start.1) | async-done | bytes 262176 | tf_op jit(solution)/shard_map/all_to_all | solution.py:104
  46.8 27.0 %all_gather.3 = bf16[8,400,128]{2,1,0:T(8,128)(2,1)S(1)} all-gather(bf16[1,400,128]{2,1,0:T(8,128)(2,1)S(1)} %all_gather_reshape.3), channel_id=1, replica_groups=mesh['req'=64,'tp'=8] {'tp'}, dimensions={0}, use_global_device_ids=true | all-gather | bytes 921600 | tf_op jit(solution)/shard_map/all_gather | solution.py:112
  73.8 0.8 reshape.290
  75.6 0.6 copy-done.5
  76.9 1.0 fusion.12
  78.2 0.8 broadcast_select_fusion
  79.2 0.5 fusion.47
  80.1 0.6 fusion.16
  81.0 0.7 copy-done
  81.7 0.7 fusion.8
  82.4 1.1 reshape.285
  83.6 21.4 %all_to_all.24 = bf16[8,400,128]{2,1,0:T(8,128)(2,1)S(1)} all-to-all(bf16[8,400,128]{2,1,0:T(8,128)(2,1)S(1)} %reshape.285), channel_id=1, replica_groups=mesh['req'=64,'tp'=8] {'tp'}, dimensions={0} | all-to-all | bytes 1638400 | tf_op jit(solution)/shard_map/all_to_all | solution.py:149
  105.7 24.5 %all_to_all.25 = bf16[64,16,128]{2,1,0:T(8,128)(2,1)S(1)} all-to-all(bf16[64,16,128]{2,1,0:T(8,128)(2,1)S(1)} %bitcast.110), channel_id=1, replica_groups=mesh['req'=64,'tp'=8] {'req'}, dimensions={0} | all-to-all | bytes 524288 | tf_op jit(solution)/shard_map/all_to_all | solution.py:156
  130.7 0.7 copy.83
  (62 shorter events, 5.1 us)
Async XLA Ops:
  0.6 32.5 %copy-start.2 = (bf16[2560,320]{0,1:T(8,128)(2,1)S(1)}, bf16[2560,320]{0,1:T(8,128)(2,1)}, u32[]{:S(2)}) copy-start(bf16[2560,320]{0,1:T(8,128)(2,1)} %param.11) | copy-start | bytes 4915204
  1.4 0.5 copy-start.10
  2.7 21.0 %all-to-all-start = ((s32[64,1,1]{2,1,0:T(1,128)}), s32[64,1,1]{2,1,0:T(1,128)S(1)}, u32[]{:S(2)}, u32[]{:S(2)}) async-start(s32[64,1,1]{2,1,0:T(1,128)} %copy.71), calls=%async_computation | async-start | bytes 65536 | tf_op jit(solution)/shard_map/all_to_all | solution.py:84
  25.0 1.1 copy-start.8
  26.0 20.2 %all-to-all-start.1 = ((bf16[64,16,128]{2,1,0:T(8,128)(2,1)}), bf16[64,16,128]{2,1,0:T(8,128)(2,1)S(1)}, u32[]{:S(2)}, u32[]{:S(2)}) async-start(bf16[64,16,128]{2,1,0:T(8,128)(2,1)} %bitcast.43), calls=%async_computation.1 | async-start | bytes 524288 | tf_op jit(solution)/shard_map/all_to_all | solution.py:104
  33.1 5.1 %copy-start.3 = (bf16[320,2560]{1,0:T(8,128)(2,1)S(1)}, bf16[320,2560]{1,0:T(8,128)(2,1)}, u32[]{:S(2)}) copy-start(bf16[320,2560]{1,0:T(8,128)(2,1)} %param.13) | copy-start | bytes 4915204
  38.2 2.5 %copy-start.14 = (pred[5,5]{1,0:T(8,128)(4,1)S(1)}, pred[5,5]{1,0:T(8,128)(4,1)}, u32[]{:S(2)}) copy-start(pred[5,5]{1,0:T(8,128)(4,1)} %iota_compare_fusion.8) | copy-start | bytes 79
  38.2 8.1 %copy-start.11 = (s32[32]{0:T(128)S(1)}, s32[32]{0:T(128)}, u32[]{:S(2)}) copy-start(s32[32]{0:T(128)} %copy-done.10) | copy-start | bytes 388
  74.9 1.2 copy-start.5
  75.2 1.6 %copy-start.1 = (bf16[8,320,320]{1,0,2:T(8,128)(2,1)S(1)}, bf16[8,320,320]{1,0,2:T(8,128)(2,1)}, u32[]{:S(2)}) copy-start(bf16[8,320,320]{1,0,2:T(8,128)(2,1)} %reshape.281) | copy-start | bytes 4915204
  76.8 1.0 copy-start.6
  76.8 1.0 copy-start.7
  76.9 1.3 %copy-start.13 = (pred[32,5,1,1]{0,1,3,2:T(8,128)(4,1)S(1)}, pred[32,5,1,1]{0,1,3,2:T(8,128)(4,1)}, u32[]{:S(2)}) copy-start(pred[32,5,1,1]{0,1,3,2:T(8,128)(4,1)} %iota_compare_fusion.7) | copy-start | bytes 484
  77.9 1.3 copy-start.4
  80.1 1.6 %copy-start = (bf16[320,8,320]{2,1,0:T(8,128)(2,1)S(1)}, bf16[320,8,320]{2,1,0:T(8,128)(2,1)}, u32[]{:S(2)}) copy-start(bf16[320,8,320]{2,1,0:T(8,128)(2,1)} %reshape.284) | copy-start | bytes 4915204
  82.4 22.8 %copy-start.12 = (s32[32]{0:T(128)S(1)}, s32[32]{0:T(128)}, u32[]{:S(2)}) copy-start(s32[32]{0:T(128)} %copy-done.10) | copy-start | bytes 388
  105.0 25.2 %copy-start.9 = (s32[64]{0:T(128)S(1)}, s32[64]{0:T(128)}, u32[]{:S(2)}) copy-start(s32[64]{0:T(128)} %copy-done.8) | copy-start | bytes 772

commit v12 on v11

--- a/solution.py
+++ b/solution.py
@@ -81,7 +81,7 @@
     local = deal_order % slot_count
     match = source[None, :] == jnp.arange(peers, dtype=jnp.int32)[:, None]
     wish = jnp.sum(jnp.where(match, local[None, :] + 1, 0), axis=1) - 1
-    wanted = lax.all_to_all(wish, "req", 0, 0, tiled=True)
+    wanted = lax.all_to_all(wish.reshape(peers, 1, 1), "req", 0, 0, tiled=True).reshape(peers)
     positions = cache_length[:, None] + jnp.arange(verified, dtype=jnp.int32)[None, :]
     cosine_part, sine_part = turning(positions)
     visible = jnp.arange(key_value_cache.shape[1], dtype=jnp.int32)[None, :] < cache_length[:, None]
@@ -109,8 +109,7 @@
     ).astype(jnp.bfloat16)
     rows = slot_count * verified
     lanes = rows * width // 128
-    features = lax.all_gather(dealt_rows.reshape(lanes, 128), "tp", axis=0, tiled=False)
-    features = features.reshape(shards, rows, width)
+    features = lax.all_gather(dealt_rows.reshape(rows, width), "tp", axis=0, tiled=False)
     widened = features.astype(jnp.float32)
     variance = jnp.mean(widened * widened, axis=(0, 2), keepdims=True)
     normed = (widened * lax.rsqrt(variance + 1e-05) * gain).astype(jnp.bfloat16)

time: 132 us -> 129 us (0.977)
  local copies, waits for them, and re-layouts: 17 us -> 14.4 us
  starting transfers between devices: 18.7 us -> 16.9 us
  waiting for transfers between devices: 8.64 us -> 10.4 us
    all_to_all x1, starting transfers between devices: 7.07 us -> 5.33 us  [body(): incoming = lax.all_to_all(outgoing, 'req', 0, 0, tiled=True)]
    all_to_all x1, waiting for transfers between devices: 3.23 us -> 4.98 us  [body(): lax.all_to_all(wish.reshape(peers, 1, 1), 'req', 0, 0, tiled=True)]
    unnamed x38 -> x14, local copies, waits for them, and re-layouts: 4.62 us -> 3.22 us
  transfers between devices with their start and end apart: 2 -> 2, of which waited for: 2 -> 2; matrix products, arithmetic and copies ran while one was open for 11% -> 9% of each run, Pallas kernels for 0% -> 0%
where the time goes in v12:
time: 129 us
  blocking collectives  73.7 us (57%)
  starting transfers between devices  16.9 us (13%)
  local copies, waits for them, and re-layouts  14.4 us (11%)
  waiting for transfers between devices  10.4 us (8%)
  other arithmetic  7.82 us (6%)
  matrix products  4.4 us (3%)
    all_gather x1, blocking collectives, body(): lax.all_gather(dealt_rows.reshape(rows, width), 'tp', axis=0, tiled=False)  27.5 us
    all_to_all x1, blocking collectives, body(): returned = lax.all_to_all(back_out, 'req', 0, 0, tiled=True)  25.8 us
    all_to_all x1, blocking collectives, body(): pieces = lax.all_to_all(pieces, 'tp', 0, 0, tiled=True)  20.4 us
    all_to_all x1, starting transfers between devices, body(): lax.all_to_all(wish.reshape(peers, 1, 1), 'req', 0, 0, tiled=True)  11.6 us
    all_to_all x1, waiting for transfers between devices, body(): incoming = lax.all_to_all(outgoing, 'req', 0, 0, tiled=True)  5.39 us
    all_to_all x1, starting transfers between devices, body(): incoming = lax.all_to_all(outgoing, 'req', 0, 0, tiled=True)  5.33 us
    all_to_all x1, waiting for transfers between devices, body(): lax.all_to_all(wish.reshape(peers, 1, 1), 'req', 0, 0, tiled=True)  4.98 us
    reshape x1, local copies, waits for them, and re-layouts, body(): output_weight.reshape(-1, shards, width)  3.24 us
  transfers between devices with their start and end apart: 2, of which 2 were waited for; matrix products, arithmetic and copies ran while one was open for 9% of the time, Pallas kernels for 0%

profile of v12, /device:TPU:1, one launch (start us, length us, event | category | flops | bytes accessed | tf_op | source)
XLA Modules:
  0.0 128.6 jit_solution(7418305848842408657)
XLA Ops:
  0.6 0.8 and_select_fusion.1
  1.5 0.7 copy.59
  2.2 11.6 %all-to-all-start = ((s32[64,1,1]{2,1,0:T(1,128)}), s32[64,1,1]{2,1,0:T(1,128)S(1)}, u32[]{:S(2)}, u32[]{:S(2)}) async-start(s32[64,1,1]{2,1,0:T(1,128)} %copy.59), calls=%async_computation | async-start | bytes 65536 | tf_op jit(solution)/shard_map/all_to_all | solution.py:84
  13.9 0.7 add_convert_fusion.1
  14.5 0.7 iota_compare_fusion.3
  15.3 0.7 iota_compare_fusion.7
  15.9 0.4 multiply_sine_fusion
  16.3 0.8 reshape.288
  17.1 1.0 copy.60
  18.2 5.0 %all-to-all-done = s32[64,1,1]{2,1,0:T(1,128)S(1)} async-done(((s32[64,1,1]{2,1,0:T(1,128)}), s32[64,1,1]{2,1,0:T(1,128)S(1)}, u32[]{:S(2)}, u32[]{:S(2)}) %all-to-all-start) | async-done | bytes 288 | tf_op jit(solution)/shard_map/all_to_all | solution.py:84
  23.2 1.2 reduce.3
  24.7 0.7 copy.80
  25.4 5.3 %all-to-all-start.1 = ((bf16[64,16,128]{2,1,0:T(8,128)(2,1)}), bf16[64,16,128]{2,1,0:T(8,128)(2,1)S(1)}, u32[]{:S(2)}, u32[]{:S(2)}) async-start(bf16[64,16,128]{2,1,0:T(8,128)(2,1)} %bitcast.44), calls=%async_computation.1 | async-start | bytes 524288 | tf_op jit(solution)/shard_map/all_to_all | solution.py:104
  30.8 2.5 %reshape.280 = bf16[8,320,320]{1,0,2:T(8,128)(2,1)} reshape(bf16[2560,320]{0,1:T(8,128)(2,1)S(1)} %copy-done.1) | data formatting | bytes 3276800 | tf_op jit(solution)/shard_map/reshape | solution.py:121
  33.3 1.9 %reshape.277 = bf16[8,320,160]{1,0,2:T(8,128)(2,1)S(1)} reshape(bf16[2560,1,160]{0,2,1:T(8,128)(2,1)} %param.12) | data formatting | bytes 1638400 | tf_op jit(solution)/shard_map/reshape
  35.2 3.2 %reshape.283 = bf16[320,8,320]{2,1,0:T(8,128)(2,1)S(1)} reshape(bf16[320,2560]{1,0:T(8,128)(2,1)} %param.13) | data formatting | bytes 3276800 | tf_op jit(solution)/shard_map/reshape | solution.py:143
  38.6 5.4 %all-to-all-done.1 = bf16[64,16,128]{2,1,0:T(8,128)(2,1)S(1)} async-done(((bf16[64,16,128]{2,1,0:T(8,128)(2,1)}), bf16[64,16,128]{2,1,0:T(8,128)(2,1)S(1)}, u32[]{:S(2)}, u32[]{:S(2)}) %all-to-all-start.1) | async-done | bytes 262176 | tf_op jit(solution)/shard_map/all_to_all | solution.py:104
  44.4 27.5 %all_gather.3 = bf16[8,160,320]{2,1,0:T(8,128)(2,1)S(1)} all-gather(bf16[1,160,320]{2,1,0:T(8,128)(2,1)S(1)} %all_gather_reshape.3), channel_id=1, replica_groups=mesh['req'=64,'tp'=8] {'tp'}, dimensions={0}, use_global_device_ids=true | all-gather | bytes 921600 | tf_op jit(solution)/shard_map/all_gather | solution.py:112
  72.0 1.0 fusion
  73.0 0.4 fusion.2
  73.4 0.4 convolution_bitcast_fusion
  73.9 0.6 copy-done
  74.6 1.0 fusion.15
  75.9 0.8 broadcast_select_fusion
  76.8 0.5 fusion.49
  77.4 0.4 fusion.30
  77.8 0.6 fusion.19
  78.7 0.7 fusion.11
  79.4 1.1 reshape.284
  80.5 20.4 %all_to_all.20 = bf16[8,400,128]{2,1,0:T(8,128)(2,1)S(1)} all-to-all(bf16[8,400,128]{2,1,0:T(8,128)(2,1)S(1)} %reshape.284), channel_id=1, replica_groups=mesh['req'=64,'tp'=8] {'tp'}, dimensions={0} | all-to-all | bytes 1638400 | tf_op jit(solution)/shard_map/all_to_all | solution.py:148
  101.6 25.8 %all_to_all.21 = bf16[64,16,128]{2,1,0:T(8,128)(2,1)S(1)} all-to-all(bf16[64,16,128]{2,1,0:T(8,128)(2,1)S(1)} %bitcast.110), channel_id=1, replica_groups=mesh['req'=64,'tp'=8] {'req'}, dimensions={0} | all-to-all | bytes 524288 | tf_op jit(solution)/shard_map/all_to_all | solution.py:155
  127.9 0.7 copy.71
  (34 shorter events, 3.1 us)
Async XLA Ops:
  0.6 30.2 %copy-start.1 = (bf16[2560,320]{0,1:T(8,128)(2,1)S(1)}, bf16[2560,320]{0,1:T(8,128)(2,1)}, u32[]{:S(2)}) copy-start(bf16[2560,320]{0,1:T(8,128)(2,1)} %param.11) | copy-start | bytes 4915204
  2.2 20.9 %all-to-all-start = ((s32[64,1,1]{2,1,0:T(1,128)}), s32[64,1,1]{2,1,0:T(1,128)S(1)}, u32[]{:S(2)}, u32[]{:S(2)}) async-start(s32[64,1,1]{2,1,0:T(1,128)} %copy.59), calls=%async_computation | async-start | bytes 65536 | tf_op jit(solution)/shard_map/all_to_all | solution.py:84
  25.4 18.5 %all-to-all-start.1 = ((bf16[64,16,128]{2,1,0:T(8,128)(2,1)}), bf16[64,16,128]{2,1,0:T(8,128)(2,1)S(1)}, u32[]{:S(2)}, u32[]{:S(2)}) async-start(bf16[64,16,128]{2,1,0:T(8,128)(2,1)} %bitcast.44), calls=%async_computation.1 | async-start | bytes 524288 | tf_op jit(solution)/shard_map/all_to_all | solution.py:104
  73.0 1.6 %copy-start = (bf16[8,320,320]{1,0,2:T(8,128)(2,1)S(1)}, bf16[8,320,320]{1,0,2:T(8,128)(2,1)}, u32[]{:S(2)}) copy-start(bf16[8,320,320]{1,0,2:T(8,128)(2,1)} %reshape.280) | copy-start | bytes 4915204
  75.6 1.3 copy-start.2

commit v13 on v12

--- a/solution.py
+++ b/solution.py
@@ -153,10 +153,11 @@
     ).astype(jnp.bfloat16)
     back_out = jnp.pad(back_out, ((0, 0), (0, padded - row_size))).reshape(peers, padded // 128, 128)
     returned = lax.all_to_all(back_out, "req", 0, 0, tiled=True)
-    returned = returned.reshape(peers, padded)[:, :row_size]
+    returned = returned.reshape(peers, padded)[:, :row_size].reshape(peers, verified, width)
     block_output = jnp.einsum(
-        "dj,dx->jx", pick, returned, preferred_element_type=jnp.float32
-    ).astype(jnp.bfloat16).reshape(slot_count, verified, width)
+        "dj,dtf->tjf", pick, returned, preferred_element_type=jnp.float32
+    ).astype(jnp.bfloat16)
+    block_output = jnp.transpose(block_output, (1, 0, 2))
     return (block_output, new_entries)
 
 

time: 129 us -> 129 us (level)
    unnamed x14 -> x13, local copies, waits for them, and re-layouts: 3.22 us -> 2.55 us
where the time goes in v13:
time: 129 us
  blocking collectives  73.7 us (57%)
  starting transfers between devices  16.9 us (13%)
  local copies, waits for them, and re-layouts  13.9 us (11%)
  waiting for transfers between devices  10.4 us (8%)
  other arithmetic  7.82 us (6%)
  matrix products  4.95 us (4%)
    all_gather x1, blocking collectives, body(): lax.all_gather(dealt_rows.reshape(rows, width), 'tp', axis=0, tiled=False)  27.5 us
    all_to_all x1, blocking collectives, body(): returned = lax.all_to_all(back_out, 'req', 0, 0, tiled=True)  25.7 us
    all_to_all x1, blocking collectives, body(): pieces = lax.all_to_all(pieces, 'tp', 0, 0, tiled=True)  20.4 us
    all_to_all x1, starting transfers between devices, body(): lax.all_to_all(wish.reshape(peers, 1, 1), 'req', 0, 0, tiled=True)  11.6 us
    all_to_all x1, waiting for transfers between devices, body(): incoming = lax.all_to_all(outgoing, 'req', 0, 0, tiled=True)  5.39 us
    all_to_all x1, starting transfers between devices, body(): incoming = lax.all_to_all(outgoing, 'req', 0, 0, tiled=True)  5.33 us
    all_to_all x1, waiting for transfers between devices, body(): lax.all_to_all(wish.reshape(peers, 1, 1), 'req', 0, 0, tiled=True)  4.98 us
    reshape x1, local copies, waits for them, and re-layouts, body(): output_weight.reshape(-1, shards, width)  3.24 us
  transfers between devices with their start and end apart: 2, of which 2 were waited for; matrix products, arithmetic and copies ran while one was open for 9% of the time, Pallas kernels for 0%

profile of v13, /device:TPU:1, one launch (start us, length us, event | category | flops | bytes accessed | tf_op | source)
XLA Modules:
  0.0 128.6 jit_solution(15058766158010626362)
XLA Ops:
  0.6 0.8 and_select_fusion.1
  1.5 0.7 copy.58
  2.2 11.6 %all-to-all-start = ((s32[64,1,1]{2,1,0:T(1,128)}), s32[64,1,1]{2,1,0:T(1,128)S(1)}, u32[]{:S(2)}, u32[]{:S(2)}) async-start(s32[64,1,1]{2,1,0:T(1,128)} %copy.58), calls=%async_computation | async-start | bytes 65536 | tf_op jit(solution)/shard_map/all_to_all | solution.py:84
  13.9 0.7 add_convert_fusion.1
  14.5 0.7 iota_compare_fusion.2
  15.3 0.7 iota_compare_fusion.6
  15.9 0.4 multiply_sine_fusion
  16.3 0.8 reshape.288
  17.1 1.0 copy.59
  18.2 5.0 %all-to-all-done = s32[64,1,1]{2,1,0:T(1,128)S(1)} async-done(((s32[64,1,1]{2,1,0:T(1,128)}), s32[64,1,1]{2,1,0:T(1,128)S(1)}, u32[]{:S(2)}, u32[]{:S(2)}) %all-to-all-start) | async-done | bytes 288 | tf_op jit(solution)/shard_map/all_to_all | solution.py:84
  23.2 1.2 reduce.3
  24.7 0.7 copy.79
  25.5 5.3 %all-to-all-start.1 = ((bf16[64,16,128]{2,1,0:T(8,128)(2,1)}), bf16[64,16,128]{2,1,0:T(8,128)(2,1)S(1)}, u32[]{:S(2)}, u32[]{:S(2)}) async-start(bf16[64,16,128]{2,1,0:T(8,128)(2,1)} %bitcast.45), calls=%async_computation.1 | async-start | bytes 524288 | tf_op jit(solution)/shard_map/all_to_all | solution.py:104
  30.8 2.5 %reshape.280 = bf16[8,320,320]{1,0,2:T(8,128)(2,1)} reshape(bf16[2560,320]{0,1:T(8,128)(2,1)S(1)} %copy-done.1) | data formatting | bytes 3276800 | tf_op jit(solution)/shard_map/reshape | solution.py:121
  33.3 1.9 %reshape.277 = bf16[8,320,160]{1,0,2:T(8,128)(2,1)S(1)} reshape(bf16[2560,1,160]{0,2,1:T(8,128)(2,1)} %param.12) | data formatting | bytes 1638400 | tf_op jit(solution)/shard_map/reshape
  35.2 3.2 %reshape.283 = bf16[320,8,320]{2,1,0:T(8,128)(2,1)S(1)} reshape(bf16[320,2560]{1,0:T(8,128)(2,1)} %param.13) | data formatting | bytes 3276800 | tf_op jit(solution)/shard_map/reshape | solution.py:143
  38.6 5.4 %all-to-all-done.1 = bf16[64,16,128]{2,1,0:T(8,128)(2,1)S(1)} async-done(((bf16[64,16,128]{2,1,0:T(8,128)(2,1)}), bf16[64,16,128]{2,1,0:T(8,128)(2,1)S(1)}, u32[]{:S(2)}, u32[]{:S(2)}) %all-to-all-start.1) | async-done | bytes 262176 | tf_op jit(solution)/shard_map/all_to_all | solution.py:104
  44.4 27.5 %all_gather.3 = bf16[8,160,320]{2,1,0:T(8,128)(2,1)S(1)} all-gather(bf16[1,160,320]{2,1,0:T(8,128)(2,1)S(1)} %all_gather_reshape.3), channel_id=1, replica_groups=mesh['req'=64,'tp'=8] {'tp'}, dimensions={0}, use_global_device_ids=true | all-gather | bytes 921600 | tf_op jit(solution)/shard_map/all_gather | solution.py:112
  72.0 1.0 fusion
  73.0 0.4 fusion.2
  73.4 0.4 convolution_bitcast_fusion
  73.9 0.6 copy-done
  74.6 1.0 fusion.15
  75.9 0.8 broadcast_select_fusion
  76.8 0.5 fusion.51
  77.4 0.4 fusion.30
  77.8 0.6 fusion.19
  78.7 0.7 fusion.11
  79.4 1.1 reshape.284
  80.5 20.4 %all_to_all.20 = bf16[8,400,128]{2,1,0:T(8,128)(2,1)S(1)} all-to-all(bf16[8,400,128]{2,1,0:T(8,128)(2,1)S(1)} %reshape.284), channel_id=1, replica_groups=mesh['req'=64,'tp'=8] {'tp'}, dimensions={0} | all-to-all | bytes 1638400 | tf_op jit(solution)/shard_map/all_to_all | solution.py:148
  101.6 25.7 %all_to_all.21 = bf16[64,16,128]{2,1,0:T(8,128)(2,1)S(1)} all-to-all(bf16[64,16,128]{2,1,0:T(8,128)(2,1)S(1)} %bitcast.113), channel_id=1, replica_groups=mesh['req'=64,'tp'=8] {'req'}, dimensions={0} | all-to-all | bytes 524288 | tf_op jit(solution)/shard_map/all_to_all | solution.py:155
  127.7 0.8 convolution_convert_fusion.4
  (34 shorter events, 2.9 us)
Async XLA Ops:
  0.6 30.2 %copy-start.1 = (bf16[2560,320]{0,1:T(8,128)(2,1)S(1)}, bf16[2560,320]{0,1:T(8,128)(2,1)}, u32[]{:S(2)}) copy-start(bf16[2560,320]{0,1:T(8,128)(2,1)} %param.11) | copy-start | bytes 4915204
  2.2 20.9 %all-to-all-start = ((s32[64,1,1]{2,1,0:T(1,128)}), s32[64,1,1]{2,1,0:T(1,128)S(1)}, u32[]{:S(2)}, u32[]{:S(2)}) async-start(s32[64,1,1]{2,1,0:T(1,128)} %copy.58), calls=%async_computation | async-start | bytes 65536 | tf_op jit(solution)/shard_map/all_to_all | solution.py:84
  25.5 18.5 %all-to-all-start.1 = ((bf16[64,16,128]{2,1,0:T(8,128)(2,1)}), bf16[64,16,128]{2,1,0:T(8,128)(2,1)S(1)}, u32[]{:S(2)}, u32[]{:S(2)}) async-start(bf16[64,16,128]{2,1,0:T(8,128)(2,1)} %bitcast.45), calls=%async_computation.1 | async-start | bytes 524288 | tf_op jit(solution)/shard_map/all_to_all | solution.py:104
  73.0 1.6 %copy-start = (bf16[8,320,320]{1,0,2:T(8,128)(2,1)S(1)}, bf16[8,320,320]{1,0,2:T(8,128)(2,1)}, u32[]{:S(2)}) copy-start(bf16[8,320,320]{1,0,2:T(8,128)(2,1)} %reshape.280) | copy-start | bytes 4915204
  75.6 1.3 copy-start.2

commit v14 on v12

--- a/solution.py
+++ b/solution.py
@@ -77,8 +77,12 @@
     slot_count = deal_order.shape[0]
     verified = hidden.shape[1]
     width = hidden.shape[2]
-    source = deal_order // slot_count
-    local = deal_order % slot_count
+    if slot_count & (slot_count - 1) == 0:
+        source = lax.shift_right_logical(deal_order, slot_count.bit_length() - 1)
+        local = lax.bitwise_and(deal_order, slot_count - 1)
+    else:
+        source = deal_order // slot_count
+        local = deal_order % slot_count
     match = source[None, :] == jnp.arange(peers, dtype=jnp.int32)[:, None]
     wish = jnp.sum(jnp.where(match, local[None, :] + 1, 0), axis=1) - 1
     wanted = lax.all_to_all(wish.reshape(peers, 1, 1), "req", 0, 0, tiled=True).reshape(peers)

time: 129 us -> 129 us (level)
  no operation moved by 1% of the time
where the time goes in v14:
time: 129 us
  blocking collectives  73.7 us (57%)
  starting transfers between devices  16.9 us (13%)
  local copies, waits for them, and re-layouts  14.4 us (11%)
  waiting for transfers between devices  10.4 us (8%)
  other arithmetic  7.81 us (6%)
  matrix products  4.39 us (3%)
    all_gather x1, blocking collectives, body(): lax.all_gather(dealt_rows.reshape(rows, width), 'tp', axis=0, tiled=False)  27.5 us
    all_to_all x1, blocking collectives, body(): returned = lax.all_to_all(back_out, 'req', 0, 0, tiled=True)  25.8 us
    all_to_all x1, blocking collectives, body(): pieces = lax.all_to_all(pieces, 'tp', 0, 0, tiled=True)  20.4 us
    all_to_all x1, starting transfers between devices, body(): lax.all_to_all(wish.reshape(peers, 1, 1), 'req', 0, 0, tiled=True)  11.6 us
    all_to_all x1, waiting for transfers between devices, body(): incoming = lax.all_to_all(outgoing, 'req', 0, 0, tiled=True)  5.39 us
    all_to_all x1, starting transfers between devices, body(): incoming = lax.all_to_all(outgoing, 'req', 0, 0, tiled=True)  5.33 us
    all_to_all x1, waiting for transfers between devices, body(): lax.all_to_all(wish.reshape(peers, 1, 1), 'req', 0, 0, tiled=True)  4.98 us
    reshape x1, local copies, waits for them, and re-layouts, body(): output_weight.reshape(-1, shards, width)  3.24 us
  transfers between devices with their start and end apart: 2, of which 2 were waited for; matrix products, arithmetic and copies ran while one was open for 9% of the time, Pallas kernels for 0%

profile of v14, /device:TPU:1, one launch (start us, length us, event | category | flops | bytes accessed | tf_op | source)
XLA Modules:
  0.0 128.6 jit_solution(17430675043931277346)
XLA Ops:
  0.6 0.8 broadcast_shift-right-logical_fusion
  1.5 0.7 copy.59
  2.2 11.6 %all-to-all-start = ((s32[64,1,1]{2,1,0:T(1,128)}), s32[64,1,1]{2,1,0:T(1,128)S(1)}, u32[]{:S(2)}, u32[]{:S(2)}) async-start(s32[64,1,1]{2,1,0:T(1,128)} %copy.59), calls=%async_computation | async-start | bytes 65536 | tf_op jit(solution)/shard_map/all_to_all | solution.py:88
  13.9 0.7 add_convert_fusion.1
  14.5 0.7 iota_compare_fusion.3
  15.3 0.7 iota_compare_fusion.7
  15.9 0.4 multiply_sine_fusion
  16.3 0.8 reshape.288
  17.1 1.0 copy.60
  18.2 5.0 %all-to-all-done = s32[64,1,1]{2,1,0:T(1,128)S(1)} async-done(((s32[64,1,1]{2,1,0:T(1,128)}), s32[64,1,1]{2,1,0:T(1,128)S(1)}, u32[]{:S(2)}, u32[]{:S(2)}) %all-to-all-start) | async-done | bytes 288 | tf_op jit(solution)/shard_map/all_to_all | solution.py:88
  23.2 1.2 reduce.3
  24.7 0.7 copy.80
  25.4 5.3 %all-to-all-start.1 = ((bf16[64,16,128]{2,1,0:T(8,128)(2,1)}), bf16[64,16,128]{2,1,0:T(8,128)(2,1)S(1)}, u32[]{:S(2)}, u32[]{:S(2)}) async-start(bf16[64,16,128]{2,1,0:T(8,128)(2,1)} %bitcast.44), calls=%async_computation.1 | async-start | bytes 524288 | tf_op jit(solution)/shard_map/all_to_all | solution.py:108
  30.8 2.5 %reshape.280 = bf16[8,320,320]{1,0,2:T(8,128)(2,1)} reshape(bf16[2560,320]{0,1:T(8,128)(2,1)S(1)} %copy-done.1) | data formatting | bytes 3276800 | tf_op jit(solution)/shard_map/reshape | solution.py:125
  33.3 1.9 %reshape.277 = bf16[8,320,160]{1,0,2:T(8,128)(2,1)S(1)} reshape(bf16[2560,1,160]{0,2,1:T(8,128)(2,1)} %param.12) | data formatting | bytes 1638400 | tf_op jit(solution)/shard_map/reshape
  35.1 3.2 %reshape.283 = bf16[320,8,320]{2,1,0:T(8,128)(2,1)S(1)} reshape(bf16[320,2560]{1,0:T(8,128)(2,1)} %param.13) | data formatting | bytes 3276800 | tf_op jit(solution)/shard_map/reshape | solution.py:147
  38.5 5.4 %all-to-all-done.1 = bf16[64,16,128]{2,1,0:T(8,128)(2,1)S(1)} async-done(((bf16[64,16,128]{2,1,0:T(8,128)(2,1)}), bf16[64,16,128]{2,1,0:T(8,128)(2,1)S(1)}, u32[]{:S(2)}, u32[]{:S(2)}) %all-to-all-start.1) | async-done | bytes 262176 | tf_op jit(solution)/shard_map/all_to_all | solution.py:108
  44.4 27.5 %all_gather.3 = bf16[8,160,320]{2,1,0:T(8,128)(2,1)S(1)} all-gather(bf16[1,160,320]{2,1,0:T(8,128)(2,1)S(1)} %all_gather_reshape.3), channel_id=1, replica_groups=mesh['req'=64,'tp'=8] {'tp'}, dimensions={0}, use_global_device_ids=true | all-gather | bytes 921600 | tf_op jit(solution)/shard_map/all_gather | solution.py:116
  71.9 1.0 fusion
  73.0 0.4 fusion.2
  73.4 0.4 convolution_bitcast_fusion
  73.9 0.6 copy-done
  74.5 1.0 fusion.15
  75.9 0.8 broadcast_select_fusion
  76.8 0.5 fusion.48
  77.4 0.4 fusion.30
  77.8 0.6 fusion.19
  78.6 0.7 fusion.11
  79.4 1.1 reshape.284
  80.5 20.4 %all_to_all.20 = bf16[8,400,128]{2,1,0:T(8,128)(2,1)S(1)} all-to-all(bf16[8,400,128]{2,1,0:T(8,128)(2,1)S(1)} %reshape.284), channel_id=1, replica_groups=mesh['req'=64,'tp'=8] {'tp'}, dimensions={0} | all-to-all | bytes 1638400 | tf_op jit(solution)/shard_map/all_to_all | solution.py:152
  101.6 25.8 %all_to_all.21 = bf16[64,16,128]{2,1,0:T(8,128)(2,1)S(1)} all-to-all(bf16[64,16,128]{2,1,0:T(8,128)(2,1)S(1)} %bitcast.110), channel_id=1, replica_groups=mesh['req'=64,'tp'=8] {'req'}, dimensions={0} | all-to-all | bytes 524288 | tf_op jit(solution)/shard_map/all_to_all | solution.py:159
  127.9 0.7 copy.71
  (34 shorter events, 3.1 us)
Async XLA Ops:
  0.6 30.1 %copy-start.1 = (bf16[2560,320]{0,1:T(8,128)(2,1)S(1)}, bf16[2560,320]{0,1:T(8,128)(2,1)}, u32[]{:S(2)}) copy-start(bf16[2560,320]{0,1:T(8,128)(2,1)} %param.11) | copy-start | bytes 4915204
  2.2 20.9 %all-to-all-start = ((s32[64,1,1]{2,1,0:T(1,128)}), s32[64,1,1]{2,1,0:T(1,128)S(1)}, u32[]{:S(2)}, u32[]{:S(2)}) async-start(s32[64,1,1]{2,1,0:T(1,128)} %copy.59), calls=%async_computation | async-start | bytes 65536 | tf_op jit(solution)/shard_map/all_to_all | solution.py:88
  25.4 18.5 %all-to-all-start.1 = ((bf16[64,16,128]{2,1,0:T(8,128)(2,1)}), bf16[64,16,128]{2,1,0:T(8,128)(2,1)S(1)}, u32[]{:S(2)}, u32[]{:S(2)}) async-start(bf16[64,16,128]{2,1,0:T(8,128)(2,1)} %bitcast.44), calls=%async_computation.1 | async-start | bytes 524288 | tf_op jit(solution)/shard_map/all_to_all | solution.py:108
  73.0 1.6 %copy-start = (bf16[8,320,320]{1,0,2:T(8,128)(2,1)S(1)}, bf16[8,320,320]{1,0,2:T(8,128)(2,1)}, u32[]{:S(2)}) copy-start(bf16[8,320,320]{1,0,2:T(8,128)(2,1)} %reshape.280) | copy-start | bytes 4915204
  75.6 1.3 copy-start.2

commit v15 on v12

--- a/solution.py
+++ b/solution.py
@@ -115,22 +115,16 @@
     normed = (widened * lax.rsqrt(variance + 1e-05) * gain).astype(jnp.bfloat16)
     heads_here = query_weight.shape[1] // HEAD_SIZE
     groups_here = key_value_matrix.shape[1]
-    query_rows = jnp.einsum(
-        "knf,kfe->ne",
-        normed,
-        query_weight.reshape(shards, width, -1),
-        preferred_element_type=jnp.float32,
+    both_weights = jnp.concatenate(
+        [query_weight.reshape(shards, width, -1), key_value_matrix.reshape(shards, width, -1)], axis=2
     )
+    both_rows = jnp.einsum("knf,kfe->ne", normed, both_weights, preferred_element_type=jnp.float32)
+    query_rows = both_rows[:, : query_weight.shape[1]]
     query_rows = query_rows.reshape(
         slot_count, verified, groups_here, heads_here // groups_here, HEAD_SIZE
     )
     query_rows = rotate(query_rows, cosine_part[:, :, None, None], sine_part[:, :, None, None]).astype(jnp.bfloat16)
-    projected = jnp.einsum(
-        "knf,kfge->nge",
-        normed,
-        key_value_matrix.reshape(shards, width, groups_here, -1),
-        preferred_element_type=jnp.float32,
-    ).reshape(slot_count, verified, groups_here, -1)
+    projected = both_rows[:, query_weight.shape[1] :].reshape(slot_count, verified, groups_here, -1)
     fresh = jnp.concatenate(
         [rotate(projected[..., :HEAD_SIZE], cosine_part[:, :, None], sine_part[:, :, None]), projected[..., HEAD_SIZE:]],
         axis=-1,

time: 129 us -> 135 us (1.047)
  blocking collectives: 73.7 us -> 48.3 us
  starting transfers between devices: 16.9 us -> 32.2 us
  waiting for transfers between devices: 10.4 us -> 20.4 us
  local copies, waits for them, and re-layouts: 14.4 us -> 19.8 us
    all_to_all x1 -> x0, blocking collectives: 25.8 us -> none  [body(): returned = lax.all_to_all(back_out, 'req', 0, 0, tiled=True)]
    all_to_all x0 -> x1, starting transfers between devices: none -> 13.6 us  [body(): returned = lax.all_to_all(back_out, 'req', 0, 0, tiled=True)]
    all_to_all x0 -> x1, waiting for transfers between devices: none -> 12.5 us  [body(): returned = lax.all_to_all(back_out, 'req', 0, 0, tiled=True)]
    unnamed x14 -> x21, local copies, waits for them, and re-layouts: 3.22 us -> 9.54 us
    reshape x2, local copies, waits for them, and re-layouts: 4.35 us -> 0.25 us  [the longest x1 0.23 us: body(): query_rows.reshape(slot_count, verified, groups_here, heads_here // group...]
    all_to_all x1, starting transfers between devices: 5.33 us -> 6.97 us  [body(): incoming = lax.all_to_all(outgoing, 'req', 0, 0, tiled=True)]
    another operation x1, local copies, waits for them, and re-layouts: 0.16 us -> 1.71 us  [body(): lax.all_gather(dealt_rows.reshape(rows, width), 'tp', axis=0, tiled=False)]
    all_to_all x1, waiting for transfers between devices: 4.98 us -> 3.52 us  [body(): lax.all_to_all(wish.reshape(peers, 1, 1), 'req', 0, 0, tiled=True)]
  transfers between devices with their start and end apart: 2 -> 3, of which waited for: 2 -> 3; matrix products, arithmetic and copies ran while one was open for 9% -> 11% of each run, Pallas kernels for 0% -> 0%
where the time goes in v15:
time: 135 us; the launch traced here: 134 us
  blocking collectives  48.3 us (36%)
  starting transfers between devices  32.2 us (24%)
  waiting for transfers between devices  20.4 us (15%)
  local copies, waits for them, and re-layouts  19.8 us (15%)
  other arithmetic  7.78 us (6%)
  matrix products  4.73 us (4%)
    all_gather x1, blocking collectives, body(): lax.all_gather(dealt_rows.reshape(rows, width), 'tp', axis=0, tiled=False)  27.7 us
    all_to_all x1, blocking collectives, body(): pieces = lax.all_to_all(pieces, 'tp', 0, 0, tiled=True)  20.6 us
    all_to_all x1, starting transfers between devices, body(): returned = lax.all_to_all(back_out, 'req', 0, 0, tiled=True)  13.6 us
    all_to_all x1, waiting for transfers between devices, body(): returned = lax.all_to_all(back_out, 'req', 0, 0, tiled=True)  12.5 us
    all_to_all x1, starting transfers between devices, body(): lax.all_to_all(wish.reshape(peers, 1, 1), 'req', 0, 0, tiled=True)  11.6 us
    unnamed x21, local copies, waits for them, and re-layouts  9.54 us
    all_to_all x1, starting transfers between devices, body(): incoming = lax.all_to_all(outgoing, 'req', 0, 0, tiled=True)  6.97 us
    all_to_all x1, waiting for transfers between devices, body(): incoming = lax.all_to_all(outgoing, 'req', 0, 0, tiled=True)  4.4 us
  transfers between devices with their start and end apart: 3, of which 3 were waited for; matrix products, arithmetic and copies ran while one was open for 11% of the time, Pallas kernels for 0%

profile of v15, /device:TPU:1, one launch (start us, length us, event | category | flops | bytes accessed | tf_op | source)
XLA Modules:
  0.0 134.1 jit_solution(12391552817658143272)
XLA Ops:
  0.6 0.8 and_select_fusion.1
  1.5 0.7 copy.51
  2.2 11.6 %all-to-all-start = ((s32[64,1,1]{2,1,0:T(1,128)}), s32[64,1,1]{2,1,0:T(1,128)S(1)}, u32[]{:S(2)}, u32[]{:S(2)}) async-start(s32[64,1,1]{2,1,0:T(1,128)} %copy.51), calls=%async_computation | async-start | bytes 65536 | tf_op jit(solution)/shard_map/all_to_all | solution.py:84
  13.9 0.7 add_convert_fusion
  14.6 0.7 iota_compare_fusion.4
  15.3 0.7 iota_compare_fusion.3
  17.2 1.4 %reshape.277 = f32[8,1,320]{2,0,1:T(8,128)} reshape(bf16[2560]{0:T(1024)(128)(2,1)} %param.10) | data formatting | bytes 15360 | tf_op jit(solution)/shard_map/convert_element_type | solution.py:93
  18.5 1.0 copy.52
  19.6 3.5 %all-to-all-done = s32[64,1,1]{2,1,0:T(1,128)S(1)} async-done(((s32[64,1,1]{2,1,0:T(1,128)}), s32[64,1,1]{2,1,0:T(1,128)S(1)}, u32[]{:S(2)}, u32[]{:S(2)}) %all-to-all-start) | async-done | bytes 288 | tf_op jit(solution)/shard_map/all_to_all | solution.py:84
  23.2 1.2 reduce.3
  24.7 0.7 copy.66
  25.4 7.0 %all-to-all-start.1 = ((bf16[64,16,128]{2,1,0:T(8,128)(2,1)}), bf16[64,16,128]{2,1,0:T(8,128)(2,1)}, u32[]{:S(2)}, u32[]{:S(2)}) async-start(bf16[64,16,128]{2,1,0:T(8,128)(2,1)} %bitcast.28), calls=%async_computation.1 | async-start | bytes 524288 | tf_op jit(solution)/shard_map/all_to_all | solution.py:104
  32.4 2.5 %copy.53 = bf16[2560,320]{1,0:T(8,128)(2,1)} copy(bf16[2560,320]{0,1:T(8,128)(2,1)S(1)} %copy-done.1) | data formatting | bytes 3276800 | tf_op args[2]
  34.9 1.5 %copy.54 = bf16[2560,1,160]{2,0,1:T(8,128)(2,1)S(1)} copy(bf16[2560,1,160]{0,2,1:T(8,128)(2,1)} %param.12) | data formatting | bytes 1638400 | tf_op args[3]
  36.4 3.2 %reshape.272 = bf16[320,8,320]{2,1,0:T(8,128)(2,1)S(1)} reshape(bf16[320,2560]{1,0:T(8,128)(2,1)} %param.13) | data formatting | bytes 3276800 | tf_op jit(solution)/shard_map/reshape | solution.py:137
  39.7 0.7 broadcast_in_dim.45
  40.4 0.7 pad_add_fusion
  41.1 4.4 %all-to-all-done.1 = bf16[64,16,128]{2,1,0:T(8,128)(2,1)} async-done(((bf16[64,16,128]{2,1,0:T(8,128)(2,1)}), bf16[64,16,128]{2,1,0:T(8,128)(2,1)}, u32[]{:S(2)}, u32[]{:S(2)}) %all-to-all-start.1) | async-done | bytes 262176 | tf_op jit(solution)/shard_map/all_to_all | solution.py:104
  45.5 1.0 copy.103
  46.5 0.9 convolution_convert_fusion.3
  47.4 1.7 %all_gather_reshape.3 = bf16[1,160,320]{2,1,0:T(8,128)(2,1)} reshape(bf16[32,1600]{1,0:T(8,128)(2,1)} %convolution_convert_fusion.3) | data formatting | bytes 204800 | tf_op jit(solution)/shard_map/all_gather;reshape | solution.py:112
  49.1 27.7 %all_gather.3 = bf16[8,160,320]{2,1,0:T(8,128)(2,1)S(1)} all-gather(bf16[1,160,320]{2,1,0:T(8,128)(2,1)} %all_gather_reshape.3), channel_id=1, replica_groups=mesh['req'=64,'tp'=8] {'tp'}, dimensions={0}, use_global_device_ids=true | all-gather | bytes 921600 | tf_op jit(solution)/shard_map/all_gather | solution.py:112
  77.1 1.1 fusion.16
  79.3 0.7 copy-done.2
  82.3 0.7 fusion.12
  83.0 1.1 reshape.273
  84.2 20.6 %all_to_all.20 = bf16[8,400,128]{2,1,0:T(8,128)(2,1)S(1)} all-to-all(bf16[8,400,128]{2,1,0:T(8,128)(2,1)S(1)} %reshape.273), channel_id=1, replica_groups=mesh['req'=64,'tp'=8] {'tp'}, dimensions={0} | all-to-all | bytes 1638400 | tf_op jit(solution)/shard_map/all_to_all | solution.py:142
  105.4 0.7 copy.68
  106.1 13.6 %all-to-all-start.3 = ((bf16[64,16,128]{2,1,0:T(8,128)(2,1)}), bf16[64,16,128]{2,1,0:T(8,128)(2,1)S(1)}, u32[]{:S(2)}, u32[]{:S(2)}) async-start(bf16[64,16,128]{2,1,0:T(8,128)(2,1)} %bitcast.33), calls=%async_computation.3 | async-start | bytes 524288 | tf_op jit(solution)/shard_map/all_to_all | solution.py:149
  119.7 0.7 copy.61
  120.4 12.5 %all-to-all-done.3 = bf16[64,16,128]{2,1,0:T(8,128)(2,1)S(1)} async-done(((bf16[64,16,128]{2,1,0:T(8,128)(2,1)}), bf16[64,16,128]{2,1,0:T(8,128)(2,1)S(1)}, u32[]{:S(2)}, u32[]{:S(2)}) %all-to-all-start.3) | async-done | bytes 262176 | tf_op jit(solution)/shard_map/all_to_all | solution.py:149
  133.4 0.7 copy.60
  (42 shorter events, 6.5 us)
Async XLA Ops:
  0.6 31.8 %copy-start.1 = (bf16[2560,320]{0,1:T(8,128)(2,1)S(1)}, bf16[2560,320]{0,1:T(8,128)(2,1)}, u32[]{:S(2)}) copy-start(bf16[2560,320]{0,1:T(8,128)(2,1)} %param.11) | copy-start | bytes 4915204
  2.2 20.9 %all-to-all-start = ((s32[64,1,1]{2,1,0:T(1,128)}), s32[64,1,1]{2,1,0:T(1,128)S(1)}, u32[]{:S(2)}, u32[]{:S(2)}) async-start(s32[64,1,1]{2,1,0:T(1,128)} %copy.51), calls=%async_computation | async-start | bytes 65536 | tf_op jit(solution)/shard_map/all_to_all | solution.py:84
  25.4 20.1 %all-to-all-start.1 = ((bf16[64,16,128]{2,1,0:T(8,128)(2,1)}), bf16[64,16,128]{2,1,0:T(8,128)(2,1)}, u32[]{:S(2)}, u32[]{:S(2)}) async-start(bf16[64,16,128]{2,1,0:T(8,128)(2,1)} %bitcast.28), calls=%async_computation.1 | async-start | bytes 524288 | tf_op jit(solution)/shard_map/all_to_all | solution.py:104
  49.1 28.0 %copy-start = (bf16[2560,320]{1,0:T(8,128)(2,1)S(1)}, bf16[2560,320]{1,0:T(8,128)(2,1)}, u32[]{:S(2)}) copy-start(bf16[2560,320]{1,0:T(8,128)(2,1)} %copy.53) | copy-start | bytes 4915204
  49.1 28.0 %copy-start.4 = (f32[8,1,320]{2,0,1:T(8,128)S(1)}, f32[8,1,320]{2,0,1:T(8,128)}, u32[]{:S(2)}) copy-start(f32[8,1,320]{2,0,1:T(8,128)} %reshape.277) | copy-start | bytes 30724
  78.7 1.2 copy-start.2
  79.2 1.2 copy-start.3
  106.1 26.8 %all-to-all-start.3 = ((bf16[64,16,128]{2,1,0:T(8,128)(2,1)}), bf16[64,16,128]{2,1,0:T(8,128)(2,1)S(1)}, u32[]{:S(2)}, u32[]{:S(2)}) async-start(bf16[64,16,128]{2,1,0:T(8,128)(2,1)} %bitcast.33), calls=%async_computation.3 | async-start | bytes 524288 | tf_op jit(solution)/shard_map/all_to_all | solution.py:149

commit v16 on v12

--- a/solution.py
+++ b/solution.py
@@ -102,11 +102,11 @@
     ).astype(jnp.bfloat16)
     outgoing = jnp.pad(outgoing, ((0, 0), (0, padded - row_size))).reshape(peers, padded // 128, 128)
     incoming = lax.all_to_all(outgoing, "req", 0, 0, tiled=True)
-    incoming = incoming.reshape(peers, padded)[:, :row_size]
+    incoming = incoming.reshape(peers, padded)
     take = match.astype(jnp.bfloat16)
     dealt_rows = jnp.einsum(
         "pi,px->ix", take, incoming, preferred_element_type=jnp.float32
-    ).astype(jnp.bfloat16)
+    ).astype(jnp.bfloat16)[:, :row_size]
     rows = slot_count * verified
     lanes = rows * width // 128
     features = lax.all_gather(dealt_rows.reshape(rows, width), "tp", axis=0, tiled=False)

time: 129 us -> 129 us (level)
    unnamed x14 -> x13, local copies, waits for them, and re-layouts: 3.22 us -> 3.15 us
where the time goes in v16:
time: 129 us; the launch traced here: 128 us
  blocking collectives  73.7 us (57%)
  starting transfers between devices  16.9 us (13%)
  local copies, waits for them, and re-layouts  14.4 us (11%)
  waiting for transfers between devices  10.4 us (8%)
  other arithmetic  7.82 us (6%)
  matrix products  4.41 us (3%)
    all_gather x1, blocking collectives, body(): lax.all_gather(dealt_rows.reshape(rows, width), 'tp', axis=0, tiled=False)  27.5 us
    all_to_all x1, blocking collectives, body(): returned = lax.all_to_all(back_out, 'req', 0, 0, tiled=True)  25.6 us
    all_to_all x1, blocking collectives, body(): pieces = lax.all_to_all(pieces, 'tp', 0, 0, tiled=True)  20.5 us
    all_to_all x1, starting transfers between devices, body(): lax.all_to_all(wish.reshape(peers, 1, 1), 'req', 0, 0, tiled=True)  11.6 us
    all_to_all x1, waiting for transfers between devices, body(): incoming = lax.all_to_all(outgoing, 'req', 0, 0, tiled=True)  5.39 us
    all_to_all x1, starting transfers between devices, body(): incoming = lax.all_to_all(outgoing, 'req', 0, 0, tiled=True)  5.33 us
    all_to_all x1, waiting for transfers between devices, body(): lax.all_to_all(wish.reshape(peers, 1, 1), 'req', 0, 0, tiled=True)  4.98 us
    reshape x1, local copies, waits for them, and re-layouts, body(): output_weight.reshape(-1, shards, width)  3.24 us
  transfers between devices with their start and end apart: 2, of which 2 were waited for; matrix products, arithmetic and copies ran while one was open for 9% of the time, Pallas kernels for 0%

profile of v16, /device:TPU:1, one launch (start us, length us, event | category | flops | bytes accessed | tf_op | source)
XLA Modules:
  0.0 128.5 jit_solution(18336747159089649876)
XLA Ops:
  0.6 0.8 and_select_fusion.1
  1.5 0.7 copy.59
  2.2 11.6 %all-to-all-start = ((s32[64,1,1]{2,1,0:T(1,128)}), s32[64,1,1]{2,1,0:T(1,128)S(1)}, u32[]{:S(2)}, u32[]{:S(2)}) async-start(s32[64,1,1]{2,1,0:T(1,128)} %copy.59), calls=%async_computation | async-start | bytes 65536 | tf_op jit(solution)/shard_map/all_to_all | solution.py:84
  13.9 0.7 add_convert_fusion.1
  14.5 0.7 iota_compare_fusion.3
  15.3 0.7 iota_compare_fusion.7
  15.9 0.4 multiply_sine_fusion
  16.3 0.8 reshape.288
  17.1 1.0 copy.60
  18.2 5.0 %all-to-all-done = s32[64,1,1]{2,1,0:T(1,128)S(1)} async-done(((s32[64,1,1]{2,1,0:T(1,128)}), s32[64,1,1]{2,1,0:T(1,128)S(1)}, u32[]{:S(2)}, u32[]{:S(2)}) %all-to-all-start) | async-done | bytes 288 | tf_op jit(solution)/shard_map/all_to_all | solution.py:84
  23.2 1.2 reduce.3
  24.7 0.7 copy.80
  25.4 5.3 %all-to-all-start.1 = ((bf16[64,16,128]{2,1,0:T(8,128)(2,1)}), bf16[64,16,128]{2,1,0:T(8,128)(2,1)S(1)}, u32[]{:S(2)}, u32[]{:S(2)}) async-start(bf16[64,16,128]{2,1,0:T(8,128)(2,1)} %bitcast.44), calls=%async_computation.1 | async-start | bytes 524288 | tf_op jit(solution)/shard_map/all_to_all | solution.py:104
  30.8 2.5 %reshape.280 = bf16[8,320,320]{1,0,2:T(8,128)(2,1)} reshape(bf16[2560,320]{0,1:T(8,128)(2,1)S(1)} %copy-done.1) | data formatting | bytes 3276800 | tf_op jit(solution)/shard_map/reshape | solution.py:121
  33.3 1.9 %reshape.277 = bf16[8,320,160]{1,0,2:T(8,128)(2,1)S(1)} reshape(bf16[2560,1,160]{0,2,1:T(8,128)(2,1)} %param.12) | data formatting | bytes 1638400 | tf_op jit(solution)/shard_map/reshape
  35.2 3.2 %reshape.283 = bf16[320,8,320]{2,1,0:T(8,128)(2,1)S(1)} reshape(bf16[320,2560]{1,0:T(8,128)(2,1)} %param.13) | data formatting | bytes 3276800 | tf_op jit(solution)/shard_map/reshape | solution.py:143
  38.6 5.4 %all-to-all-done.1 = bf16[64,16,128]{2,1,0:T(8,128)(2,1)S(1)} async-done(((bf16[64,16,128]{2,1,0:T(8,128)(2,1)}), bf16[64,16,128]{2,1,0:T(8,128)(2,1)S(1)}, u32[]{:S(2)}, u32[]{:S(2)}) %all-to-all-start.1) | async-done | bytes 262176 | tf_op jit(solution)/shard_map/all_to_all | solution.py:104
  44.4 27.5 %all_gather.3 = bf16[8,160,320]{2,1,0:T(8,128)(2,1)S(1)} all-gather(bf16[1,160,320]{2,1,0:T(8,128)(2,1)S(1)} %all_gather_reshape.3), channel_id=1, replica_groups=mesh['req'=64,'tp'=8] {'tp'}, dimensions={0}, use_global_device_ids=true | all-gather | bytes 921600 | tf_op jit(solution)/shard_map/all_gather | solution.py:112
  71.9 1.0 fusion
  73.0 0.4 fusion.2
  73.4 0.4 convolution_bitcast_fusion
  73.9 0.6 copy-done
  74.5 1.0 fusion.15
  75.8 0.8 broadcast_select_fusion
  76.8 0.5 fusion.51
  77.3 0.4 fusion.30
  77.8 0.6 fusion.19
  78.6 0.7 fusion.11
  79.3 1.1 reshape.284
  80.5 20.5 %all_to_all.20 = bf16[8,400,128]{2,1,0:T(8,128)(2,1)S(1)} all-to-all(bf16[8,400,128]{2,1,0:T(8,128)(2,1)S(1)} %reshape.284), channel_id=1, replica_groups=mesh['req'=64,'tp'=8] {'tp'}, dimensions={0} | all-to-all | bytes 1638400 | tf_op jit(solution)/shard_map/all_to_all | solution.py:148
  101.7 25.6 %all_to_all.21 = bf16[64,16,128]{2,1,0:T(8,128)(2,1)S(1)} all-to-all(bf16[64,16,128]{2,1,0:T(8,128)(2,1)S(1)} %bitcast.110), channel_id=1, replica_groups=mesh['req'=64,'tp'=8] {'req'}, dimensions={0} | all-to-all | bytes 524288 | tf_op jit(solution)/shard_map/all_to_all | solution.py:155
  127.8 0.7 copy.71
  (34 shorter events, 3.0 us)
Async XLA Ops:
  0.6 30.2 %copy-start.1 = (bf16[2560,320]{0,1:T(8,128)(2,1)S(1)}, bf16[2560,320]{0,1:T(8,128)(2,1)}, u32[]{:S(2)}) copy-start(bf16[2560,320]{0,1:T(8,128)(2,1)} %param.11) | copy-start | bytes 4915204
  2.2 20.9 %all-to-all-start = ((s32[64,1,1]{2,1,0:T(1,128)}), s32[64,1,1]{2,1,0:T(1,128)S(1)}, u32[]{:S(2)}, u32[]{:S(2)}) async-start(s32[64,1,1]{2,1,0:T(1,128)} %copy.59), calls=%async_computation | async-start | bytes 65536 | tf_op jit(solution)/shard_map/all_to_all | solution.py:84
  25.4 18.5 %all-to-all-start.1 = ((bf16[64,16,128]{2,1,0:T(8,128)(2,1)}), bf16[64,16,128]{2,1,0:T(8,128)(2,1)S(1)}, u32[]{:S(2)}, u32[]{:S(2)}) async-start(bf16[64,16,128]{2,1,0:T(8,128)(2,1)} %bitcast.44), calls=%async_computation.1 | async-start | bytes 524288 | tf_op jit(solution)/shard_map/all_to_all | solution.py:104
  73.0 1.6 %copy-start = (bf16[8,320,320]{1,0,2:T(8,128)(2,1)S(1)}, bf16[8,320,320]{1,0,2:T(8,128)(2,1)}, u32[]{:S(2)}) copy-start(bf16[8,320,320]{1,0,2:T(8,128)(2,1)} %reshape.280) | copy-start | bytes 4915204
  75.5 1.3 copy-start.2

commit v17 on v12

--- a/solution.py
+++ b/solution.py
@@ -153,10 +153,10 @@
     ).astype(jnp.bfloat16)
     back_out = jnp.pad(back_out, ((0, 0), (0, padded - row_size))).reshape(peers, padded // 128, 128)
     returned = lax.all_to_all(back_out, "req", 0, 0, tiled=True)
-    returned = returned.reshape(peers, padded)[:, :row_size]
+    returned = returned.reshape(peers, padded)
     block_output = jnp.einsum(
         "dj,dx->jx", pick, returned, preferred_element_type=jnp.float32
-    ).astype(jnp.bfloat16).reshape(slot_count, verified, width)
+    ).astype(jnp.bfloat16)[:, :row_size].reshape(slot_count, verified, width)
     return (block_output, new_entries)
 
 

time: 129 us -> 129 us (level)
    unnamed x14 -> x13, local copies, waits for them, and re-layouts: 3.22 us -> 3.15 us
where the time goes in v17:
time: 129 us
  blocking collectives  73.7 us (57%)
  starting transfers between devices  16.9 us (13%)
  local copies, waits for them, and re-layouts  14.4 us (11%)
  waiting for transfers between devices  10.4 us (8%)
  other arithmetic  7.82 us (6%)
  matrix products  4.41 us (3%)
    all_gather x1, blocking collectives, body(): lax.all_gather(dealt_rows.reshape(rows, width), 'tp', axis=0, tiled=False)  27.5 us
    all_to_all x1, blocking collectives, body(): returned = lax.all_to_all(back_out, 'req', 0, 0, tiled=True)  25.8 us
    all_to_all x1, blocking collectives, body(): pieces = lax.all_to_all(pieces, 'tp', 0, 0, tiled=True)  20.4 us
    all_to_all x1, starting transfers between devices, body(): lax.all_to_all(wish.reshape(peers, 1, 1), 'req', 0, 0, tiled=True)  11.6 us
    all_to_all x1, waiting for transfers between devices, body(): incoming = lax.all_to_all(outgoing, 'req', 0, 0, tiled=True)  5.39 us
    all_to_all x1, starting transfers between devices, body(): incoming = lax.all_to_all(outgoing, 'req', 0, 0, tiled=True)  5.33 us
    all_to_all x1, waiting for transfers between devices, body(): lax.all_to_all(wish.reshape(peers, 1, 1), 'req', 0, 0, tiled=True)  4.98 us
    reshape x1, local copies, waits for them, and re-layouts, body(): output_weight.reshape(-1, shards, width)  3.24 us
  transfers between devices with their start and end apart: 2, of which 2 were waited for; matrix products, arithmetic and copies ran while one was open for 9% of the time, Pallas kernels for 0%

profile of v17, /device:TPU:1, one launch (start us, length us, event | category | flops | bytes accessed | tf_op | source)
XLA Modules:
  0.0 128.5 jit_solution(12936536229568094930)
XLA Ops:
  0.6 0.8 and_select_fusion.1
  1.5 0.7 copy.59
  2.2 11.6 %all-to-all-start = ((s32[64,1,1]{2,1,0:T(1,128)}), s32[64,1,1]{2,1,0:T(1,128)S(1)}, u32[]{:S(2)}, u32[]{:S(2)}) async-start(s32[64,1,1]{2,1,0:T(1,128)} %copy.59), calls=%async_computation | async-start | bytes 65536 | tf_op jit(solution)/shard_map/all_to_all | solution.py:84
  13.9 0.7 add_convert_fusion.1
  14.5 0.7 iota_compare_fusion.3
  15.3 0.7 iota_compare_fusion.7
  15.9 0.4 multiply_sine_fusion
  16.3 0.8 reshape.288
  17.1 1.0 copy.60
  18.2 5.0 %all-to-all-done = s32[64,1,1]{2,1,0:T(1,128)S(1)} async-done(((s32[64,1,1]{2,1,0:T(1,128)}), s32[64,1,1]{2,1,0:T(1,128)S(1)}, u32[]{:S(2)}, u32[]{:S(2)}) %all-to-all-start) | async-done | bytes 288 | tf_op jit(solution)/shard_map/all_to_all | solution.py:84
  23.2 1.2 reduce.3
  24.7 0.7 copy.80
  25.4 5.3 %all-to-all-start.1 = ((bf16[64,16,128]{2,1,0:T(8,128)(2,1)}), bf16[64,16,128]{2,1,0:T(8,128)(2,1)S(1)}, u32[]{:S(2)}, u32[]{:S(2)}) async-start(bf16[64,16,128]{2,1,0:T(8,128)(2,1)} %bitcast.44), calls=%async_computation.1 | async-start | bytes 524288 | tf_op jit(solution)/shard_map/all_to_all | solution.py:104
  30.8 2.5 %reshape.280 = bf16[8,320,320]{1,0,2:T(8,128)(2,1)} reshape(bf16[2560,320]{0,1:T(8,128)(2,1)S(1)} %copy-done.1) | data formatting | bytes 3276800 | tf_op jit(solution)/shard_map/reshape | solution.py:121
  33.3 1.9 %reshape.277 = bf16[8,320,160]{1,0,2:T(8,128)(2,1)S(1)} reshape(bf16[2560,1,160]{0,2,1:T(8,128)(2,1)} %param.12) | data formatting | bytes 1638400 | tf_op jit(solution)/shard_map/reshape
  35.2 3.2 %reshape.283 = bf16[320,8,320]{2,1,0:T(8,128)(2,1)S(1)} reshape(bf16[320,2560]{1,0:T(8,128)(2,1)} %param.13) | data formatting | bytes 3276800 | tf_op jit(solution)/shard_map/reshape | solution.py:143
  38.6 5.4 %all-to-all-done.1 = bf16[64,16,128]{2,1,0:T(8,128)(2,1)S(1)} async-done(((bf16[64,16,128]{2,1,0:T(8,128)(2,1)}), bf16[64,16,128]{2,1,0:T(8,128)(2,1)S(1)}, u32[]{:S(2)}, u32[]{:S(2)}) %all-to-all-start.1) | async-done | bytes 262176 | tf_op jit(solution)/shard_map/all_to_all | solution.py:104
  44.4 27.5 %all_gather.3 = bf16[8,160,320]{2,1,0:T(8,128)(2,1)S(1)} all-gather(bf16[1,160,320]{2,1,0:T(8,128)(2,1)S(1)} %all_gather_reshape.3), channel_id=1, replica_groups=mesh['req'=64,'tp'=8] {'tp'}, dimensions={0}, use_global_device_ids=true | all-gather | bytes 921600 | tf_op jit(solution)/shard_map/all_gather | solution.py:112
  72.0 1.0 fusion
  73.0 0.4 fusion.2
  73.4 0.4 convolution_bitcast_fusion
  73.9 0.6 copy-done
  74.6 1.0 fusion.15
  75.9 0.8 broadcast_select_fusion
  76.8 0.5 fusion.51
  77.4 0.4 fusion.30
  77.8 0.6 fusion.19
  78.7 0.7 fusion.11
  79.4 1.1 reshape.284
  80.5 20.4 %all_to_all.20 = bf16[8,400,128]{2,1,0:T(8,128)(2,1)S(1)} all-to-all(bf16[8,400,128]{2,1,0:T(8,128)(2,1)S(1)} %reshape.284), channel_id=1, replica_groups=mesh['req'=64,'tp'=8] {'tp'}, dimensions={0} | all-to-all | bytes 1638400 | tf_op jit(solution)/shard_map/all_to_all | solution.py:148
  101.6 25.8 %all_to_all.21 = bf16[64,16,128]{2,1,0:T(8,128)(2,1)S(1)} all-to-all(bf16[64,16,128]{2,1,0:T(8,128)(2,1)S(1)} %bitcast.111), channel_id=1, replica_groups=mesh['req'=64,'tp'=8] {'req'}, dimensions={0} | all-to-all | bytes 524288 | tf_op jit(solution)/shard_map/all_to_all | solution.py:155
  127.9 0.7 copy.71
  (34 shorter events, 3.0 us)
Async XLA Ops:
  0.6 30.2 %copy-start.1 = (bf16[2560,320]{0,1:T(8,128)(2,1)S(1)}, bf16[2560,320]{0,1:T(8,128)(2,1)}, u32[]{:S(2)}) copy-start(bf16[2560,320]{0,1:T(8,128)(2,1)} %param.11) | copy-start | bytes 4915204
  2.2 20.9 %all-to-all-start = ((s32[64,1,1]{2,1,0:T(1,128)}), s32[64,1,1]{2,1,0:T(1,128)S(1)}, u32[]{:S(2)}, u32[]{:S(2)}) async-start(s32[64,1,1]{2,1,0:T(1,128)} %copy.59), calls=%async_computation | async-start | bytes 65536 | tf_op jit(solution)/shard_map/all_to_all | solution.py:84
  25.4 18.5 %all-to-all-start.1 = ((bf16[64,16,128]{2,1,0:T(8,128)(2,1)}), bf16[64,16,128]{2,1,0:T(8,128)(2,1)S(1)}, u32[]{:S(2)}, u32[]{:S(2)}) async-start(bf16[64,16,128]{2,1,0:T(8,128)(2,1)} %bitcast.44), calls=%async_computation.1 | async-start | bytes 524288 | tf_op jit(solution)/shard_map/all_to_all | solution.py:104
  73.0 1.6 %copy-start = (bf16[8,320,320]{1,0,2:T(8,128)(2,1)S(1)}, bf16[8,320,320]{1,0,2:T(8,128)(2,1)}, u32[]{:S(2)}) copy-start(bf16[8,320,320]{1,0,2:T(8,128)(2,1)} %reshape.280) | copy-start | bytes 4915204
  75.6 1.3 copy-start.2
